TPU v7x, 128 devices: a whole 4x4x4 slice. The times are simulated.
128 devices in a mesh: shards: 8 (over x, core), tensor: 4 (over z), section: 4 (over y).
Axes of the slice: x: 4, y: 4, z: 4, core: 2. Of those that a mesh axis runs over, the one named last changes fastest.
Arguments:
- attn_grad: bfloat16 [16, 4, 1024, 1024], P('section', None, 'shards', 'tensor'), may hold values from -60 to 60
- mlp_in_grad: bfloat16 [16, 2, 1024, 2816], P('section', None, 'shards', 'tensor'), may hold values from -60 to 60
- mlp_out_grad: bfloat16 [16, 2816, 1024], P('section', 'tensor', 'shards'), may hold values from -60 to 60
- attn_momentum: bfloat16 [16, 4, 1024, 1024], P('section', None, 'shards', 'tensor'), may hold values from -3 to 3
- mlp_in_momentum: bfloat16 [16, 2, 1024, 2816], P('section', None, 'shards', 'tensor'), may hold values from -3 to 3
- mlp_out_momentum: bfloat16 [16, 2816, 1024], P('section', 'tensor', 'shards'), may hold values from -3 to 3
- owners: int32 [16, 7], P('section'), may hold values from 0 to 31, as said below
- embed_weight: float32 [32128, 1024], P(('shards', 'tensor', 'section')), may hold values from -6 to 6
- embed_grad: bfloat16 [32128, 1024], P(('shards', 'tensor', 'section')), may hold values from -6 to 6
- embed_moment: float32 [32128, 1024], P(('shards', 'tensor', 'section')), may hold values from -3 to 3
- embed_second: float32 [32128, 1024], P(('shards', 'tensor', 'section')), may hold values from 0.01 to 1
- norm_scale: float32 [16, 2048], P('section'), may hold values from 0.5 to 1.5
- norm_partial: float32 [16, 32, 2048], P('section', ('shards', 'tensor')), may hold values from -2 to 2
- norm_moment: float32 [16, 2048], P('section'), may hold values from -3 to 3
- norm_second: float32 [16, 2048], P('section'), may hold values from 0.01 to 0.5
- bias_table: float32 [32, 16], replicated, may hold values from -3 to 3
- bias_partial: float32 [128, 32, 16], P(('shards', 'tensor', 'section')), may hold values from -2 to 2
- bias_moment: float32 [32, 16], replicated, may hold values from -3 to 3
- bias_second: float32 [32, 16], replicated, may hold values from 0.01 to 1
Outputs:
- attn_momentum_new: bfloat16 [16, 4, 1024, 1024], P('section', None, 'shards', 'tensor')
- mlp_in_momentum_new: bfloat16 [16, 2, 1024, 2816], P('section', None, 'shards', 'tensor')
- mlp_out_momentum_new: bfloat16 [16, 2816, 1024], P('section', 'tensor', 'shards')
- attn_update: float32 [16, 4, 1024, 1024], P('section', None, 'shards', 'tensor')
- mlp_in_update: float32 [16, 2, 1024, 2816], P('section', None, 'shards', 'tensor')
- mlp_out_update: float32 [16, 2816, 1024], P('section', 'tensor', 'shards')
- owner_rms: float32 [128], P(('shards', 'tensor', 'section'))
- embed_weight_new: float32 [32128, 1024], P(('shards', 'tensor', 'section'))
- embed_moment_new: float32 [32128, 1024], P(('shards', 'tensor', 'section'))
- embed_second_new: float32 [32128, 1024], P(('shards', 'tensor', 'section'))
- norm_scale_new: float32 [16, 2048], P('section')
- norm_moment_new: float32 [16, 2048], P('section')
- norm_second_new: float32 [16, 2048], P('section')
- bias_table_new: float32 [32, 16], replicated
- bias_moment_new: float32 [32, 16], replicated
- bias_second_new: float32 [32, 16], replicated
Inputs may be any that keep to these rules, and one draw needn't show every extreme that they name: Owner o names the device of index o among the 32 devices of the layer's section, in the order of the mesh (shards first); the 28 matrices of the layers of one section have distinct owners, so a device owns at most one matrix.
All inputs are finite; a program needn't handle non-finite values.
Results may differ from a plain program's by a relative error of at most 0.018.
Values may be sent and summed in bfloat16 or wider, within the bound.
No kernel may reach another device: no remote copies, remote signals or barrier semaphores. Data moves between devices by JAX's collectives and lax.ppermute only.
A program may use at most 192 MiB of HBM per device.

v0:
```python
import math

import jax
import jax.numpy as jnp
from jax import lax
from jax.sharding import PartitionSpec as P

D = 1024
FF = 2816
NS_STEPS = 2


coef_first = 3.4445
coef_second = -4.775
coef_third = 2.0315


def orthogonalize(matrix):
    norm_value = jnp.sqrt(jnp.sum(matrix * matrix))
    current = (matrix / (norm_value + 1e-07)).astype(jnp.bfloat16)
    for sweep_index in range(NS_STEPS):
        gram_form = jnp.dot(current, current.T, preferred_element_type=jnp.float32).astype(
            jnp.bfloat16
        )
        square_form = jnp.dot(gram_form, gram_form, preferred_element_type=jnp.float32)
        polynomial = (
            coef_second * gram_form.astype(jnp.float32) + coef_third * square_form
        ).astype(jnp.bfloat16)
        current = (
            coef_first * current.astype(jnp.float32)
            + jnp.dot(polynomial, current, preferred_element_type=jnp.float32)
        ).astype(jnp.bfloat16)
    rms_value = norm_value / math.sqrt(matrix.shape[0] * matrix.shape[1])
    return (current, rms_value)


def zeroed(matrix):
    return (jnp.zeros(matrix.shape, jnp.bfloat16), jnp.zeros((), jnp.float32))


def refresh(gradient, moment):
    fresh_moment = (0.95 * moment.astype(jnp.float32) + gradient.astype(jnp.float32)).astype(
        jnp.bfloat16
    )
    advance = (gradient.astype(jnp.float32) + 0.95 * fresh_moment.astype(jnp.float32)).astype(
        jnp.bfloat16
    )
    return (fresh_moment, advance)


def adamw_update(weight, gradient, moment, second, decay_rate):
    moment_new = 0.9 * moment + 0.1 * gradient
    second_new = 0.95 * second + 0.05 * gradient * gradient
    weight_new = weight - 0.02 * (moment_new / (jnp.sqrt(second_new) + 1e-08) + decay_rate * weight)
    return (weight_new, moment_new, second_new)


def on_device(
    attn_grad,
    mlp_in_grad,
    mlp_out_grad,
    attn_momentum,
    mlp_in_momentum,
    mlp_out_momentum,
    owners,
    embed_weight,
    embed_grad,
    embed_moment,
    embed_second,
    norm_scale,
    norm_partial,
    norm_moment,
    norm_second,
    bias_table,
    bias_partial,
    bias_moment,
    bias_second,
):
    shards_count = lax.axis_size("shards")
    tensor_count = lax.axis_size("tensor")
    group_count = shards_count * tensor_count
    my_index = lax.axis_index(("shards", "tensor"))
    layers_here = owners.shape[0]
    rows_block = attn_grad.shape[2]
    cols_block = attn_grad.shape[3]
    ff_block = mlp_in_grad.shape[3]
    square_width = rows_block * cols_block
    rect_width = rows_block * ff_block
    attn_fresh, attn_ahead = refresh(attn_grad, attn_momentum)
    inner_fresh, inner_ahead = refresh(mlp_in_grad, mlp_in_momentum)
    outer_fresh, outer_ahead = refresh(mlp_out_grad, mlp_out_momentum)
    rect_ahead = jnp.concatenate([inner_ahead, jnp.swapaxes(outer_ahead, 1, 2)[:, None]], axis=1)
    slots = jnp.arange(group_count, dtype=jnp.int32)
    square_owner = owners[:, :4].reshape(-1)
    rect_owner = owners[:, 4:].reshape(-1)
    square_pick = (slots[:, None] == square_owner[None, :]).astype(jnp.bfloat16)
    rect_pick = (slots[:, None] == rect_owner[None, :]).astype(jnp.bfloat16)
    square_send = jnp.dot(
        square_pick,
        attn_ahead.reshape(layers_here * 4, square_width),
        preferred_element_type=jnp.float32,
    ).astype(jnp.bfloat16)
    rect_send = jnp.dot(
        rect_pick,
        rect_ahead.reshape(layers_here * 3, rect_width),
        preferred_element_type=jnp.float32,
    ).astype(jnp.bfloat16)
    outgoing = jnp.concatenate([square_send, rect_send], axis=1)
    incoming = lax.all_to_all(
        outgoing, ("shards", "tensor"), split_axis=0, concat_axis=0, tiled=True
    )
    square_in = incoming[:, :square_width]
    rect_in = incoming[:, square_width:]
    square_whole = (
        square_in.astype(jnp.float32)
        .reshape(shards_count, tensor_count, rows_block, cols_block)
        .transpose(0, 2, 1, 3)
        .reshape(shards_count * rows_block, tensor_count * cols_block)
    )
    rect_whole = (
        rect_in.astype(jnp.float32)
        .reshape(shards_count, tensor_count, rows_block, ff_block)
        .transpose(0, 2, 1, 3)
        .reshape(shards_count * rows_block, tensor_count * ff_block)
    )
    owns_square = jnp.any(square_owner == my_index)
    owns_rect = jnp.any(rect_owner == my_index)
    square_done, square_rms = lax.cond(owns_square, orthogonalize, zeroed, square_whole)
    rect_done, rect_rms = lax.cond(owns_rect, orthogonalize, zeroed, rect_whole)
    square_back = (
        square_done.reshape(shards_count, rows_block, tensor_count, cols_block)
        .transpose(0, 2, 1, 3)
        .reshape(group_count, square_width)
    )
    rect_back = (
        rect_done.reshape(shards_count, rows_block, tensor_count, ff_block)
        .transpose(0, 2, 1, 3)
        .reshape(group_count, rect_width)
    )
    returning = jnp.concatenate([square_back, rect_back], axis=1)
    arrived = lax.all_to_all(
        returning, ("shards", "tensor"), split_axis=0, concat_axis=0, tiled=True
    )
    square_arrived = arrived[:, :square_width]
    rect_arrived = arrived[:, square_width:]
    square_rows = jnp.take(square_arrived, square_owner, axis=0).reshape(
        layers_here, 4, rows_block, cols_block
    ).astype(jnp.float32) * (0.2 * math.sqrt(D))
    rect_rows = jnp.take(rect_arrived, rect_owner, axis=0).reshape(
        layers_here, 3, rows_block, ff_block
    ).astype(jnp.float32) * (0.2 * math.sqrt(FF))
    mlp_in_update = rect_rows[:, :2]
    mlp_out_update = jnp.swapaxes(rect_rows[:, 2], 1, 2)
    owner_rms = (square_rms + rect_rms).reshape(1)
    norm_grad = lax.psum(norm_partial[:, 0].astype(jnp.bfloat16), ("shards", "tensor")).astype(
        jnp.float32
    )
    bias_grad = lax.psum(bias_partial[0], ("shards", "tensor", "section"))
    embed_results = adamw_update(
        embed_weight, embed_grad.astype(jnp.float32), embed_moment, embed_second, 0.1
    )
    norm_results = adamw_update(norm_scale, norm_grad, norm_moment, norm_second, 0.0)
    bias_results = adamw_update(bias_table, bias_grad, bias_moment, bias_second, 0.0)
    return (
        attn_fresh,
        inner_fresh,
        outer_fresh,
        square_rows,
        mlp_in_update,
        mlp_out_update,
        owner_rms,
        embed_results[0],
        embed_results[1],
        embed_results[2],
        norm_results[0],
        norm_results[1],
        norm_results[2],
        bias_results[0],
        bias_results[1],
        bias_results[2],
    )


def solution(mesh):
    placed = (
        P("section", None, "shards", "tensor"),
        P("section", None, "shards", "tensor"),
        P("section", "tensor", "shards"),
        P("section", None, "shards", "tensor"),
        P("section", None, "shards", "tensor"),
        P("section", "tensor", "shards"),
        P("section", None),
        P(("shards", "tensor", "section"), None),
        P(("shards", "tensor", "section"), None),
        P(("shards", "tensor", "section"), None),
        P(("shards", "tensor", "section"), None),
        P("section", None),
        P("section", ("shards", "tensor"), None),
        P("section", None),
        P("section", None),
        P(),
        P(("shards", "tensor", "section"), None, None),
        P(),
        P(),
    )
    return jax.shard_map(
        on_device,
        mesh=mesh,
        in_specs=placed,
        out_specs=(
            P("section", None, "shards", "tensor"),
            P("section", None, "shards", "tensor"),
            P("section", "tensor", "shards"),
            P("section", None, "shards", "tensor"),
            P("section", None, "shards", "tensor"),
            P("section", "tensor", "shards"),
            P(("shards", "tensor", "section")),
            P(("shards", "tensor", "section"), None),
            P(("shards", "tensor", "section"), None),
            P(("shards", "tensor", "section"), None),
            P("section", None),
            P("section", None),
            P("section", None),
            P(),
            P(),
            P(),
        ),
        check_vma=False,
    )
```

profile of v0, /device:TPU:0, one launch (start us, length us, event | category | flops | bytes accessed | tf_op | source)
XLA Modules:
  0.0 756.3 jit_solution(7406743752380418459)
XLA Ops:
  12.9 5.0 reshape.176
  21.1 4.2 convolution_convert_fusion
  25.3 6.8 maximum_bitcast_fusion
  32.7 11.0 %reduce.4 = bf16[32,122880]{1,0:T(8,128)(2,1)} reduce(bf16[32,1,122880]{2,0,1:T(8,128)(2,1)} %maximum_bitcast_fusion, bf16[]{:T(256)} %broadcast.176), dimensions={1}, to_apply=%copy.71.reduce_sub_computation | reduce | bytes 15728642 | tf_op jit(solution)/shard_map/all_to_all | solution.py:109
  43.7 10.4 %reshape.205 = bf16[32,2,61440]{2,1,0:T(2,128)(2,1)} reshape(bf16[32,122880]{1,0:T(8,128)(2,1)} %reduce.4) | data formatting | bytes 15728640
  54.1 8.5 %all-to-all-start = ((bf16[32,2,61440]{2,1,0:T(2,128)(2,1)}), bf16[32,2,61440]{2,1,0:T(2,128)(2,1)}, u32[]{:S(2)}, u32[]{:S(2)}) async-start(bf16[32,2,61440]{2,1,0:T(2,128)(2,1)} %reshape.205), calls=%async_computation | async-start | bytes 15728640 | tf_op jit(solution)/shard_map/all_to_all | solution.py:109
  66.3 94.9 %all-to-all-done = bf16[32,2,61440]{2,1,0:T(2,128)(2,1)} async-done(((bf16[32,2,61440]{2,1,0:T(2,128)(2,1)}), bf16[32,2,61440]{2,1,0:T(2,128)(2,1)}, u32[]{:S(2)}, u32[]{:S(2)}) %all-to-all-start) | async-done | bytes 7864352 | tf_op jit(solution)/shard_map/all_to_all | solution.py:109
  161.3 23.8 %reshape.206 = bf16[32,1,122880]{2,1,0:T(2,128)(2,1)} reshape(bf16[32,2,61440]{2,1,0:T(2,128)(2,1)} %all-to-all-done) | data formatting | bytes 15728640
  185.1 17.1 %copy.103 = bf16[32,1,122880]{2,0,1:T(8,128)(2,1)} copy(bf16[32,1,122880]{2,1,0:T(2,128)(2,1)} %reshape.206) | data formatting | bytes 15728640
  204.1 7.6 %slice_convert_fusion = f32[32,90112]{1,0:T(8,128)} fusion(bf16[32,122880]{1,0:T(8,128)(2,1)} %bitcast.90), kind=kLoop, calls=%fused_computation.31 | loop fusion | flops 2883584 | bytes 17301504 | tf_op jit(solution)/shard_map/transpose | solution.py:123
  213.0 4.8 copy.105
  217.8 36.5 %conditional.2 = (bf16[1024,1024]{1,0:T(8,128)(2,1)S(1)}, f32[]{:T(128)}) conditional(s32[]{:T(128)} %convert_element_type.167, () %tuple.24, f32[8,128,4,256]{3,2,1,0:T(4,128)} %bitcast.88), branch_computations={%region_1.0_spmd, %region_2.4_spmd} | conditional | flops 12907970560 | bytes 35651640 | solution.py:128
  217.8 4.9 multiply_reduce_fusion
  230.6 8.8 %add_convert_fusion.2 = bf16[1024,1024]{1,0:T(8,128)(2,1)} fusion(bf16[1024,1024]{1,0:T(8,128)(2,1)S(1)} %bitcast.108, bf16[1024,1024]{1,0:T(8,128)(2,1)} %fusion.38), kind=kOutput, calls=%fused_computation.4 | convolution fusion | flops 4304404480 | bytes 6291456 | tf_op jit(solution)/shard_map/cond/branch_1_fun/dot_general | solution.py:31
  239.5 5.9 fusion.39
  245.4 8.8 %add_convert_fusion = bf16[1024,1024]{1,0:T(8,128)(2,1)S(1)} fusion(bf16[1024,1024]{1,0:T(8,128)(2,1)} %add_convert_fusion.2, bf16[1024,1024]{1,0:T(8,128)(2,1)} %fusion.39), kind=kOutput, calls=%fused_computation.2 | convolution fusion | flops 4304404480 | bytes 6291456 | tf_op jit(solution)/shard_map/cond/branch_1_fun/dot_general | solution.py:31
  260.3 12.1 %reshape.187 = f32[8,4,128,704]{3,2,1,0:T(8,128)} reshape(f32[32,90112]{1,0:T(8,128)} %slice_convert_fusion) | data formatting | bytes 23068672 | tf_op jit(solution)/shard_map/transpose | solution.py:123
  272.4 11.3 %conditional.3 = (bf16[1024,2816]{1,0:T(8,128)(2,1)}, f32[]{:T(128)}) conditional(s32[]{:T(128)} %convert_element_type.176, () %tuple.25, f32[8,128,4,704]{3,1,2,0:T(8,128)} %bitcast.87), branch_computations={%region_5.0_spmd, %region_6.0_spmd} | conditional | flops 27962376192 | bytes 174063744 | solution.py:129
  283.7 14.0 %reshape.204 = bf16[8,128,4,704]{3,2,1,0:T(4,128)(2,1)} reshape(bf16[1024,2816]{1,0:T(8,128)(2,1)} %get-tuple-element.25) | data formatting | bytes 11534336 | tf_op jit(solution)/shard_map/reshape | solution.py:136
  297.7 6.6 copy.104
  304.4 10.1 %reshape.182 = bf16[32,90112]{1,0:T(8,128)(2,1)} reshape(bf16[8,4,128,704]{3,2,1,0:T(8,128)(2,1)} %bitcast.93) | data formatting | bytes 11534336 | tf_op jit(solution)/shard_map/reshape | solution.py:138
  314.5 6.2 maximum_bitcast_fusion.1
  320.7 11.0 %reduce.5 = bf16[32,122880]{1,0:T(8,128)(2,1)} reduce(bf16[32,1,122880]{2,0,1:T(8,128)(2,1)} %maximum_bitcast_fusion.1, bf16[]{:T(256)} %broadcast.176), dimensions={1}, to_apply=%copy.77.reduce_sub_computation | reduce | bytes 15728642 | tf_op jit(solution)/shard_map/all_to_all | solution.py:141
  331.6 10.4 %reshape.207 = bf16[32,2,61440]{2,1,0:T(2,128)(2,1)} reshape(bf16[32,122880]{1,0:T(8,128)(2,1)} %reduce.5) | data formatting | bytes 15728640
  342.1 46.6 %all-to-all-start.1 = ((bf16[32,2,61440]{2,1,0:T(2,128)(2,1)}), bf16[32,2,61440]{2,1,0:T(2,128)(2,1)}, u32[]{:S(2)}, u32[]{:S(2)}) async-start(bf16[32,2,61440]{2,1,0:T(2,128)(2,1)} %reshape.207), calls=%async_computation.1 | async-start | bytes 15728640 | tf_op jit(solution)/shard_map/all_to_all | solution.py:141
  388.9 159.0 %psum.15 = f32[32,16]{0,1:T(8,128)S(1)} all-reduce(f32[32,16]{0,1:T(8,128)S(1)} %bitcast.112), channel_id=1, replica_groups=mesh['shards'=8,'tensor'=4,'section'=4] {'shards','tensor','section'}, use_global_device_ids=true, to_apply=%region_9.10 | all-reduce | flops 512 | bytes 4096 | tf_op jit(solution)/shard_map/psum | solution.py:158
  547.9 125.6 %psum.14 = bf16[4,2048]{1,0:T(4,128)(2,1)S(1)} all-reduce(bf16[4,2048]{1,0:T(4,128)(2,1)S(1)} %bitcast.109), channel_id=1, replica_groups=mesh['shards'=8,'tensor'=4,'section'=4] {'shards','tensor'}, use_global_device_ids=true, to_apply=%region_8.9 | all-reduce | flops 8192 | bytes 32768 | tf_op jit(solution)/shard_map/psum | solution.py:155
  678.2 23.2 %reshape.208 = bf16[32,1,122880]{2,1,0:T(2,128)(2,1)} reshape(bf16[32,2,61440]{2,1,0:T(2,128)(2,1)} %all-to-all-done.1) | data formatting | bytes 15728640
  701.3 17.1 %copy.102 = bf16[32,1,122880]{2,0,1:T(8,128)(2,1)} copy(bf16[32,1,122880]{2,1,0:T(2,128)(2,1)} %reshape.208) | data formatting | bytes 15728640
  720.2 5.6 slice.39
  725.7 9.0 %gather_fusion.1 = bf16[12,90112]{1,0:T(8,128)(2,1)} fusion(bf16[32,90112]{1,0:T(8,128)(2,1)} %slice.39, s32[1024]{0:T(1024)S(1)} %pad_clamp_fusion), kind=kCustom, calls=%fused_computation.1 | custom fusion | bytes 4325424 | tf_op jit(solution)/shard_map/jit(_take)/gather | solution.py:149
  734.7 5.2 gather.15
  (88 shorter events, 58.9 us)
Async XLA Ops:
  1.4 5.5 copy-start.16
  2.3 4.7 copy-start.8
  2.3 4.7 copy-start.9
  5.4 2.8 copy-start.3
  5.4 2.8 copy-start.4
  54.1 8.5 %copy-start.10 = (s32[4,7]{1,0:T(4,128)S(1)}, s32[4,7]{1,0:T(4,128)}, u32[]{:S(2)}) copy-start(s32[4,7]{1,0:T(4,128)} %param.29) | copy-start | bytes 340
  54.1 107.2 %all-to-all-start = ((bf16[32,2,61440]{2,1,0:T(2,128)(2,1)}), bf16[32,2,61440]{2,1,0:T(2,128)(2,1)}, u32[]{:S(2)}, u32[]{:S(2)}) async-start(bf16[32,2,61440]{2,1,0:T(2,128)(2,1)} %reshape.205), calls=%async_computation | async-start | bytes 15728640 | tf_op jit(solution)/shard_map/all_to_all | solution.py:109
  342.0 46.6 %copy-start.11 = (s32[4,7]{1,0:T(4,128)S(1)}, s32[4,7]{1,0:T(4,128)}, u32[]{:S(2)}) copy-start(s32[4,7]{1,0:T(4,128)} %param.29) | copy-start | bytes 340
  342.0 46.7 %copy-start.17 = (s32[4,3]{1,0:T(4,128)S(1)}, s32[4,3]{1,0:T(4,128)}, u32[]{:S(2)}) copy-start(s32[4,3]{1,0:T(4,128)} %copy-done.16) | copy-start | bytes 148
  342.0 46.8 %copy-start.12 = (f32[4,1,2048]{2,1,0:T(1,128)S(1)}, f32[4,1,2048]{2,1,0:T(1,128)}, u32[]{:S(2)}) copy-start(f32[4,1,2048]{2,1,0:T(1,128)} %param.35) | copy-start | bytes 98308
  342.0 46.8 %copy-start.21 = (f32[1,32,16]{1,2,0:T(8,128)S(1)}, f32[1,32,16]{1,2,0:T(8,128)}, u32[]{:S(2)}) copy-start(f32[1,32,16]{1,2,0:T(8,128)} %param.39) | copy-start | bytes 6148
  342.1 331.5 %copy-start.18 = (f32[32,16]{0,1:T(8,128)S(1)}, f32[32,16]{0,1:T(8,128)}, u32[]{:S(2)}) copy-start(f32[32,16]{0,1:T(8,128)} %param.38) | copy-start | bytes 6148
  342.1 331.5 %copy-start.19 = (f32[32,16]{0,1:T(8,128)S(1)}, f32[32,16]{0,1:T(8,128)}, u32[]{:S(2)}) copy-start(f32[32,16]{0,1:T(8,128)} %param.41) | copy-start | bytes 6148
  342.1 331.5 %copy-start.20 = (f32[32,16]{0,1:T(8,128)S(1)}, f32[32,16]{0,1:T(8,128)}, u32[]{:S(2)}) copy-start(f32[32,16]{0,1:T(8,128)} %param.40) | copy-start | bytes 6148
  342.1 332.1 %copy-start.5 = (f32[251,1024]{1,0:T(8,128)S(1)}, f32[251,1024]{1,0:T(8,128)}, u32[]{:S(2)}) copy-start(f32[251,1024]{1,0:T(8,128)} %param.30) | copy-start | bytes 3084292
  342.1 332.1 %copy-start.6 = (f32[251,1024]{1,0:T(8,128)S(1)}, f32[251,1024]{1,0:T(8,128)}, u32[]{:S(2)}) copy-start(f32[251,1024]{1,0:T(8,128)} %param.33) | copy-start | bytes 3084292
  342.1 332.1 %copy-start.7 = (f32[251,1024]{1,0:T(8,128)S(1)}, f32[251,1024]{1,0:T(8,128)}, u32[]{:S(2)}) copy-start(f32[251,1024]{1,0:T(8,128)} %param.32) | copy-start | bytes 3084292
  342.1 336.0 %all-to-all-start.1 = ((bf16[32,2,61440]{2,1,0:T(2,128)(2,1)}), bf16[32,2,61440]{2,1,0:T(2,128)(2,1)}, u32[]{:S(2)}, u32[]{:S(2)}) async-start(bf16[32,2,61440]{2,1,0:T(2,128)(2,1)} %reshape.207), calls=%async_computation.1 | async-start | bytes 15728640 | tf_op jit(solution)/shard_map/all_to_all | solution.py:141
  674.2 3.2 copy-start.13
  674.3 3.2 copy-start.14
  674.3 3.2 copy-start.15
  734.7 5.2 copy-start.22
  747.9 3.6 copy-start.1
  747.9 5.2 copy-start.2
  747.9 5.2 copy-start.23
where the time goes:
time: 762 us; the launch traced here: 756 us
  blocking collectives  285 us (37%)
  local copies, waits for them, and re-layouts  204 us (27%)
  waiting for transfers between devices  94.9 us (12%)
  other arithmetic  69.7 us (9%)
  starting transfers between devices  55.1 us (7%)
  matrix products  34.7 us (5%)
  loops' own time  9.38 us (1%)
    psum x1, blocking collectives, on_device(): bias_grad = lax.psum(bias_partial[0], ('shards', 'tensor', 'section'))  159 us
    psum x1, blocking collectives, on_device(): lax.psum(norm_partial[:, 0].astype(jnp.bfloat16), ('shards', 'tensor'))  126 us
    unnamed x59, local copies, waits for them, and re-layouts  113 us
    all_to_all x1, waiting for transfers between devices, on_device(): lax.all_to_all(outgoing, ('shards', 'tensor'), split_axis=0, concat_axis=...  94.9 us
    all_to_all x1, starting transfers between devices, on_device(): lax.all_to_all(returning, ('shards', 'tensor'), split_axis=0, concat_axis...  46.6 us
    all_to_all x2, other arithmetic, on_device(): lax.all_to_all(outgoing, ('shards', 'tensor'), split_axis=0, concat_axis=...  17.8 us
    dot_general x2, matrix products, orthogonalize(): jnp.dot(polynomial, current, preferred_element_type=jnp.float32)  17.6 us
    all_to_all x2, other arithmetic, on_device(): lax.all_to_all(returning, ('shards', 'tensor'), split_axis=0, concat_axis...  17.2 us
  transfers between devices with their start and end apart: 2, of which 1 were waited for; matrix products, arithmetic and copies ran while one was open for 1% of the time, Pallas kernels for 0%

commit v1 on v0

v1 whole, which is shorter than its diff:
```python
import math

import jax
import jax.numpy as jnp
from jax import lax
from jax.sharding import PartitionSpec as P

D = 1024
FF = 2816
NS_STEPS = 2


coef_first = 3.4445
coef_second = -4.775
coef_third = 2.0315


def newton_schulz(blocks_bf16, norm_value):
    current = (blocks_bf16.astype(jnp.float32) / (norm_value + 1e-07)).astype(jnp.bfloat16)
    for sweep_index in range(NS_STEPS):
        gram_form = jnp.dot(current, current.T, preferred_element_type=jnp.float32).astype(
            jnp.bfloat16
        )
        square_form = jnp.dot(gram_form, gram_form, preferred_element_type=jnp.float32)
        polynomial = (
            coef_second * gram_form.astype(jnp.float32) + coef_third * square_form
        ).astype(jnp.bfloat16)
        current = (
            coef_first * current.astype(jnp.float32)
            + jnp.dot(polynomial, current, preferred_element_type=jnp.float32)
        ).astype(jnp.bfloat16)
    return current


def refresh(gradient, moment):
    fresh_moment = (0.95 * moment.astype(jnp.float32) + gradient.astype(jnp.float32)).astype(
        jnp.bfloat16
    )
    advance = (gradient.astype(jnp.float32) + 0.95 * fresh_moment.astype(jnp.float32)).astype(
        jnp.bfloat16
    )
    return (fresh_moment, advance)


def adamw_update(weight, gradient, moment, second, decay_rate):
    moment_new = 0.9 * moment + 0.1 * gradient
    second_new = 0.95 * second + 0.05 * gradient * gradient
    weight_new = weight - 0.02 * (moment_new / (jnp.sqrt(second_new) + 1e-08) + decay_rate * weight)
    return (weight_new, moment_new, second_new)


def block_plan(shards_count, tensor_count):
    kind = [0] * (shards_count * tensor_count)
    index = [0] * (shards_count * tensor_count)
    chips = [(x, z) for x in range(shards_count // 2) for z in range(tensor_count)]
    for number, (x, z) in enumerate(chips):
        kind[(2 * x + 1) * tensor_count + z] = 1
        index[(2 * x + 1) * tensor_count + z] = number
    for number, (x, z) in enumerate(chips[:12]):
        kind[(2 * x) * tensor_count + z] = 2
        index[(2 * x) * tensor_count + z] = number
    return kind, index


def on_device(
    attn_grad,
    mlp_in_grad,
    mlp_out_grad,
    attn_momentum,
    mlp_in_momentum,
    mlp_out_momentum,
    owners,
    embed_weight,
    embed_grad,
    embed_moment,
    embed_second,
    norm_scale,
    norm_partial,
    norm_moment,
    norm_second,
    bias_table,
    bias_partial,
    bias_moment,
    bias_second,
):
    shards_count = lax.axis_size("shards")
    tensor_count = lax.axis_size("tensor")
    group_count = shards_count * tensor_count
    my_index = lax.axis_index(("shards", "tensor"))
    my_row = my_index // tensor_count
    my_col = my_index % tensor_count
    layers_here = owners.shape[0]
    rows_block = attn_grad.shape[2]
    cols_block = attn_grad.shape[3]
    ff_block = mlp_in_grad.shape[3]
    square_width = rows_block * cols_block
    rect_width = rows_block * ff_block
    n_square = layers_here * 4
    n_rect = layers_here * 3
    kind_list, index_list = block_plan(shards_count, tensor_count)
    assert sum(k == 1 for k in kind_list) == n_square and sum(k == 2 for k in kind_list) == n_rect
    kind_table = jnp.array(kind_list, jnp.int32)
    index_table = jnp.array(index_list, jnp.int32)
    square_home = [0] * n_square
    rect_home = [0] * n_rect
    for device, (k, i) in enumerate(zip(kind_list, index_list)):
        if k == 1:
            square_home[i] = device
        elif k == 2:
            rect_home[i] = device

    attn_fresh, attn_ahead = refresh(attn_grad, attn_momentum)
    inner_fresh, inner_ahead = refresh(mlp_in_grad, mlp_in_momentum)
    outer_fresh, outer_ahead = refresh(mlp_out_grad, mlp_out_momentum)
    square_table = attn_ahead.reshape(n_square, rows_block, cols_block)
    rect_table = jnp.concatenate(
        [inner_ahead, jnp.swapaxes(outer_ahead, 1, 2)[:, None]], axis=1
    ).reshape(n_rect, rows_block, ff_block)

    square_ss = jnp.sum(jnp.square(square_table.astype(jnp.float32)), axis=(1, 2))
    rect_ss = jnp.sum(jnp.square(rect_table.astype(jnp.float32)), axis=(1, 2))
    norm_width = norm_partial.shape[0] * norm_partial.shape[2]
    packed = jnp.concatenate([norm_partial.reshape(norm_width), square_ss, rect_ss])
    packed = jnp.pad(packed, (0, (-packed.shape[0]) % 128))
    gathered = jnp.sum(lax.all_gather(packed, ("shards", "tensor"), axis=0, tiled=False), axis=0)
    norm_grad = gathered[:norm_width].reshape(norm_partial.shape[0], norm_partial.shape[2])
    square_norm = jnp.sqrt(gathered[norm_width : norm_width + n_square])
    rect_norm = jnp.sqrt(gathered[norm_width + n_square : norm_width + n_square + n_rect])
    bias_flat = bias_partial.reshape(-1)
    bias_pad = jnp.pad(bias_flat, (0, 2048 - bias_flat.shape[0]))
    bias_all = lax.all_gather(bias_pad, ("shards", "tensor", "section"), axis=0, tiled=False)
    bias_grad = jnp.sum(bias_all, axis=0)[: bias_flat.shape[0]].reshape(bias_table.shape)

    rms_all = jnp.concatenate(
        [
            square_norm.reshape(layers_here, 4) / math.sqrt(D * D),
            rect_norm.reshape(layers_here, 3) / math.sqrt(D * FF),
        ],
        axis=1,
    )
    owner_rms = jnp.sum(jnp.where(owners == my_index, rms_all, 0.0)).reshape(1)

    shifts = [(a, b) for a in range(shards_count) for b in range(tensor_count)]
    step_a = jnp.array([a for a, b in shifts], jnp.int32)
    step_b = jnp.array([b for a, b in shifts], jnp.int32)
    dest = ((my_row + step_a) % shards_count) * tensor_count + (my_col + step_b) % tensor_count
    dest_kind = kind_table[dest]
    dest_index = index_table[dest]
    square_rot = jnp.dot(
        ((dest_kind == 1)[:, None] & (dest_index[:, None] == jnp.arange(n_square)[None, :])).astype(
            jnp.bfloat16
        ),
        square_table.reshape(n_square, square_width),
        preferred_element_type=jnp.float32,
    ).astype(jnp.bfloat16)
    rect_rot = jnp.dot(
        ((dest_kind == 2)[:, None] & (dest_index[:, None] == jnp.arange(n_rect)[None, :])).astype(
            jnp.bfloat16
        ),
        rect_table.reshape(n_rect, rect_width),
        preferred_element_type=jnp.float32,
    ).astype(jnp.bfloat16)

    def shift_pairs(a, b, sign, wanted, by_dest):
        pairs = []
        for s in range(shards_count):
            for t in range(tensor_count):
                src = s * tensor_count + t
                dst = ((s + sign * a) % shards_count) * tensor_count + (t + sign * b) % tensor_count
                if kind_list[dst if by_dest else src] == wanted:
                    pairs.append((src, dst))
        return pairs

    square_in = [square_rot[0]]
    rect_in = [rect_rot[0]]
    for k, (a, b) in enumerate(shifts[1:], start=1):
        square_in.append(
            lax.ppermute(square_rot[k], ("shards", "tensor"), shift_pairs(a, b, 1, 1, True))
        )
        rect_in.append(lax.ppermute(rect_rot[k], ("shards", "tensor"), shift_pairs(a, b, 1, 2, True)))

    def assemble(blocks, width):
        rows = [
            jnp.concatenate(blocks[a * tensor_count : (a + 1) * tensor_count], axis=1).reshape(
                rows_block, tensor_count * width
            )
            for a in range(shards_count)
        ]
        return jnp.concatenate(rows, axis=0)

    def run(blocks, width, norm_value):
        whole = assemble([x.reshape(rows_block, width) for x in blocks], width)
        done = newton_schulz(whole, norm_value)
        return [
            done[a * rows_block : (a + 1) * rows_block, b * width : (b + 1) * width]
            for a, b in shifts
        ]

    my_kind = kind_table[my_index]
    my_mat = index_table[my_index]

    def square_branch(operands):
        square_blocks, rect_blocks = operands
        out = run(square_blocks, cols_block, square_norm[my_mat])
        return jnp.stack(out), jnp.zeros((group_count, rows_block, ff_block), jnp.bfloat16)

    def rect_branch(operands):
        square_blocks, rect_blocks = operands
        out = run(rect_blocks, ff_block, rect_norm[my_mat])
        return jnp.zeros((group_count, rows_block, cols_block), jnp.bfloat16), jnp.stack(out)

    def idle_branch(operands):
        return (
            jnp.zeros((group_count, rows_block, cols_block), jnp.bfloat16),
            jnp.zeros((group_count, rows_block, ff_block), jnp.bfloat16),
        )

    square_done, rect_done = lax.switch(
        my_kind, [idle_branch, square_branch, rect_branch], (square_in, rect_in)
    )

    square_back = [square_done[0]]
    rect_back = [rect_done[0]]
    for k, (a, b) in enumerate(shifts[1:], start=1):
        square_back.append(
            lax.ppermute(square_done[k], ("shards", "tensor"), shift_pairs(a, b, -1, 1, False))
        )
        rect_back.append(
            lax.ppermute(rect_done[k], ("shards", "tensor"), shift_pairs(a, b, -1, 2, False))
        )
    square_back = jnp.stack(square_back).reshape(group_count, square_width)
    rect_back = jnp.stack(rect_back).reshape(group_count, rect_width)

    def arrival_round(home):
        home = jnp.array(home, jnp.int32)
        a = (home // tensor_count - my_row) % shards_count
        b = (home % tensor_count - my_col) % tensor_count
        return a * tensor_count + b

    square_pick = (
        arrival_round(square_home)[:, None] == jnp.arange(group_count)[None, :]
    ).astype(jnp.bfloat16)
    rect_pick = (arrival_round(rect_home)[:, None] == jnp.arange(group_count)[None, :]).astype(
        jnp.bfloat16
    )
    square_rows = jnp.dot(square_pick, square_back, preferred_element_type=jnp.float32).reshape(
        layers_here, 4, rows_block, cols_block
    ) * (0.2 * math.sqrt(D))
    rect_rows = jnp.dot(rect_pick, rect_back, preferred_element_type=jnp.float32).reshape(
        layers_here, 3, rows_block, ff_block
    ) * (0.2 * math.sqrt(FF))
    mlp_in_update = rect_rows[:, :2]
    mlp_out_update = jnp.swapaxes(rect_rows[:, 2], 1, 2)

    embed_results = adamw_update(
        embed_weight, embed_grad.astype(jnp.float32), embed_moment, embed_second, 0.1
    )
    norm_results = adamw_update(norm_scale, norm_grad, norm_moment, norm_second, 0.0)
    bias_results = adamw_update(bias_table, bias_grad, bias_moment, bias_second, 0.0)
    return (
        attn_fresh,
        inner_fresh,
        outer_fresh,
        square_rows,
        mlp_in_update,
        mlp_out_update,
        owner_rms,
        embed_results[0],
        embed_results[1],
        embed_results[2],
        norm_results[0],
        norm_results[1],
        norm_results[2],
        bias_results[0],
        bias_results[1],
        bias_results[2],
    )


def solution(mesh):
    placed = (
        P("section", None, "shards", "tensor"),
        P("section", None, "shards", "tensor"),
        P("section", "tensor", "shards"),
        P("section", None, "shards", "tensor"),
        P("section", None, "shards", "tensor"),
        P("section", "tensor", "shards"),
        P("section", None),
        P(("shards", "tensor", "section"), None),
        P(("shards", "tensor", "section"), None),
        P(("shards", "tensor", "section"), None),
        P(("shards", "tensor", "section"), None),
        P("section", None),
        P("section", ("shards", "tensor"), None),
        P("section", None),
        P("section", None),
        P(),
        P(("shards", "tensor", "section"), None, None),
        P(),
        P(),
    )
    return jax.shard_map(
        on_device,
        mesh=mesh,
        in_specs=placed,
        out_specs=(
            P("section", None, "shards", "tensor"),
            P("section", None, "shards", "tensor"),
            P("section", "tensor", "shards"),
            P("section", None, "shards", "tensor"),
            P("section", None, "shards", "tensor"),
            P("section", "tensor", "shards"),
            P(("shards", "tensor", "section")),
            P(("shards", "tensor", "section"), None),
            P(("shards", "tensor", "section"), None),
            P(("shards", "tensor", "section"), None),
            P("section", None),
            P("section", None),
            P("section", None),
            P(),
            P(),
            P(),
        ),
        check_vma=False,
    )
```

time: 762 us -> 1320 us (1.73)
  the two profiles are of different devices: /device:TPU:0 before, /device:TPU:2 now
where the time goes in v1:
time: 1320 us; the launch traced here: 1300 us
  starting transfers between devices  863 us (65%)
  local copies, waits for them, and re-layouts  313 us (24%)
  matrix products  59.5 us (5%)
  other arithmetic  20.5 us (2%)
  between operations  19.3 us (1%)
    ppermute x31, starting transfers between devices, on_device(): lax.ppermute(rect_rot[k], ('shards', 'tensor'), shift_pairs(a, b, 1, 2, T...  263 us
    ppermute x31, starting transfers between devices, on_device(): lax.ppermute(square_rot[k], ('shards', 'tensor'), shift_pairs(a, b, 1, 1,...  206 us
    ppermute x31, starting transfers between devices, on_device(): lax.ppermute(rect_done[k], ('shards', 'tensor'), shift_pairs(a, b, -1, 2,...  197 us
    ppermute x31, starting transfers between devices, on_device(): lax.ppermute(square_done[k], ('shards', 'tensor'), shift_pairs(a, b, -1,...  197 us
    another operation x33, local copies, waits for them, and re-layouts, on_device(): rect_back = jnp.stack(rect_back).reshape(group_count, rect_width)  80.5 us
    slice x2, local copies, waits for them, and re-layouts, on_device(): rect_rot[k]  49.3 us
    cond x76, local copies, waits for them, and re-layouts  43.9 us
    unnamed x336, local copies, waits for them, and re-layouts  39.8 us
  transfers between devices with their start and end apart: 126, of which 2 were waited for; matrix products, arithmetic and copies ran while one was open for 14% of the time, Pallas kernels for 0%

profile of v1, /device:TPU:2, one launch (start us, length us, event | category | flops | bytes accessed | tf_op | source)
XLA Modules:
  0.0 1295.8 jit_solution(4532017407508907768)
XLA Ops:
  25.9 11.6 collective-permute-start.12
  37.4 10.8 collective-permute-start.13
  48.2 10.8 collective-permute-start.14
  78.8 20.4 %collective-permute-start.19 = (bf16[32768]{0:T(1024)(128)(2,1)}, bf16[32768]{0:T(1024)(128)(2,1)S(1)}, u32[]{:S(2)}, u32[]{:S(2)}) collective-permute-start(bf16[32768]{0:T(1024)(128)(2,1)} %get-tuple-element.350), channel_id=1, source_target_pairs={{0,80},{4,84},{8,88},{12,92},{32,112},{36,116},{40,120},{44,124},{... | collective-permute-start | bytes 196616 | tf_op jit(solution)/shard_map/ppermute | solution.py:178
  135.7 24.9 %slice_reduce_fusion.2 = (bf16[90112]{0:T(1024)(128)(2,1)}, bf16[90112]{0:T(1024)(128)(2,1)}, bf16[90112]{0:T(1024)(128)(2,1)}, bf16[90112]{0:T(1024)(128)(2,1)}...) fusion(bf16[32,90112]{1,0:T(8,128)(2,1)S(1)} %convolution_conve, ...), kind=kLoop, calls=%fused_computation.199 | loop fusion | bytes 6848512 | tf_op jit(solution)/shard_map/slice | solution.py:180
  162.1 19.5 %collective-permute-start.27 = (bf16[32768]{0:T(1024)(128)(2,1)S(1)}, bf16[32768]{0:T(1024)(128)(2,1)S(1)}, u32[]{:S(2)}, u32[]{:S(2)}) collective-permute-start(bf16[32768]{0:T(1024)(128)(2,1)S(1)} %copy-done.83), channel_id=1, source_target_pairs={{0,112},{4,116},{8,120},{12,124},{32,16},{36,20},{40,24},{44,28},{... | collective-permute-start | bytes 196616 | tf_op jit(solution)/shard_map/ppermute | solution.py:178
  216.7 11.9 collective-permute-start.30
  234.8 13.8 %collective-permute-start.11 = (bf16[32768]{0:T(1024)(128)(2,1)}, bf16[32768]{0:T(1024)(128)(2,1)S(1)}, u32[]{:S(2)}, u32[]{:S(2)}) collective-permute-start(bf16[32768]{0:T(1024)(128)(2,1)} %get-tuple-element.358), channel_id=1, source_target_pairs={{0,48},{4,52},{8,56},{12,60},{32,80},{36,84},{40,88},{44,92},{64,1... | collective-permute-start | bytes 196616 | tf_op jit(solution)/shard_map/ppermute | solution.py:178
  249.3 10.8 collective-permute-start.3
  293.6 11.3 collective-permute-start.47
  407.2 18.0 %collective-permute-start.58 = (bf16[90112]{0:T(1024)(128)(2,1)}, bf16[90112]{0:T(1024)(128)(2,1)S(1)}, u32[]{:S(2)}, u32[]{:S(2)}) collective-permute-start(bf16[90112]{0:T(1024)(128)(2,1)} %get-tuple-element.311), channel_id=1, source_target_pairs={{16,0},{20,4},{24,8},{28,12},{48,32},{52,36},{56,40},{60,44},{80,6... | collective-permute-start | bytes 540680 | tf_op jit(solution)/shard_map/ppermute | solution.py:180
  425.3 24.3 %slice_reduce_fusion.21 = (bf16[90112]{0:T(1024)(128)(2,1)S(1)}, bf16[90112]{0:T(1024)(128)(2,1)S(1)}, bf16[90112]{0:T(1024)(128)(2,1)S(1)}, bf16[90112]{0:T(102...) fusion(bf16[32,90112]{1,0:T(8,128)(2,1)} %copy-done.2), kind=kLoop, calls=%fused_computation.218 | loop fusion | bytes 4325376 | tf_op jit(solution)/shard_map/slice | solution.py:180
  545.1 11.5 collective-permute-start.42
  557.9 11.2 collective-permute-start.5
  583.1 131.2 %conditional.1 = (bf16[32,128,256]{2,1,0:T(8,128)(2,1)}, bf16[32,128,704]{2,1,0:T(8,128)(2,1)}) conditional(s32[]{:T(128)} %bitcast.69, () %tuple.20, (bf16[32,32768]{1,0:T(8,128)(2,1)S(1)}, bf16[32768]{0:T(1024)(128)(2,1)}, bf16[32768]{0:T(1024)(128)(2,1)}, bf16[32768]{0:T(1024)(128)(2,1)}, bf16[32768]{0:T(1024)(128)(2,1)}, ...), branch_computations={%region_3.4_spmd, %region_4.5_spmd, %region_5.6_spmd} | conditional | flops 27976794112 | bytes 128385736 | solution.py:218
  634.4 14.8 %add_convert_fusion.5 = bf16[1024,2816]{1,0:T(8,128)(2,1)} fusion(f32[]{:T(128)} %bitcast.33, bf16[1024,2816]{1,0:T(8,128)(2,1)} %constant_dynamic-update-slice_fusion.32, bf16[1024,1024]{1,0:T(8,128)(2,1)S(1)} %fusion.45), kind=kOutput, calls=%fused_computation.88 | convolution fusion | flops 8087142400 | bytes 13631492 | tf_op jit(solution)/shard_map/cond/branch_2_fun/dot_general | solution.py:30
  659.8 14.6 %add_convert_fusion.4 = bf16[1024,2816]{1,0:T(8,128)(2,1)} fusion(bf16[1024,2816]{1,0:T(8,128)(2,1)} %add_convert_fusion.5, bf16[1024,1024]{1,0:T(8,128)(2,1)S(1)} %fusion.102), kind=kOutput, calls=%fused_computation.87 | convolution fusion | flops 8069840896 | bytes 13631488 | tf_op jit(solution)/shard_map/cond/branch_2_fun/dot_general | solution.py:30
  751.7 18.8 %collective-permute-start.81 = (bf16[128,256]{1,0:T(8,128)(2,1)S(1)}, bf16[128,256]{1,0:T(8,128)(2,1)S(1)}, u32[]{:S(2)}, u32[]{:S(2)}) collective-permute-start(bf16[128,256]{1,0:T(8,128)(2,1)S(1)} %get-tuple-element.429), channel_id=1, source_target_pairs={{16,64},{20,68},{24,72},{28,76},{48,96},{52,100},{56,104},{60,108}... | collective-permute-start | bytes 196616 | tf_op jit(solution)/shard_map/ppermute | solution.py:226
  807.5 15.9 %collective-permute-start.89 = (bf16[128,256]{1,0:T(8,128)(2,1)S(1)}, bf16[128,256]{1,0:T(8,128)(2,1)S(1)}, u32[]{:S(2)}, u32[]{:S(2)}) collective-permute-start(bf16[128,256]{1,0:T(8,128)(2,1)S(1)} %get-tuple-element.421), channel_id=1, source_target_pairs={{16,32},{20,36},{24,40},{28,44},{48,64},{52,68},{56,72},{60,76},{8... | collective-permute-start | bytes 196616 | tf_op jit(solution)/shard_map/ppermute | solution.py:226
  858.6 16.6 %collective-permute-start.65 = (bf16[128,256]{1,0:T(8,128)(2,1)}, bf16[128,256]{1,0:T(8,128)(2,1)S(1)}, u32[]{:S(2)}, u32[]{:S(2)}) collective-permute-start(bf16[128,256]{1,0:T(8,128)(2,1)} %get-tuple-element.445), channel_id=1, source_target_pairs={{16,0},{20,4},{24,8},{28,12},{48,32},{52,36},{56,40},{60,44},{80,6... | collective-permute-start | bytes 196616 | tf_op jit(solution)/shard_map/ppermute | solution.py:226
  909.4 12.8 collective-permute-start.105
  924.3 16.6 %collective-permute-start.73 = (bf16[128,256]{1,0:T(8,128)(2,1)S(1)}, bf16[128,256]{1,0:T(8,128)(2,1)S(1)}, u32[]{:S(2)}, u32[]{:S(2)}) collective-permute-start(bf16[128,256]{1,0:T(8,128)(2,1)S(1)} %copy-done.174), channel_id=1, source_target_pairs={{16,96},{20,100},{24,104},{28,108},{48,0},{52,4},{56,8},{60,12},{8... | collective-permute-start | bytes 196616 | tf_op jit(solution)/shard_map/ppermute | solution.py:226
  943.2 10.6 collective-permute-start.106
  1052.7 10.9 collective-permute-start.97
  1063.6 10.9 collective-permute-start.98
  1074.5 11.3 collective-permute-start.99
  1112.8 11.5 stack.426
  1134.6 10.8 collective-permute-start.101
  1145.4 10.8 collective-permute-start.102
  1156.3 10.9 collective-permute-start.103
  1167.2 11.7 collective-permute-start.104
  1228.7 33.1 %stack.459 = bf16[32,90112]{1,0:T(8,128)(2,1)} concatenate(bf16[1,90112]{1,0:T(2,128)(2,1)S(1)} %stack.427, bf16[1,90112]{1,0:T(2,128)(2,1)} %stack.428, bf16[1,90112]{1,0:T(2,128)(2,1)} %stack.429, bf16[1,90112]{1,0:T(2,128)(2,1)} %stack.430, bf16[1,90112]{1,0:T(2,128)(2,1)} %stack.431, bf16[1,90112]{1,0:T(2,128)(2,1)} %stack.432, bf16[1,90112]{1,0:T(2,128)(2,1)} %stack.433, ...), dimensions={0} | concatenate | bytes 11534336 | tf_op jit(solution)/shard_map/stack | solution.py:232
  (777 shorter events, 811.4 us)
Async XLA Ops:
  8.0 523.9 %all-gather.8.cloned.1.call-start = ((), (), s32[]{:S(2)}) async-start(), calls=%async_computation.1 | async-start | bytes 1098240 | tf_op jit(solution)/shard_map/all_gather | solution.py:125
  25.9 51.6 %collective-permute-start.12 = (bf16[32768]{0:T(1024)(128)(2,1)}, bf16[32768]{0:T(1024)(128)(2,1)}, u32[]{:S(2)}, u32[]{:S(2)}) collective-permute-start(bf16[32768]{0:T(1024)(128)(2,1)} %get-tuple-element.357), channel_id=1, source_target_pairs={{0,52},{4,56},{8,60},{12,48},{32,84},{36,88},{40,92},{44,80},{64,1... | collective-permute-start | bytes 196616 | tf_op jit(solution)/shard_map/ppermute | solution.py:178
  60.3 52.8 %collective-permute-start.16 = (bf16[32768]{0:T(1024)(128)(2,1)}, bf16[32768]{0:T(1024)(128)(2,1)}, u32[]{:S(2)}, u32[]{:S(2)}) collective-permute-start(bf16[32768]{0:T(1024)(128)(2,1)} %get-tuple-element.353), channel_id=1, source_target_pairs={{16,84},{20,88},{24,92},{28,80},{48,116},{52,120},{56,124},{60,112... | collective-permute-start | bytes 196616 | tf_op jit(solution)/shard_map/ppermute | solution.py:178
  78.1 55.4 %collective-permute-start.18 = (bf16[32768]{0:T(1024)(128)(2,1)}, bf16[32768]{0:T(1024)(128)(2,1)S(1)}, u32[]{:S(2)}, u32[]{:S(2)}) collective-permute-start(bf16[32768]{0:T(1024)(128)(2,1)} %get-tuple-element.351), channel_id=1, source_target_pairs={{16,92},{20,80},{24,84},{28,88},{48,124},{52,112},{56,116},{60,120... | collective-permute-start | bytes 196616 | tf_op jit(solution)/shard_map/ppermute | solution.py:178
  78.8 55.4 %collective-permute-start.19 = (bf16[32768]{0:T(1024)(128)(2,1)}, bf16[32768]{0:T(1024)(128)(2,1)S(1)}, u32[]{:S(2)}, u32[]{:S(2)}) collective-permute-start(bf16[32768]{0:T(1024)(128)(2,1)} %get-tuple-element.350), channel_id=1, source_target_pairs={{0,80},{4,84},{8,88},{12,92},{32,112},{36,116},{40,120},{44,124},{... | collective-permute-start | bytes 196616 | tf_op jit(solution)/shard_map/ppermute | solution.py:178
  102.9 57.8 %collective-permute-start.20 = (bf16[32768]{0:T(1024)(128)(2,1)S(1)}, bf16[32768]{0:T(1024)(128)(2,1)S(1)}, u32[]{:S(2)}, u32[]{:S(2)}) collective-permute-start(bf16[32768]{0:T(1024)(128)(2,1)S(1)} %copy-done.90), channel_id=1, source_target_pairs={{0,84},{4,88},{8,92},{12,80},{32,116},{36,120},{40,124},{44,112},{... | collective-permute-start | bytes 196616 | tf_op jit(solution)/shard_map/ppermute | solution.py:178
  134.9 56.9 %collective-permute-start.24 = (bf16[32768]{0:T(1024)(128)(2,1)S(1)}, bf16[32768]{0:T(1024)(128)(2,1)S(1)}, u32[]{:S(2)}, u32[]{:S(2)}) collective-permute-start(bf16[32768]{0:T(1024)(128)(2,1)S(1)} %copy-done.86), channel_id=1, source_target_pairs={{16,116},{20,120},{24,124},{28,112},{48,20},{52,24},{56,28},{60,16... | collective-permute-start | bytes 196616 | tf_op jit(solution)/shard_map/ppermute | solution.py:178
  161.4 55.3 %collective-permute-start.26 = (bf16[32768]{0:T(1024)(128)(2,1)S(1)}, bf16[32768]{0:T(1024)(128)(2,1)S(1)}, u32[]{:S(2)}, u32[]{:S(2)}) collective-permute-start(bf16[32768]{0:T(1024)(128)(2,1)S(1)} %copy-done.84), channel_id=1, source_target_pairs={{16,124},{20,112},{24,116},{28,120},{48,28},{52,16},{56,20},{60,24... | collective-permute-start | bytes 196616 | tf_op jit(solution)/shard_map/ppermute | solution.py:178
  162.1 66.5 %collective-permute-start.27 = (bf16[32768]{0:T(1024)(128)(2,1)S(1)}, bf16[32768]{0:T(1024)(128)(2,1)S(1)}, u32[]{:S(2)}, u32[]{:S(2)}) collective-permute-start(bf16[32768]{0:T(1024)(128)(2,1)S(1)} %copy-done.83), channel_id=1, source_target_pairs={{0,112},{4,116},{8,120},{12,124},{32,16},{36,20},{40,24},{44,28},{... | collective-permute-start | bytes 196616 | tf_op jit(solution)/shard_map/ppermute | solution.py:178
  207.2 97.7 %collective-permute-start.43 = (bf16[90112]{0:T(1024)(128)(2,1)}, bf16[90112]{0:T(1024)(128)(2,1)}, u32[]{:S(2)}, u32[]{:S(2)}) collective-permute-start(bf16[90112]{0:T(1024)(128)(2,1)} %get-tuple-element.326), channel_id=1, source_target_pairs={{16,68},{20,72},{24,76},{28,64},{80,4},{84,8},{88,12},{92,0},{112,... | collective-permute-start | bytes 540680 | tf_op jit(solution)/shard_map/ppermute | solution.py:180
  234.7 803.6 %all-gather.6.cloned.1.call-start = ((), (), s32[]{:S(2)}) async-start(), calls=%async_computation | async-start | bytes 1056768 | tf_op jit(solution)/shard_map/all_gather | solution.py:131
  293.6 51.9 %collective-permute-start.47 = (bf16[90112]{0:T(1024)(128)(2,1)}, bf16[90112]{0:T(1024)(128)(2,1)S(1)}, u32[]{:S(2)}, u32[]{:S(2)}) collective-permute-start(bf16[90112]{0:T(1024)(128)(2,1)} %get-tuple-element.322), channel_id=1, source_target_pairs={{0,68},{4,72},{8,76},{12,64},{64,4},{68,8},{72,12},{76,0},{96,36},... | collective-permute-start | bytes 540680 | tf_op jit(solution)/shard_map/ppermute | solution.py:180
  345.4 50.9 %collective-permute-start.52 = (bf16[90112]{0:T(1024)(128)(2,1)}, bf16[90112]{0:T(1024)(128)(2,1)S(1)}, u32[]{:S(2)}, u32[]{:S(2)}) collective-permute-start(bf16[90112]{0:T(1024)(128)(2,1)} %get-tuple-element.317), channel_id=1, source_target_pairs={{48,8},{52,12},{56,0},{60,4},{80,40},{84,44},{88,32},{92,36},{112,... | collective-permute-start | bytes 540680 | tf_op jit(solution)/shard_map/ppermute | solution.py:180
  355.4 51.2 %collective-permute-start.53 = (bf16[90112]{0:T(1024)(128)(2,1)}, bf16[90112]{0:T(1024)(128)(2,1)S(1)}, u32[]{:S(2)}, u32[]{:S(2)}) collective-permute-start(bf16[90112]{0:T(1024)(128)(2,1)} %get-tuple-element.316), channel_id=1, source_target_pairs={{48,12},{52,0},{56,4},{60,8},{80,44},{84,32},{88,36},{92,40},{112,... | collective-permute-start | bytes 540680 | tf_op jit(solution)/shard_map/ppermute | solution.py:180
  365.3 84.3 %collective-permute-start.54 = (bf16[90112]{0:T(1024)(128)(2,1)}, bf16[90112]{0:T(1024)(128)(2,1)S(1)}, u32[]{:S(2)}, u32[]{:S(2)}) collective-permute-start(bf16[90112]{0:T(1024)(128)(2,1)} %get-tuple-element.315), channel_id=1, source_target_pairs={{32,0},{36,4},{40,8},{44,12},{64,32},{68,36},{72,40},{76,44},{96,6... | collective-permute-start | bytes 540680 | tf_op jit(solution)/shard_map/ppermute | solution.py:180
  375.9 83.9 %collective-permute-start.55 = (bf16[90112]{0:T(1024)(128)(2,1)}, bf16[90112]{0:T(1024)(128)(2,1)S(1)}, u32[]{:S(2)}, u32[]{:S(2)}) collective-permute-start(bf16[90112]{0:T(1024)(128)(2,1)} %get-tuple-element.314), channel_id=1, source_target_pairs={{32,4},{36,8},{40,12},{44,0},{64,36},{68,40},{72,44},{76,32},{96,6... | collective-permute-start | bytes 540680 | tf_op jit(solution)/shard_map/ppermute | solution.py:180
  386.1 83.6 %collective-permute-start.56 = (bf16[90112]{0:T(1024)(128)(2,1)}, bf16[90112]{0:T(1024)(128)(2,1)S(1)}, u32[]{:S(2)}, u32[]{:S(2)}) collective-permute-start(bf16[90112]{0:T(1024)(128)(2,1)} %get-tuple-element.313), channel_id=1, source_target_pairs={{32,8},{36,12},{40,0},{44,4},{64,40},{68,44},{72,32},{76,36},{96,7... | collective-permute-start | bytes 540680 | tf_op jit(solution)/shard_map/ppermute | solution.py:180
  396.3 83.3 %collective-permute-start.57 = (bf16[90112]{0:T(1024)(128)(2,1)}, bf16[90112]{0:T(1024)(128)(2,1)S(1)}, u32[]{:S(2)}, u32[]{:S(2)}) collective-permute-start(bf16[90112]{0:T(1024)(128)(2,1)} %get-tuple-element.312), channel_id=1, source_target_pairs={{32,12},{36,0},{40,4},{44,8},{64,44},{68,32},{72,36},{76,40},{96,7... | collective-permute-start | bytes 540680 | tf_op jit(solution)/shard_map/ppermute | solution.py:180
  407.2 76.0 %collective-permute-start.58 = (bf16[90112]{0:T(1024)(128)(2,1)}, bf16[90112]{0:T(1024)(128)(2,1)S(1)}, u32[]{:S(2)}, u32[]{:S(2)}) collective-permute-start(bf16[90112]{0:T(1024)(128)(2,1)} %get-tuple-element.311), channel_id=1, source_target_pairs={{16,0},{20,4},{24,8},{28,12},{48,32},{52,36},{56,40},{60,44},{80,6... | collective-permute-start | bytes 540680 | tf_op jit(solution)/shard_map/ppermute | solution.py:180
  747.1 53.2 %collective-permute-start.80 = (bf16[128,256]{1,0:T(8,128)(2,1)S(1)}, bf16[128,256]{1,0:T(8,128)(2,1)S(1)}, u32[]{:S(2)}, u32[]{:S(2)}) collective-permute-start(bf16[128,256]{1,0:T(8,128)(2,1)S(1)} %get-tuple-element.430), channel_id=1, source_target_pairs={{16,84},{20,88},{24,92},{28,80},{48,116},{52,120},{56,124},{60,112... | collective-permute-start | bytes 196616 | tf_op jit(solution)/shard_map/ppermute | solution.py:226
  802.4 53.4 %collective-permute-start.88 = (bf16[128,256]{1,0:T(8,128)(2,1)S(1)}, bf16[128,256]{1,0:T(8,128)(2,1)S(1)}, u32[]{:S(2)}, u32[]{:S(2)}) collective-permute-start(bf16[128,256]{1,0:T(8,128)(2,1)S(1)} %get-tuple-element.422), channel_id=1, source_target_pairs={{16,52},{20,56},{24,60},{28,48},{48,84},{52,88},{56,92},{60,80},{8... | collective-permute-start | bytes 196616 | tf_op jit(solution)/shard_map/ppermute | solution.py:226
  909.4 69.2 %collective-permute-start.105 = (bf16[128,704]{1,0:T(8,128)(2,1)S(1)}, bf16[128,704]{1,0:T(8,128)(2,1)}, u32[]{:S(2)}, u32[]{:S(2)}) collective-permute-start(bf16[128,704]{1,0:T(8,128)(2,1)S(1)} %get-tuple-element.404), channel_id=1, source_target_pairs={{0,92},{4,80},{8,84},{12,88},{32,124},{36,112},{40,116},{44,120},{... | collective-permute-start | bytes 540680 | tf_op jit(solution)/shard_map/ppermute | solution.py:229
  1040.1 84.2 %collective-permute-start.95 = (bf16[128,704]{1,0:T(8,128)(2,1)}, bf16[128,704]{1,0:T(8,128)(2,1)}, u32[]{:S(2)}, u32[]{:S(2)}) collective-permute-start(bf16[128,704]{1,0:T(8,128)(2,1)} %get-tuple-element.414), channel_id=1, source_target_pairs={{0,4},{4,8},{8,12},{12,0},{32,36},{36,40},{40,44},{44,32},{64,68},... | collective-permute-start | bytes 540680 | tf_op jit(solution)/shard_map/ppermute | solution.py:229
  1042.9 91.6 %collective-permute-start.96 = (bf16[128,704]{1,0:T(8,128)(2,1)}, bf16[128,704]{1,0:T(8,128)(2,1)}, u32[]{:S(2)}, u32[]{:S(2)}) collective-permute-start(bf16[128,704]{1,0:T(8,128)(2,1)} %get-tuple-element.413), channel_id=1, source_target_pairs={{0,112},{4,116},{8,120},{12,124},{32,16},{36,20},{40,24},{44,28},{... | collective-permute-start | bytes 540680 | tf_op jit(solution)/shard_map/ppermute | solution.py:229
  1052.7 92.7 %collective-permute-start.97 = (bf16[128,704]{1,0:T(8,128)(2,1)}, bf16[128,704]{1,0:T(8,128)(2,1)}, u32[]{:S(2)}, u32[]{:S(2)}) collective-permute-start(bf16[128,704]{1,0:T(8,128)(2,1)} %get-tuple-element.412), channel_id=1, source_target_pairs={{0,124},{4,112},{8,116},{12,120},{32,28},{36,16},{40,20},{44,24},{... | collective-permute-start | bytes 540680 | tf_op jit(solution)/shard_map/ppermute | solution.py:229
  1063.6 92.7 %collective-permute-start.98 = (bf16[128,704]{1,0:T(8,128)(2,1)}, bf16[128,704]{1,0:T(8,128)(2,1)}, u32[]{:S(2)}, u32[]{:S(2)}) collective-permute-start(bf16[128,704]{1,0:T(8,128)(2,1)} %get-tuple-element.411), channel_id=1, source_target_pairs={{0,120},{4,124},{8,112},{12,116},{32,24},{36,28},{40,16},{44,20},{... | collective-permute-start | bytes 540680 | tf_op jit(solution)/shard_map/ppermute | solution.py:229
  1074.5 92.7 %collective-permute-start.99 = (bf16[128,704]{1,0:T(8,128)(2,1)}, bf16[128,704]{1,0:T(8,128)(2,1)}, u32[]{:S(2)}, u32[]{:S(2)}) collective-permute-start(bf16[128,704]{1,0:T(8,128)(2,1)} %get-tuple-element.410), channel_id=1, source_target_pairs={{0,116},{4,120},{8,124},{12,112},{32,20},{36,24},{40,28},{44,16},{... | collective-permute-start | bytes 540680 | tf_op jit(solution)/shard_map/ppermute | solution.py:229
  1124.4 94.6 %collective-permute-start.100 = (bf16[128,704]{1,0:T(8,128)(2,1)}, bf16[128,704]{1,0:T(8,128)(2,1)}, u32[]{:S(2)}, u32[]{:S(2)}) collective-permute-start(bf16[128,704]{1,0:T(8,128)(2,1)} %get-tuple-element.409), channel_id=1, source_target_pairs={{0,96},{4,100},{8,104},{12,108},{32,0},{36,4},{40,8},{44,12},{64,3... | collective-permute-start | bytes 540680 | tf_op jit(solution)/shard_map/ppermute | solution.py:229
  1134.6 86.4 %collective-permute-start.101 = (bf16[128,704]{1,0:T(8,128)(2,1)}, bf16[128,704]{1,0:T(8,128)(2,1)}, u32[]{:S(2)}, u32[]{:S(2)}) collective-permute-start(bf16[128,704]{1,0:T(8,128)(2,1)} %get-tuple-element.408), channel_id=1, source_target_pairs={{0,108},{4,96},{8,100},{12,104},{32,12},{36,0},{40,4},{44,8},{64,4... | collective-permute-start | bytes 540680 | tf_op jit(solution)/shard_map/ppermute | solution.py:229
  1145.4 77.4 %collective-permute-start.102 = (bf16[128,704]{1,0:T(8,128)(2,1)}, bf16[128,704]{1,0:T(8,128)(2,1)}, u32[]{:S(2)}, u32[]{:S(2)}) collective-permute-start(bf16[128,704]{1,0:T(8,128)(2,1)} %get-tuple-element.407), channel_id=1, source_target_pairs={{0,104},{4,108},{8,96},{12,100},{32,8},{36,12},{40,0},{44,4},{64,4... | collective-permute-start | bytes 540680 | tf_op jit(solution)/shard_map/ppermute | solution.py:229
  1156.3 68.5 %collective-permute-start.103 = (bf16[128,704]{1,0:T(8,128)(2,1)}, bf16[128,704]{1,0:T(8,128)(2,1)}, u32[]{:S(2)}, u32[]{:S(2)}) collective-permute-start(bf16[128,704]{1,0:T(8,128)(2,1)} %get-tuple-element.406), channel_id=1, source_target_pairs={{0,100},{4,104},{8,108},{12,96},{32,4},{36,8},{40,12},{44,0},{64,3... | collective-permute-start | bytes 540680 | tf_op jit(solution)/shard_map/ppermute | solution.py:229
  1167.2 59.6 %collective-permute-start.104 = (bf16[128,704]{1,0:T(8,128)(2,1)}, bf16[128,704]{1,0:T(8,128)(2,1)}, u32[]{:S(2)}, u32[]{:S(2)}) collective-permute-start(bf16[128,704]{1,0:T(8,128)(2,1)} %get-tuple-element.405), channel_id=1, source_target_pairs={{0,80},{4,84},{8,88},{12,92},{32,112},{36,116},{40,120},{44,124},{... | collective-permute-start | bytes 540680 | tf_op jit(solution)/shard_map/ppermute | solution.py:229
  (263 other events, 8576.3 us)
Sparse Core Ops, SparseCore 0:
  234.8 47.6 all-gather.7
Sparse Core Ops, SparseCore 1:
  858.7 71.3 all-gather.5

commit v2 on v1

--- a/solution.py
+++ b/solution.py
@@ -140,115 +140,57 @@
     )
     owner_rms = jnp.sum(jnp.where(owners == my_index, rms_all, 0.0)).reshape(1)
 
-    shifts = [(a, b) for a in range(shards_count) for b in range(tensor_count)]
-    step_a = jnp.array([a for a, b in shifts], jnp.int32)
-    step_b = jnp.array([b for a, b in shifts], jnp.int32)
-    dest = ((my_row + step_a) % shards_count) * tensor_count + (my_col + step_b) % tensor_count
-    dest_kind = kind_table[dest]
-    dest_index = index_table[dest]
-    square_rot = jnp.dot(
-        ((dest_kind == 1)[:, None] & (dest_index[:, None] == jnp.arange(n_square)[None, :])).astype(
-            jnp.bfloat16
-        ),
-        square_table.reshape(n_square, square_width),
-        preferred_element_type=jnp.float32,
-    ).astype(jnp.bfloat16)
-    rect_rot = jnp.dot(
-        ((dest_kind == 2)[:, None] & (dest_index[:, None] == jnp.arange(n_rect)[None, :])).astype(
-            jnp.bfloat16
-        ),
-        rect_table.reshape(n_rect, rect_width),
-        preferred_element_type=jnp.float32,
-    ).astype(jnp.bfloat16)
-
-    def shift_pairs(a, b, sign, wanted, by_dest):
-        pairs = []
-        for s in range(shards_count):
-            for t in range(tensor_count):
-                src = s * tensor_count + t
-                dst = ((s + sign * a) % shards_count) * tensor_count + (t + sign * b) % tensor_count
-                if kind_list[dst if by_dest else src] == wanted:
-                    pairs.append((src, dst))
-        return pairs
-
-    square_in = [square_rot[0]]
-    rect_in = [rect_rot[0]]
-    for k, (a, b) in enumerate(shifts[1:], start=1):
-        square_in.append(
-            lax.ppermute(square_rot[k], ("shards", "tensor"), shift_pairs(a, b, 1, 1, True))
+    def padded(block):
+        return jnp.pad(block, ((0, 0), (0, ff_block - block.shape[1])))
+
+    zero_slot = jnp.zeros((rows_block, ff_block), jnp.bfloat16)
+    slots_out = []
+    for device in range(group_count):
+        if kind_list[device] == 1:
+            slots_out.append(padded(square_table[index_list[device]]))
+        elif kind_list[device] == 2:
+            slots_out.append(rect_table[index_list[device]])
+        else:
+            slots_out.append(zero_slot)
+    outgoing = jnp.stack(slots_out)
+    incoming = lax.all_to_all(outgoing, ("shards", "tensor"), split_axis=0, concat_axis=0, tiled=True)
+
+    def run(arrived_blocks, width, norm_value):
+        whole = (
+            arrived_blocks[:, :, :width]
+            .reshape(shards_count, tensor_count, rows_block, width)
+            .transpose(0, 2, 1, 3)
+            .reshape(shards_count * rows_block, tensor_count * width)
         )
-        rect_in.append(lax.ppermute(rect_rot[k], ("shards", "tensor"), shift_pairs(a, b, 1, 2, True)))
-
-    def assemble(blocks, width):
-        rows = [
-            jnp.concatenate(blocks[a * tensor_count : (a + 1) * tensor_count], axis=1).reshape(
-                rows_block, tensor_count * width
-            )
-            for a in range(shards_count)
-        ]
-        return jnp.concatenate(rows, axis=0)
-
-    def run(blocks, width, norm_value):
-        whole = assemble([x.reshape(rows_block, width) for x in blocks], width)
         done = newton_schulz(whole, norm_value)
-        return [
-            done[a * rows_block : (a + 1) * rows_block, b * width : (b + 1) * width]
-            for a, b in shifts
-        ]
+        back = (
+            done.reshape(shards_count, rows_block, tensor_count, width)
+            .transpose(0, 2, 1, 3)
+            .reshape(group_count, rows_block, width)
+        )
+        return jnp.pad(back, ((0, 0), (0, 0), (0, ff_block - width)))
 
     my_kind = kind_table[my_index]
     my_mat = index_table[my_index]
 
-    def square_branch(operands):
-        square_blocks, rect_blocks = operands
-        out = run(square_blocks, cols_block, square_norm[my_mat])
-        return jnp.stack(out), jnp.zeros((group_count, rows_block, ff_block), jnp.bfloat16)
-
-    def rect_branch(operands):
-        square_blocks, rect_blocks = operands
-        out = run(rect_blocks, ff_block, rect_norm[my_mat])
-        return jnp.zeros((group_count, rows_block, cols_block), jnp.bfloat16), jnp.stack(out)
-
-    def idle_branch(operands):
-        return (
-            jnp.zeros((group_count, rows_block, cols_block), jnp.bfloat16),
-            jnp.zeros((group_count, rows_block, ff_block), jnp.bfloat16),
-        )
-
-    square_done, rect_done = lax.switch(
-        my_kind, [idle_branch, square_branch, rect_branch], (square_in, rect_in)
-    )
-
-    square_back = [square_done[0]]
-    rect_back = [rect_done[0]]
-    for k, (a, b) in enumerate(shifts[1:], start=1):
-        square_back.append(
-            lax.ppermute(square_done[k], ("shards", "tensor"), shift_pairs(a, b, -1, 1, False))
-        )
-        rect_back.append(
-            lax.ppermute(rect_done[k], ("shards", "tensor"), shift_pairs(a, b, -1, 2, False))
-        )
-    square_back = jnp.stack(square_back).reshape(group_count, square_width)
-    rect_back = jnp.stack(rect_back).reshape(group_count, rect_width)
-
-    def arrival_round(home):
-        home = jnp.array(home, jnp.int32)
-        a = (home // tensor_count - my_row) % shards_count
-        b = (home % tensor_count - my_col) % tensor_count
-        return a * tensor_count + b
-
-    square_pick = (
-        arrival_round(square_home)[:, None] == jnp.arange(group_count)[None, :]
-    ).astype(jnp.bfloat16)
-    rect_pick = (arrival_round(rect_home)[:, None] == jnp.arange(group_count)[None, :]).astype(
-        jnp.bfloat16
-    )
-    square_rows = jnp.dot(square_pick, square_back, preferred_element_type=jnp.float32).reshape(
+    def square_branch(arrived_blocks):
+        return run(arrived_blocks, cols_block, square_norm[my_mat])
+
+    def rect_branch(arrived_blocks):
+        return run(arrived_blocks, ff_block, rect_norm[my_mat])
+
+    def idle_branch(arrived_blocks):
+        return jnp.zeros((group_count, rows_block, ff_block), jnp.bfloat16)
+
+    returning = lax.switch(my_kind, [idle_branch, square_branch, rect_branch], incoming)
+    arrived = lax.all_to_all(returning, ("shards", "tensor"), split_axis=0, concat_axis=0, tiled=True)
+
+    square_rows = jnp.stack([arrived[device, :, :cols_block] for device in square_home]).reshape(
         layers_here, 4, rows_block, cols_block
-    ) * (0.2 * math.sqrt(D))
-    rect_rows = jnp.dot(rect_pick, rect_back, preferred_element_type=jnp.float32).reshape(
+    ).astype(jnp.float32) * (0.2 * math.sqrt(D))
+    rect_rows = jnp.stack([arrived[device] for device in rect_home]).reshape(
         layers_here, 3, rows_block, ff_block
-    ) * (0.2 * math.sqrt(FF))
+    ).astype(jnp.float32) * (0.2 * math.sqrt(FF))
     mlp_in_update = rect_rows[:, :2]
     mlp_out_update = jnp.swapaxes(rect_rows[:, 2], 1, 2)
 

time: 1320 us -> 360 us (0.27)
  the two profiles are of different devices: /device:TPU:2 before, /device:TPU:1 now
where the time goes in v2:
time: 360 us; the launch traced here: 354 us
  waiting for transfers between devices  168 us (47%)
  local copies, waits for them, and re-layouts  59.2 us (16%)
  starting transfers between devices  51.2 us (14%)
  matrix products  27.6 us (8%)
  other arithmetic  17.5 us (5%)
  between operations  17 us (5%)
  loops' own time  13.8 us (4%)
    all_gather x1, waiting for transfers between devices, on_device(): lax.all_gather(bias_pad, ('shards', 'tensor', 'section'), axis=0, tiled=F...  92.8 us
    all_gather x1, waiting for transfers between devices, on_device(): lax.all_gather(packed, ('shards', 'tensor'), axis=0, tiled=False)  74.9 us
    all_to_all x1, starting transfers between devices, on_device(): lax.all_to_all(returning, ('shards', 'tensor'), split_axis=0, concat_axis...  41.5 us
    unnamed x76, local copies, waits for them, and re-layouts  22 us
    dot_general x2, matrix products, newton_schulz(): jnp.dot(polynomial, current, preferred_element_type=jnp.float32)  17.8 us
    another operation x1, loops' own time, on_device(): lax.switch(my_kind, [idle_branch, square_branch, rect_branch], incoming)  13.8 us
    dot_general x2, matrix products, newton_schulz(): jnp.dot(current, current.T, preferred_element_type=jnp.float32)  9.75 us
    all_to_all x1, starting transfers between devices, on_device(): lax.all_to_all(outgoing, ('shards', 'tensor'), split_axis=0, concat_axis=...  9.6 us
  transfers between devices with their start and end apart: 4, of which 2 were waited for; matrix products, arithmetic and copies ran while one was open for 3% of the time, Pallas kernels for 0%

profile of v2, /device:TPU:1, one launch (start us, length us, event | category | flops | bytes accessed | tf_op | source)
XLA Modules:
  0.0 354.1 jit_solution(17982492252029622993)
XLA Ops:
  8.0 3.8 %fusion.14 = (bf16[4,2,128,704]{2,3,1,0:T(8,128)(2,1)S(1)}, bf16[4,2,128,704]{2,3,1,0:T(8,128)(2,1)}) fusion(bf16[4,2,128,704]{2,3,1,0:T(8,128)(2,1)} %param.25, bf16[4,2,128,704]{2,3,1,0:T(8,128)(2,1)} %param.28), kind=kLoop, calls=%fused_computation.25 | loop fusion | flops 6488064 | bytes 5767168 | tf_op jit(solution)/shard_map/convert_element_type | solution.py:39
  11.9 1.2 fusion.21
  13.3 1.3 copy-done.1
  14.6 0.9 slice_dynamic-update-slice_fusion.2
  15.6 1.8 multiply_reduce_fusion.1
  20.6 2.0 slice_dynamic-update-slice_fusion.1
  25.9 2.0 slice_dynamic-update-slice_fusion
  31.1 0.9 broadcast_dynamic-update-slice_fusion
  32.5 0.7 bitcast_dynamic-update-slice_fusion.3
  35.3 9.6 %all-to-all-start = ((bf16[32,128,704]{1,2,0:T(8,128)(2,1)}), bf16[32,128,704]{1,2,0:T(8,128)(2,1)}, u32[]{:S(2)}, u32[]{:S(2)}) async-start(bf16[32,128,704]{1,2,0:T(8,128)(2,1)} %bitcast_dynamic-update-slice_fusion), calls=%async_computation | async-start | bytes 11534336 | tf_op jit(solution)/shard_map/all_to_all | solution.py:156
  48.3 74.9 %all-gather.8.cloned.1.call-done = f32[32,1,8320]{2,1,0:T(1,128)} async-done(((f32[1,1,8320]{2,1,0:T(1,128)}), f32[32,1,8320]{2,1,0:T(1,128)}) %all-gather.8.cloned.1.call-update) | async-done | bytes 1064976 | tf_op jit(solution)/shard_map/all_gather | solution.py:125
  123.2 1.8 reduce_sum.53
  125.1 61.8 %conditional.1 = (bf16[32,128,704]{2,1,0:T(8,128)(2,1)}) conditional(s32[]{:T(128)} %bitcast.12, () %tuple.17, (bf16[32,128,704]{1,2,0:T(8,128)(2,1)}, f32[16]{0:T(128)S(1)}, s32[]{:T(128)}) %tuple.18, (bf16[32,128,704]{1,2,0:T(8,128)(2,1)}, f32[12]{0:T(128)S(1)}, s32[]{:T(128)}) %tuple.19), branch_computations={%region_3.4_spmd, %region_4.5_spmd, %region_5.6_spmd} | conditional | flops 27959492608 | bytes 185598208 | solution.py:185
  125.1 8.6 %copy.214 = bf16[32,128,704]{2,1,0:T(8,128)(2,1)} copy(bf16[32,128,704]{1,2,0:T(8,128)(2,1)} %get-tuple-element.145) | data formatting | bytes 11534336 | tf_op jit(solution)/shard_map
  136.9 2.1 divide_convert_fusion
  138.9 1.6 copy.190
  141.1 3.7 %fusion.36 = bf16[1024,1024]{1,0:T(8,128)(2,1)} fusion(bf16[1024,1024]{1,0:T(8,128)(2,1)S(1)} %bitcast.128), kind=kOutput, calls=%fused_computation.79 | convolution fusion | flops 2147483648 | bytes 4194304 | tf_op jit(solution)/shard_map/cond/branch_1_fun/dot_general | solution.py:21
  144.8 8.9 %add_convert_fusion.2 = bf16[1024,1024]{1,0:T(8,128)(2,1)} fusion(bf16[1024,1024]{1,0:T(8,128)(2,1)S(1)} %bitcast.129, bf16[1024,1024]{1,0:T(8,128)(2,1)} %fusion.36), kind=kOutput, calls=%fused_computation.2 | convolution fusion | flops 4304404480 | bytes 6291456 | tf_op jit(solution)/shard_map/cond/branch_1_fun/dot_general | solution.py:30
  153.7 6.1 %fusion.37 = bf16[1024,1024]{1,0:T(8,128)(2,1)} fusion(bf16[1024,1024]{1,0:T(8,128)(2,1)} %add_convert_fusion.2), kind=kOutput, calls=%fused_computation.80 | convolution fusion | flops 2147483648 | bytes 4194304 | tf_op jit(solution)/shard_map/cond/branch_1_fun/dot_general | solution.py:21
  159.7 8.9 %add_convert_fusion = bf16[1024,1024]{1,0:T(8,128)(2,1)} fusion(bf16[1024,1024]{1,0:T(8,128)(2,1)S(1)} %copy-done.21, bf16[1024,1024]{1,0:T(8,128)(2,1)} %fusion.37), kind=kOutput, calls=%fused_computation | convolution fusion | flops 4304404480 | bytes 6291456 | tf_op jit(solution)/shard_map/cond/branch_1_fun/dot_general | solution.py:30
  168.6 3.3 reshape.127
  172.4 3.3 pad.42
  186.9 8.4 %copy.215 = bf16[32,128,704]{1,2,0:T(8,128)(2,1)} copy(bf16[32,128,704]{2,1,0:T(8,128)(2,1)} %get-tuple-element.207) | data formatting | bytes 11534336 | tf_op jit(solution)/shard_map/cond | solution.py:185
  195.3 41.5 %all-to-all-start.1 = ((bf16[32,128,704]{1,2,0:T(8,128)(2,1)}), bf16[32,128,704]{1,2,0:T(8,128)(2,1)}, u32[]{:S(2)}, u32[]{:S(2)}) async-start(bf16[32,128,704]{1,2,0:T(8,128)(2,1)} %copy.215), calls=%async_computation.1 | async-start | bytes 11534336 | tf_op jit(solution)/shard_map/all_to_all | solution.py:186
  237.8 3.2 multiply_subtract_fusion
  242.6 92.8 %all-gather.6.cloned.1.call-done = f32[262144]{0:T(1024)} async-done(((f32[2048]{0:T(1024)}), f32[262144]{0:T(1024)}) %all-gather.6.cloned.1.call-update) | async-done | bytes 1048592 | tf_op jit(solution)/shard_map/all_gather | solution.py:131
  335.4 1.4 reshape.144
  337.6 1.7 fusion.33
  339.8 1.8 slice.219
  341.6 1.2 slice_bitcast_fusion
  342.8 1.3 fusion.34
  344.3 1.8 copy.220
  (108 shorter events, 20.6 us)
Async XLA Ops:
  8.0 3.8 %copy-start.8 = (bf16[4,704,128]{2,1,0:T(8,128)(2,1)S(1)}, bf16[4,704,128]{2,1,0:T(8,128)(2,1)}, u32[]{:S(2)}) copy-start(bf16[4,704,128]{2,1,0:T(8,128)(2,1)} %param.26) | copy-start | bytes 2162692
  8.0 3.8 %copy-start.9 = (bf16[4,704,128]{2,1,0:T(8,128)(2,1)S(1)}, bf16[4,704,128]{2,1,0:T(8,128)(2,1)}, u32[]{:S(2)}) copy-start(bf16[4,704,128]{2,1,0:T(8,128)(2,1)} %param.29) | copy-start | bytes 2162692
  11.9 3.7 %copy-start.3 = (bf16[4,4,128,256]{3,2,1,0:T(8,128)(2,1)S(1)}, bf16[4,4,128,256]{3,2,1,0:T(8,128)(2,1)}, u32[]{:S(2)}) copy-start(bf16[4,4,128,256]{3,2,1,0:T(8,128)(2,1)} %param.24) | copy-start | bytes 3145732
  11.9 3.7 %copy-start.4 = (bf16[4,4,128,256]{3,2,1,0:T(8,128)(2,1)S(1)}, bf16[4,4,128,256]{3,2,1,0:T(8,128)(2,1)}, u32[]{:S(2)}) copy-start(bf16[4,4,128,256]{3,2,1,0:T(8,128)(2,1)} %param.27) | copy-start | bytes 3145732
  13.3 1.3 copy-start.1
  35.3 10.4 %copy-start.13 = (f32[4,1,2048]{2,1,0:T(1,128)S(1)}, f32[4,1,2048]{2,1,0:T(1,128)}, u32[]{:S(2)}) copy-start(f32[4,1,2048]{2,1,0:T(1,128)} %param.36) | copy-start | bytes 98308
  35.3 11.2 %copy-start.20 = (s32[32]{0:T(128)S(1)}, s32[32]{0:T(128)}, u32[]{:S(2)}) copy-start(s32[32]{0:T(128)} %constant.45.clone) | copy-start | bytes 388
  35.3 11.7 %copy-start.19 = (s32[32]{0:T(128)S(1)}, s32[32]{0:T(128)}, u32[]{:S(2)}) copy-start(s32[32]{0:T(128)} %constant.102.clone) | copy-start | bytes 388
  35.3 89.8 %all-to-all-start = ((bf16[32,128,704]{1,2,0:T(8,128)(2,1)}), bf16[32,128,704]{1,2,0:T(8,128)(2,1)}, u32[]{:S(2)}, u32[]{:S(2)}) async-start(bf16[32,128,704]{1,2,0:T(8,128)(2,1)} %bitcast_dynamic-update-slice_fusion), calls=%async_computation | async-start | bytes 11534336 | tf_op jit(solution)/shard_map/all_to_all | solution.py:156
  44.9 78.3 %all-gather.8.cloned.1.call-start = ((), (), s32[]{:S(2)}) async-start(), calls=%async_computation.3 | async-start | bytes 1098240 | tf_op jit(solution)/shard_map/all_gather | solution.py:125
  153.7 6.1 %copy-start.21 = (bf16[1024,1024]{1,0:T(8,128)(2,1)S(1)}, bf16[1024,1024]{1,0:T(8,128)(2,1)}, u32[]{:S(2)}) copy-start(bf16[1024,1024]{1,0:T(8,128)(2,1)} %add_convert_fusion.2) | copy-start | bytes 6291460 | tf_op jit(solution)/shard_map/cond
  195.3 41.6 %copy-start.14 = (f32[1,32,16]{1,2,0:T(8,128)S(1)}, f32[1,32,16]{1,2,0:T(8,128)}, u32[]{:S(2)}) copy-start(f32[1,32,16]{1,2,0:T(8,128)} %param.40) | copy-start | bytes 6148
  195.3 42.4 %copy-start.5 = (f32[251,1024]{1,0:T(8,128)S(1)}, f32[251,1024]{1,0:T(8,128)}, u32[]{:S(2)}) copy-start(f32[251,1024]{1,0:T(8,128)} %param.31) | copy-start | bytes 3084292
  195.3 42.4 %copy-start.6 = (f32[251,1024]{1,0:T(8,128)S(1)}, f32[251,1024]{1,0:T(8,128)}, u32[]{:S(2)}) copy-start(f32[251,1024]{1,0:T(8,128)} %param.34) | copy-start | bytes 3084292
  195.3 42.5 %copy-start.7 = (f32[251,1024]{1,0:T(8,128)S(1)}, f32[251,1024]{1,0:T(8,128)}, u32[]{:S(2)}) copy-start(f32[251,1024]{1,0:T(8,128)} %param.33) | copy-start | bytes 3084292
  195.3 142.3 %all-to-all-start.1 = ((bf16[32,128,704]{1,2,0:T(8,128)(2,1)}), bf16[32,128,704]{1,2,0:T(8,128)(2,1)}, u32[]{:S(2)}, u32[]{:S(2)}) async-start(bf16[32,128,704]{1,2,0:T(8,128)(2,1)} %copy.215), calls=%async_computation.1 | async-start | bytes 11534336 | tf_op jit(solution)/shard_map/all_to_all | solution.py:186
  236.9 4.3 %copy-start.18 = (s32[4,7]{1,0:T(4,128)S(1)}, s32[4,7]{1,0:T(4,128)}, u32[]{:S(2)}) copy-start(s32[4,7]{1,0:T(4,128)} %param.30) | copy-start | bytes 340
  236.9 5.0 %copy-start.10 = (f32[4,2048]{1,0:T(4,128)S(1)}, f32[4,2048]{1,0:T(4,128)}, u32[]{:S(2)}) copy-start(f32[4,2048]{1,0:T(4,128)} %param.35) | copy-start | bytes 98308
  236.9 5.0 %copy-start.11 = (f32[4,2048]{1,0:T(4,128)S(1)}, f32[4,2048]{1,0:T(4,128)}, u32[]{:S(2)}) copy-start(f32[4,2048]{1,0:T(4,128)} %param.38) | copy-start | bytes 98308
  236.9 5.0 %copy-start.12 = (f32[4,2048]{1,0:T(4,128)S(1)}, f32[4,2048]{1,0:T(4,128)}, u32[]{:S(2)}) copy-start(f32[4,2048]{1,0:T(4,128)} %param.37) | copy-start | bytes 98308
  236.9 98.5 %all-gather.6.cloned.1.call-start = ((), (), s32[]{:S(2)}) async-start(), calls=%async_computation.2 | async-start | bytes 1056768 | tf_op jit(solution)/shard_map/all_gather | solution.py:131
  237.8 99.2 %copy-start.15 = (f32[32,16]{0,1:T(8,128)S(1)}, f32[32,16]{0,1:T(8,128)}, u32[]{:S(2)}) copy-start(f32[32,16]{0,1:T(8,128)} %param.39) | copy-start | bytes 6148
  237.8 99.2 %copy-start.16 = (f32[32,16]{0,1:T(8,128)S(1)}, f32[32,16]{0,1:T(8,128)}, u32[]{:S(2)}) copy-start(f32[32,16]{0,1:T(8,128)} %param.42) | copy-start | bytes 6148
  237.8 99.2 %copy-start.17 = (f32[32,16]{0,1:T(8,128)S(1)}, f32[32,16]{0,1:T(8,128)}, u32[]{:S(2)}) copy-start(f32[32,16]{0,1:T(8,128)} %param.41) | copy-start | bytes 6148
Sparse Core Ops, SparseCore 0:
  48.6 74.5 all-gather.7
Sparse Core Ops, SparseCore 1:
  240.7 94.6 all-gather.5

commit v3 on v2

--- a/solution.py
+++ b/solution.py
@@ -15,19 +15,23 @@
 coef_third = 2.0315
 
 
-def newton_schulz(blocks_bf16, norm_value):
-    current = (blocks_bf16.astype(jnp.float32) / (norm_value + 1e-07)).astype(jnp.bfloat16)
+def newton_schulz_transposed(rows_bf16):
+    as_f32 = rows_bf16.astype(jnp.float32)
+    norm_value = jnp.sqrt(jnp.sum(as_f32 * as_f32))
+    current = (as_f32 / (norm_value + 1e-07)).astype(jnp.bfloat16)
     for sweep_index in range(NS_STEPS):
-        gram_form = jnp.dot(current, current.T, preferred_element_type=jnp.float32).astype(
-            jnp.bfloat16
-        )
+        gram_form = lax.dot_general(
+            current, current, (((0,), (0,)), ((), ())), preferred_element_type=jnp.float32
+        ).astype(jnp.bfloat16)
         square_form = jnp.dot(gram_form, gram_form, preferred_element_type=jnp.float32)
         polynomial = (
             coef_second * gram_form.astype(jnp.float32) + coef_third * square_form
         ).astype(jnp.bfloat16)
         current = (
             coef_first * current.astype(jnp.float32)
-            + jnp.dot(polynomial, current, preferred_element_type=jnp.float32)
+            + lax.dot_general(
+                current, polynomial, (((1,), (1,)), ((), ())), preferred_element_type=jnp.float32
+            )
         ).astype(jnp.bfloat16)
     return current
 
@@ -112,38 +116,17 @@
     attn_fresh, attn_ahead = refresh(attn_grad, attn_momentum)
     inner_fresh, inner_ahead = refresh(mlp_in_grad, mlp_in_momentum)
     outer_fresh, outer_ahead = refresh(mlp_out_grad, mlp_out_momentum)
-    square_table = attn_ahead.reshape(n_square, rows_block, cols_block)
+    square_table = jnp.swapaxes(attn_ahead, 2, 3).reshape(n_square, cols_block, rows_block)
     rect_table = jnp.concatenate(
-        [inner_ahead, jnp.swapaxes(outer_ahead, 1, 2)[:, None]], axis=1
-    ).reshape(n_rect, rows_block, ff_block)
+        [jnp.swapaxes(inner_ahead, 2, 3), outer_ahead[:, None]], axis=1
+    ).reshape(n_rect, ff_block, rows_block)
 
     square_ss = jnp.sum(jnp.square(square_table.astype(jnp.float32)), axis=(1, 2))
     rect_ss = jnp.sum(jnp.square(rect_table.astype(jnp.float32)), axis=(1, 2))
-    norm_width = norm_partial.shape[0] * norm_partial.shape[2]
-    packed = jnp.concatenate([norm_partial.reshape(norm_width), square_ss, rect_ss])
-    packed = jnp.pad(packed, (0, (-packed.shape[0]) % 128))
-    gathered = jnp.sum(lax.all_gather(packed, ("shards", "tensor"), axis=0, tiled=False), axis=0)
-    norm_grad = gathered[:norm_width].reshape(norm_partial.shape[0], norm_partial.shape[2])
-    square_norm = jnp.sqrt(gathered[norm_width : norm_width + n_square])
-    rect_norm = jnp.sqrt(gathered[norm_width + n_square : norm_width + n_square + n_rect])
-    bias_flat = bias_partial.reshape(-1)
-    bias_pad = jnp.pad(bias_flat, (0, 2048 - bias_flat.shape[0]))
-    bias_all = lax.all_gather(bias_pad, ("shards", "tensor", "section"), axis=0, tiled=False)
-    bias_grad = jnp.sum(bias_all, axis=0)[: bias_flat.shape[0]].reshape(bias_table.shape)
-
-    rms_all = jnp.concatenate(
-        [
-            square_norm.reshape(layers_here, 4) / math.sqrt(D * D),
-            rect_norm.reshape(layers_here, 3) / math.sqrt(D * FF),
-        ],
-        axis=1,
-    )
-    owner_rms = jnp.sum(jnp.where(owners == my_index, rms_all, 0.0)).reshape(1)
-
     def padded(block):
-        return jnp.pad(block, ((0, 0), (0, ff_block - block.shape[1])))
-
-    zero_slot = jnp.zeros((rows_block, ff_block), jnp.bfloat16)
+        return jnp.pad(block, ((0, ff_block - block.shape[0]), (0, 0)))
+
+    zero_slot = jnp.zeros((ff_block, rows_block), jnp.bfloat16)
     slots_out = []
     for device in range(group_count):
         if kind_list[device] == 1:
@@ -155,44 +138,70 @@
     outgoing = jnp.stack(slots_out)
     incoming = lax.all_to_all(outgoing, ("shards", "tensor"), split_axis=0, concat_axis=0, tiled=True)
 
-    def run(arrived_blocks, width, norm_value):
+    norm_partial_late, square_ss, rect_ss, bias_partial_late, incoming = lax.optimization_barrier(
+        (norm_partial, square_ss, rect_ss, bias_partial, incoming)
+    )
+    norm_width = norm_partial.shape[0] * norm_partial.shape[2]
+    packed = jnp.concatenate([norm_partial_late.reshape(norm_width), square_ss, rect_ss])
+    packed = jnp.pad(packed, (0, (-packed.shape[0]) % 128))
+    gathered_all = lax.all_gather(packed, ("shards", "tensor"), axis=0, tiled=False)
+    bias_flat = bias_partial_late.reshape(-1)
+    bias_pad = jnp.pad(bias_flat, (0, 2048 - bias_flat.shape[0]))
+    bias_all = lax.all_gather(bias_pad, ("shards", "tensor", "section"), axis=0, tiled=False)
+
+    def run(arrived_blocks, width):
         whole = (
-            arrived_blocks[:, :, :width]
-            .reshape(shards_count, tensor_count, rows_block, width)
-            .transpose(0, 2, 1, 3)
-            .reshape(shards_count * rows_block, tensor_count * width)
+            arrived_blocks[:, :width]
+            .reshape(shards_count, tensor_count, width, rows_block)
+            .transpose(1, 2, 0, 3)
+            .reshape(tensor_count * width, shards_count * rows_block)
         )
-        done = newton_schulz(whole, norm_value)
+        done = newton_schulz_transposed(whole)
         back = (
-            done.reshape(shards_count, rows_block, tensor_count, width)
-            .transpose(0, 2, 1, 3)
-            .reshape(group_count, rows_block, width)
+            done.reshape(tensor_count, width, shards_count, rows_block)
+            .transpose(2, 0, 1, 3)
+            .reshape(group_count, width, rows_block)
         )
-        return jnp.pad(back, ((0, 0), (0, 0), (0, ff_block - width)))
+        return jnp.pad(back, ((0, 0), (0, ff_block - width), (0, 0)))
 
     my_kind = kind_table[my_index]
-    my_mat = index_table[my_index]
 
     def square_branch(arrived_blocks):
-        return run(arrived_blocks, cols_block, square_norm[my_mat])
+        return run(arrived_blocks, cols_block)
 
     def rect_branch(arrived_blocks):
-        return run(arrived_blocks, ff_block, rect_norm[my_mat])
+        return run(arrived_blocks, ff_block)
 
     def idle_branch(arrived_blocks):
-        return jnp.zeros((group_count, rows_block, ff_block), jnp.bfloat16)
+        return jnp.zeros((group_count, ff_block, rows_block), jnp.bfloat16)
 
     returning = lax.switch(my_kind, [idle_branch, square_branch, rect_branch], incoming)
+    returning, gathered_all, bias_all = lax.optimization_barrier((returning, gathered_all, bias_all))
     arrived = lax.all_to_all(returning, ("shards", "tensor"), split_axis=0, concat_axis=0, tiled=True)
 
-    square_rows = jnp.stack([arrived[device, :, :cols_block] for device in square_home]).reshape(
-        layers_here, 4, rows_block, cols_block
-    ).astype(jnp.float32) * (0.2 * math.sqrt(D))
+    gathered = jnp.sum(gathered_all, axis=0)
+    norm_grad = gathered[:norm_width].reshape(norm_partial.shape[0], norm_partial.shape[2])
+    square_norm = jnp.sqrt(gathered[norm_width : norm_width + n_square])
+    rect_norm = jnp.sqrt(gathered[norm_width + n_square : norm_width + n_square + n_rect])
+    bias_grad = jnp.sum(bias_all, axis=0)[: bias_flat.shape[0]].reshape(bias_table.shape)
+    rms_all = jnp.concatenate(
+        [
+            square_norm.reshape(layers_here, 4) / math.sqrt(D * D),
+            rect_norm.reshape(layers_here, 3) / math.sqrt(D * FF),
+        ],
+        axis=1,
+    )
+    owner_rms = jnp.sum(jnp.where(owners == my_index, rms_all, 0.0)).reshape(1)
+
+
+    square_rows = jnp.swapaxes(
+        jnp.stack([arrived[device, :cols_block] for device in square_home]), 1, 2
+    ).reshape(layers_here, 4, rows_block, cols_block).astype(jnp.float32) * (0.2 * math.sqrt(D))
     rect_rows = jnp.stack([arrived[device] for device in rect_home]).reshape(
-        layers_here, 3, rows_block, ff_block
+        layers_here, 3, ff_block, rows_block
     ).astype(jnp.float32) * (0.2 * math.sqrt(FF))
-    mlp_in_update = rect_rows[:, :2]
-    mlp_out_update = jnp.swapaxes(rect_rows[:, 2], 1, 2)
+    mlp_in_update = jnp.swapaxes(rect_rows[:, :2], 2, 3)
+    mlp_out_update = rect_rows[:, 2]
 
     embed_results = adamw_update(
         embed_weight, embed_grad.astype(jnp.float32), embed_moment, embed_second, 0.1

time: 360 us -> 323 us (0.90)
  the two profiles are of different devices: /device:TPU:1 before, /device:TPU:2 now
where the time goes in v3:
time: 323 us; the launch traced here: 318 us
  waiting for transfers between devices  159 us (49%)
  matrix products  49.2 us (15%)
  local copies, waits for them, and re-layouts  47.9 us (15%)
  other arithmetic  24.9 us (8%)
  between operations  15.3 us (5%)
  starting transfers between devices  15.2 us (5%)
  loops' own time  6.46 us (2%)
    all_to_all x1, waiting for transfers between devices, on_device(): lax.all_to_all(outgoing, ('shards', 'tensor'), split_axis=0, concat_axis=...  70.6 us
    all_to_all x1, waiting for transfers between devices, on_device(): lax.all_to_all(returning, ('shards', 'tensor'), split_axis=0, concat_axis...  64.8 us
    dot_general x2, matrix products, newton_schulz_transposed(): lax.dot_general(current, polynomial, (((1,), (1,)), ((), ())), preferred_...  32.4 us
    all_gather x1, waiting for transfers between devices, on_device(): lax.all_gather(bias_pad, ('shards', 'tensor', 'section'), axis=0, tiled=F...  23.8 us
    unnamed x70, local copies, waits for them, and re-layouts  23.3 us
    dot_general x2, matrix products, newton_schulz_transposed(): lax.dot_general(current, current, (((0,), (0,)), ((), ())), preferred_ele...  16.8 us
    all_to_all x1, starting transfers between devices, on_device(): lax.all_to_all(outgoing, ('shards', 'tensor'), split_axis=0, concat_axis=...  8.65 us
    cond x3, local copies, waits for them, and re-layouts  6.58 us
  transfers between devices with their start and end apart: 4, of which 3 were waited for; matrix products, arithmetic and copies ran while one was open for 26% of the time, Pallas kernels for 0%

profile of v3, /device:TPU:2, one launch (start us, length us, event | category | flops | bytes accessed | tf_op | source)
XLA Modules:
  0.0 318.1 jit_solution(911309541188210363)
XLA Ops:
  7.2 3.8 %fusion.45 = (bf16[4,2,704,128]{3,2,1,0:T(8,128)(2,1)S(1)}, bf16[4,2,128,704]{2,3,1,0:T(8,128)(2,1)}) fusion(bf16[4,2,128,704]{2,3,1,0:T(8,128)(2,1)} %param.24, bf16[4,2,128,704]{2,3,1,0:T(8,128)(2,1)} %param.27), kind=kLoop, calls=%fused_computation.62 | loop fusion | flops 6488064 | bytes 5767168 | tf_op jit(solution)/shard_map/transpose | solution.py:121
  11.0 1.2 fusion.48
  12.5 1.3 copy-done
  13.8 0.9 slice_dynamic-update-slice_fusion.2
  14.7 1.8 multiply_reduce_fusion.1
  19.8 2.0 slice_dynamic-update-slice_fusion.1
  25.1 2.1 slice_dynamic-update-slice_fusion
  30.4 0.9 broadcast_dynamic-update-slice_fusion
  34.6 8.6 %all-to-all-start = ((bf16[32,704,128]{2,1,0:T(8,128)(2,1)}), bf16[32,704,128]{2,1,0:T(8,128)(2,1)}, u32[]{:S(2)}, u32[]{:S(2)}) async-start(bf16[32,704,128]{2,1,0:T(8,128)(2,1)} %bitcast_dynamic-update-slice_fusion), calls=%async_computation | async-start | bytes 11534336 | tf_op jit(solution)/shard_map/all_to_all | solution.py:139
  44.0 70.6 %all-to-all-done = bf16[32,704,128]{2,1,0:T(8,128)(2,1)} async-done(((bf16[32,704,128]{2,1,0:T(8,128)(2,1)}), bf16[32,704,128]{2,1,0:T(8,128)(2,1)}, u32[]{:S(2)}, u32[]{:S(2)}) %all-to-all-start) | async-done | bytes 5767200 | tf_op jit(solution)/shard_map/all_to_all | solution.py:139
  117.5 80.7 %conditional.1 = (bf16[32,704,128]{2,1,0:T(8,128)(2,1)}) conditional(s32[]{:T(128)} %bitcast.8, () %tuple.19, bf16[32,704,128]{2,1,0:T(8,128)(2,1)} %all-to-all-done, bf16[32,704,128]{2,1,0:T(8,128)(2,1)} %all-to-all-done), branch_computations={%region_2.3_spmd, %region_3.5_spmd, %region_5.7_spmd} | conditional | flops 27968143360 | bytes 129499200 | solution.py:178
  123.0 6.2 %fusion.21 = f32[]{:T(128)} fusion(bf16[32,704,128]{2,1,0:T(8,128)(2,1)} %param.2), kind=kLoop, calls=%fused_computation.24 | loop fusion | flops 8650751 | bytes 5767172 | tf_op jit(solution)/shard_map/cond/branch_2_fun/reduce_sum | solution.py:20
  129.9 4.2 %fusion.22 = bf16[32,704,128]{2,1,0:T(8,128)(2,1)S(1)} fusion(bf16[32,704,128]{2,1,0:T(8,128)(2,1)} %param.2, f32[]{:T(128)S(6)} %add.73), kind=kLoop, calls=%fused_computation.25 | loop fusion | flops 8650752 | bytes 11534340 | tf_op jit(solution)/shard_map/convert.3
  134.2 3.7 %copy.121 = bf16[8,4,704,128]{3,0,2,1:T(8,128)(2,1)S(1)} copy(bf16[8,4,704,128]{3,2,1,0:T(8,128)(2,1)S(1)} %bitcast.127) | data formatting | bytes 11534336 | tf_op jit(solution)/shard_map/cond/branch_2_fun/div | solution.py:21
  137.9 2.4 copy-done.1
  140.3 6.8 %fusion.23 = bf16[1024,1024]{1,0:T(8,128)(2,1)S(1)} fusion(bf16[352,8,8,128]{3,2,1,0:T(8,128)(2,1)S(1)} %bitcast.138), kind=kOutput, calls=%fused_computation.29 | convolution fusion | flops 5905580032 | bytes 7864320 | tf_op jit(solution)/shard_map/cond/branch_2_fun/dot_general | solution.py:23
  147.2 17.7 %add_convert_fusion.5 = bf16[2816,1024]{1,0:T(8,128)(2,1)} fusion(bf16[352,8,8,128]{3,2,1,0:T(8,128)(2,1)} %bitcast.139, bf16[1024,1024]{1,0:T(8,128)(2,1)S(1)} %fusion.23), kind=kOutput, calls=%fused_computation.27 | convolution fusion | flops 8069840896 | bytes 13631488 | tf_op jit(solution)/shard_map/cond/branch_2_fun/dot_general | solution.py:32
  164.9 9.9 %fusion.66 = bf16[1024,1024]{1,0:T(8,128)(2,1)S(1)} fusion(bf16[2816,1024]{1,0:T(8,128)(2,1)} %add_convert_fusion.5), kind=kOutput, calls=%fused_computation.108 | convolution fusion | flops 5905580032 | bytes 7864320 | tf_op jit(solution)/shard_map/cond/branch_2_fun/dot_general | solution.py:23
  174.8 14.7 %fusion.28 = bf16[352,8,8,128]{3,1,2,0:T(8,128)(2,1)} fusion(bf16[2816,1024]{1,0:T(8,128)(2,1)} %add_convert_fusion.5, bf16[1024,1024]{1,0:T(8,128)(2,1)S(1)} %fusion.66), kind=kOutput, calls=%fused_computation.36 | convolution fusion | flops 8069840896 | bytes 13631488 | tf_op jit(solution)/shard_map/cond/branch_2_fun/dot_general | solution.py:32
  189.6 4.1 %copy.165 = bf16[352,8,8,128]{3,2,1,0:T(8,128)(2,1)S(1)} copy(bf16[352,8,8,128]{3,1,2,0:T(8,128)(2,1)} %fusion.28) | data formatting | bytes 11534336 | tf_op jit(solution)/shard_map/cond
  194.1 3.9 %copy.122 = bf16[8,4,704,128]{3,2,1,0:T(8,128)(2,1)} copy(bf16[8,4,704,128]{3,0,2,1:T(8,128)(2,1)S(1)} %bitcast_bitcast_fusion.1) | data formatting | bytes 11534336 | tf_op jit(solution)/shard_map/cond/branch_2_fun/transpose | solution.py:162
  198.2 1.3 copy.183
  199.5 23.8 %all-gather.6.cloned.1.call-done = f32[262144]{0:T(1024)} async-done(((f32[2048]{0:T(1024)}), f32[262144]{0:T(1024)}) %all-gather.6.cloned.1.call-update) | async-done | bytes 1048592 | tf_op jit(solution)/shard_map/all_gather | solution.py:150
  223.3 1.4 reshape.142
  224.7 6.5 %all-to-all-start.1 = ((bf16[32,704,128]{2,1,0:T(8,128)(2,1)}), bf16[32,704,128]{2,1,0:T(8,128)(2,1)}, u32[]{:S(2)}, u32[]{:S(2)}) async-start(bf16[32,704,128]{2,1,0:T(8,128)(2,1)} %get-tuple-element.141), calls=%async_computation.1 | async-start | bytes 11534336 | tf_op jit(solution)/shard_map/all_to_all | solution.py:180
  231.3 3.9 %multiply_subtract_fusion = (f32[251,1024]{1,0:T(8,128)}, f32[251,1024]{1,0:T(8,128)}, f32[251,1024]{1,0:T(8,128)}) fusion(f32[251,1024]{1,0:T(8,128)S(1)} %copy-done.4, bf16[251,1024]{1,0:T(8,128)(2,1)} %param.31, f32[251,1024]{1,0:T(8,128)} %param.33, f32[251,1024]{1,0:T(8,128)} %param.32), kind=kLoop, calls=%fused_computation.68 | loop fusion | flops 3598336 | bytes 6682624 | tf_op jit(solution)/shard_map/sub | solution.py:52
  237.8 64.8 %all-to-all-done.1 = bf16[32,704,128]{2,1,0:T(8,128)(2,1)} async-done(((bf16[32,704,128]{2,1,0:T(8,128)(2,1)}), bf16[32,704,128]{2,1,0:T(8,128)(2,1)}, u32[]{:S(2)}, u32[]{:S(2)}) %all-to-all-start.1) | async-done | bytes 5767200 | tf_op jit(solution)/shard_map/all_to_all | solution.py:180
  302.6 1.7 fusion.62
  304.8 1.8 slice_bitcast_fusion
  306.5 1.2 slice_bitcast_fusion.1
  307.7 1.3 fusion.63
  309.3 1.8 copy.144
  (98 shorter events, 19.8 us)
Async XLA Ops:
  7.2 3.8 %copy-start.5 = (bf16[4,704,128]{2,1,0:T(8,128)(2,1)S(1)}, bf16[4,704,128]{2,1,0:T(8,128)(2,1)}, u32[]{:S(2)}) copy-start(bf16[4,704,128]{2,1,0:T(8,128)(2,1)} %param.25) | copy-start | bytes 2162692
  7.2 3.8 %copy-start.6 = (bf16[4,704,128]{2,1,0:T(8,128)(2,1)S(1)}, bf16[4,704,128]{2,1,0:T(8,128)(2,1)}, u32[]{:S(2)}) copy-start(bf16[4,704,128]{2,1,0:T(8,128)(2,1)} %param.28) | copy-start | bytes 2162692
  11.0 3.7 %copy-start.2 = (bf16[4,4,128,256]{3,2,1,0:T(8,128)(2,1)S(1)}, bf16[4,4,128,256]{3,2,1,0:T(8,128)(2,1)}, u32[]{:S(2)}) copy-start(bf16[4,4,128,256]{3,2,1,0:T(8,128)(2,1)} %param.23) | copy-start | bytes 3145732
  11.0 3.7 %copy-start.3 = (bf16[4,4,128,256]{3,2,1,0:T(8,128)(2,1)S(1)}, bf16[4,4,128,256]{3,2,1,0:T(8,128)(2,1)}, u32[]{:S(2)}) copy-start(bf16[4,4,128,256]{3,2,1,0:T(8,128)(2,1)} %param.26) | copy-start | bytes 3145732
  12.5 1.3 copy-start
  34.6 80.1 %copy-start.10 = (f32[4,1,2048]{2,1,0:T(1,128)S(1)}, f32[4,1,2048]{2,1,0:T(1,128)}, u32[]{:S(2)}) copy-start(f32[4,1,2048]{2,1,0:T(1,128)} %param.35) | copy-start | bytes 98308
  34.6 80.9 %copy-start.11 = (f32[1,32,16]{1,2,0:T(8,128)S(1)}, f32[1,32,16]{1,2,0:T(8,128)}, u32[]{:S(2)}) copy-start(f32[1,32,16]{1,2,0:T(8,128)} %param.39) | copy-start | bytes 6148
  34.6 81.7 %copy-start.16 = (s32[32]{0:T(128)S(1)}, s32[32]{0:T(128)}, u32[]{:S(2)}) copy-start(s32[32]{0:T(128)} %constant.40.clone) | copy-start | bytes 388
  34.6 80.1 %all-to-all-start = ((bf16[32,704,128]{2,1,0:T(8,128)(2,1)}), bf16[32,704,128]{2,1,0:T(8,128)(2,1)}, u32[]{:S(2)}, u32[]{:S(2)}) async-start(bf16[32,704,128]{2,1,0:T(8,128)(2,1)} %bitcast_dynamic-update-slice_fusion), calls=%async_computation | async-start | bytes 11534336 | tf_op jit(solution)/shard_map/all_to_all | solution.py:139
  43.2 155.0 %all-gather.8.cloned.1.call-start = ((), (), s32[]{:S(2)}) async-start(), calls=%async_computation.3 | async-start | bytes 1098240 | tf_op jit(solution)/shard_map/all_gather | solution.py:147
  115.4 107.9 %all-gather.6.cloned.1.call-start = ((), (), s32[]{:S(2)}) async-start(), calls=%async_computation.2 | async-start | bytes 1056768 | tf_op jit(solution)/shard_map/all_gather | solution.py:150
  137.9 2.5 copy-start.1
  224.7 6.5 %copy-start.4 = (f32[251,1024]{1,0:T(8,128)S(1)}, f32[251,1024]{1,0:T(8,128)}, u32[]{:S(2)}) copy-start(f32[251,1024]{1,0:T(8,128)} %param.30) | copy-start | bytes 3084292
  224.7 77.9 %all-to-all-start.1 = ((bf16[32,704,128]{2,1,0:T(8,128)(2,1)}), bf16[32,704,128]{2,1,0:T(8,128)(2,1)}, u32[]{:S(2)}, u32[]{:S(2)}) async-start(bf16[32,704,128]{2,1,0:T(8,128)(2,1)} %get-tuple-element.141), calls=%async_computation.1 | async-start | bytes 11534336 | tf_op jit(solution)/shard_map/all_to_all | solution.py:180
  231.2 4.6 %copy-start.15 = (s32[4,7]{1,0:T(4,128)S(1)}, s32[4,7]{1,0:T(4,128)}, u32[]{:S(2)}) copy-start(s32[4,7]{1,0:T(4,128)} %param.29) | copy-start | bytes 340
  231.2 5.3 %copy-start.12 = (f32[32,16]{0,1:T(8,128)S(1)}, f32[32,16]{0,1:T(8,128)}, u32[]{:S(2)}) copy-start(f32[32,16]{0,1:T(8,128)} %param.38) | copy-start | bytes 6148
  231.2 5.3 %copy-start.13 = (f32[32,16]{0,1:T(8,128)S(1)}, f32[32,16]{0,1:T(8,128)}, u32[]{:S(2)}) copy-start(f32[32,16]{0,1:T(8,128)} %param.41) | copy-start | bytes 6148
  231.2 5.2 %copy-start.14 = (f32[32,16]{0,1:T(8,128)S(1)}, f32[32,16]{0,1:T(8,128)}, u32[]{:S(2)}) copy-start(f32[32,16]{0,1:T(8,128)} %param.40) | copy-start | bytes 6148
  231.2 5.9 %copy-start.7 = (f32[4,2048]{1,0:T(4,128)S(1)}, f32[4,2048]{1,0:T(4,128)}, u32[]{:S(2)}) copy-start(f32[4,2048]{1,0:T(4,128)} %param.34) | copy-start | bytes 98308
  231.2 5.9 %copy-start.8 = (f32[4,2048]{1,0:T(4,128)S(1)}, f32[4,2048]{1,0:T(4,128)}, u32[]{:S(2)}) copy-start(f32[4,2048]{1,0:T(4,128)} %param.37) | copy-start | bytes 98308
  231.3 5.8 %copy-start.9 = (f32[4,2048]{1,0:T(4,128)S(1)}, f32[4,2048]{1,0:T(4,128)}, u32[]{:S(2)}) copy-start(f32[4,2048]{1,0:T(4,128)} %param.36) | copy-start | bytes 98308
Sparse Core Ops, SparseCore 0:
  115.5 42.4 all-gather.7
  161.3 61.9 all-gather.5

commit v4 on v3

--- a/solution.py
+++ b/solution.py
@@ -53,16 +53,10 @@
     return (weight_new, moment_new, second_new)
 
 
-def block_plan(shards_count, tensor_count):
-    kind = [0] * (shards_count * tensor_count)
-    index = [0] * (shards_count * tensor_count)
-    chips = [(x, z) for x in range(shards_count // 2) for z in range(tensor_count)]
-    for number, (x, z) in enumerate(chips):
-        kind[(2 * x + 1) * tensor_count + z] = 1
-        index[(2 * x + 1) * tensor_count + z] = number
-    for number, (x, z) in enumerate(chips[:12]):
-        kind[(2 * x) * tensor_count + z] = 2
-        index[(2 * x) * tensor_count + z] = number
+def block_plan(shards_count, tensor_count, n_square, n_rect):
+    group = shards_count * tensor_count
+    kind = [2] * n_rect + [1] * n_square + [0] * (group - n_rect - n_square)
+    index = list(range(n_rect)) + list(range(n_square)) + [0] * (group - n_rect - n_square)
     return kind, index
 
 
@@ -101,7 +95,7 @@
     rect_width = rows_block * ff_block
     n_square = layers_here * 4
     n_rect = layers_here * 3
-    kind_list, index_list = block_plan(shards_count, tensor_count)
+    kind_list, index_list = block_plan(shards_count, tensor_count, n_square, n_rect)
     assert sum(k == 1 for k in kind_list) == n_square and sum(k == 2 for k in kind_list) == n_rect
     kind_table = jnp.array(kind_list, jnp.int32)
     index_table = jnp.array(index_list, jnp.int32)
@@ -126,28 +120,27 @@
     def padded(block):
         return jnp.pad(block, ((0, ff_block - block.shape[0]), (0, 0)))
 
-    zero_slot = jnp.zeros((ff_block, rows_block), jnp.bfloat16)
-    slots_out = []
-    for device in range(group_count):
-        if kind_list[device] == 1:
-            slots_out.append(padded(square_table[index_list[device]]))
-        elif kind_list[device] == 2:
-            slots_out.append(rect_table[index_list[device]])
-        else:
-            slots_out.append(zero_slot)
-    outgoing = jnp.stack(slots_out)
+    idle_count = group_count - n_rect - n_square
+    outgoing = jnp.concatenate(
+        [
+            rect_table,
+            jnp.pad(square_table, ((0, 0), (0, ff_block - cols_block), (0, 0))),
+            jnp.zeros((idle_count, ff_block, rows_block), jnp.bfloat16),
+        ]
+    )
     incoming = lax.all_to_all(outgoing, ("shards", "tensor"), split_axis=0, concat_axis=0, tiled=True)
 
     norm_partial_late, square_ss, rect_ss, bias_partial_late, incoming = lax.optimization_barrier(
         (norm_partial, square_ss, rect_ss, bias_partial, incoming)
     )
     norm_width = norm_partial.shape[0] * norm_partial.shape[2]
-    packed = jnp.concatenate([norm_partial_late.reshape(norm_width), square_ss, rect_ss])
+    bias_flat = bias_partial_late.reshape(-1)
+    bias_width = bias_flat.shape[0]
+    packed = jnp.concatenate([norm_partial_late.reshape(norm_width), bias_flat, square_ss, rect_ss])
     packed = jnp.pad(packed, (0, (-packed.shape[0]) % 128))
-    gathered_all = lax.all_gather(packed, ("shards", "tensor"), axis=0, tiled=False)
-    bias_flat = bias_partial_late.reshape(-1)
-    bias_pad = jnp.pad(bias_flat, (0, 2048 - bias_flat.shape[0]))
-    bias_all = lax.all_gather(bias_pad, ("shards", "tensor", "section"), axis=0, tiled=False)
+    gathered = jnp.sum(lax.all_gather(packed, ("shards", "tensor"), axis=0, tiled=False), axis=0)
+    bias_section = jnp.pad(gathered[norm_width : norm_width + bias_width], (0, 65536 - bias_width))
+    bias_all = lax.all_gather(bias_section, "section", axis=0, tiled=False)
 
     def run(arrived_blocks, width):
         whole = (
@@ -176,14 +169,14 @@
         return jnp.zeros((group_count, ff_block, rows_block), jnp.bfloat16)
 
     returning = lax.switch(my_kind, [idle_branch, square_branch, rect_branch], incoming)
-    returning, gathered_all, bias_all = lax.optimization_barrier((returning, gathered_all, bias_all))
+    returning, gathered, bias_all = lax.optimization_barrier((returning, gathered, bias_all))
     arrived = lax.all_to_all(returning, ("shards", "tensor"), split_axis=0, concat_axis=0, tiled=True)
 
-    gathered = jnp.sum(gathered_all, axis=0)
     norm_grad = gathered[:norm_width].reshape(norm_partial.shape[0], norm_partial.shape[2])
-    square_norm = jnp.sqrt(gathered[norm_width : norm_width + n_square])
-    rect_norm = jnp.sqrt(gathered[norm_width + n_square : norm_width + n_square + n_rect])
-    bias_grad = jnp.sum(bias_all, axis=0)[: bias_flat.shape[0]].reshape(bias_table.shape)
+    ss_start = norm_width + bias_width
+    square_norm = jnp.sqrt(gathered[ss_start : ss_start + n_square])
+    rect_norm = jnp.sqrt(gathered[ss_start + n_square : ss_start + n_square + n_rect])
+    bias_grad = jnp.sum(bias_all, axis=0)[:bias_width].reshape(bias_table.shape)
     rms_all = jnp.concatenate(
         [
             square_norm.reshape(layers_here, 4) / math.sqrt(D * D),

time: 323 us -> 329 us (1.019)
  local copies, waits for them, and re-layouts: 47.9 us -> 24.6 us
  waiting for transfers between devices: 159 us -> 178 us
  other arithmetic: 24.9 us -> 36 us
    all_gather x1, waiting for transfers between devices: 0.02 us -> 42.5 us  [on_device(): lax.all_gather(packed, ('shards', 'tensor'), axis=0, tiled=False)]
    all_gather x1, waiting for transfers between devices: 23.8 us -> 0.02 us  [on_device(): bias_all = lax.all_gather(bias_section, 'section', axis=0, tiled=False)]
    unnamed x70 -> x28, local copies, waits for them, and re-layouts: 23.3 us -> 2.54 us
    concatenate x0 -> x1, other arithmetic: none -> 3.64 us  [on_device(): jnp.concatenate([rect_table, jnp.pad(square_table, ((0, 0), (0, ff_block...]
  transfers between devices with their start and end apart: 4 -> 4, of which waited for: 3 -> 3; matrix products, arithmetic and copies ran while one was open for 26% -> 25% of each run, Pallas kernels for 0% -> 0%
where the time goes in v4:
time: 329 us; the launch traced here: 324 us
  waiting for transfers between devices  178 us (54%)
  matrix products  49.1 us (15%)
  other arithmetic  36 us (11%)
  local copies, waits for them, and re-layouts  24.6 us (7%)
  between operations  15.2 us (5%)
  starting transfers between devices  14.3 us (4%)
  loops' own time  6.46 us (2%)
    all_to_all x1, waiting for transfers between devices, on_device(): lax.all_to_all(outgoing, ('shards', 'tensor'), split_axis=0, concat_axis=...  70.6 us
    all_to_all x1, waiting for transfers between devices, on_device(): lax.all_to_all(returning, ('shards', 'tensor'), split_axis=0, concat_axis...  64.7 us
    all_gather x1, waiting for transfers between devices, on_device(): lax.all_gather(packed, ('shards', 'tensor'), axis=0, tiled=False)  42.5 us
    dot_general x2, matrix products, newton_schulz_transposed(): lax.dot_general(current, polynomial, (((1,), (1,)), ((), ())), preferred_...  32.4 us
    dot_general x2, matrix products, newton_schulz_transposed(): lax.dot_general(current, current, (((0,), (0,)), ((), ())), preferred_ele...  16.7 us
    all_to_all x1, starting transfers between devices, on_device(): lax.all_to_all(outgoing, ('shards', 'tensor'), split_axis=0, concat_axis=...  8.64 us
  transfers between devices with their start and end apart: 4, of which 3 were waited for; matrix products, arithmetic and copies ran while one was open for 25% of the time, Pallas kernels for 0%

profile of v4, /device:TPU:2, one launch (start us, length us, event | category | flops | bytes accessed | tf_op | source)
XLA Modules:
  0.0 323.5 jit_solution(12659428344724820004)
XLA Ops:
  7.2 3.4 %multiply_reduce_fusion.1 = (f32[4,4]{1,0:T(4,128)S(1)}, bf16[4,4,128,256]{3,2,1,0:T(8,128)(2,1)S(1)}, bf16[4,4,128,256]{3,2,1,0:T(8,128)(2,1)}) fusion(bf16[4,4,128,256]{3,2,1,0:T(8,128)(2,1)} %param.23, bf16[4,4,128,256]{3,2,1,0:T(8,128)(2,1)} %param.26), kind=kLoop, calls=%fused_computation.62 | loop fusion | flops 6291440 | bytes 4194368 | tf_op jit(solution)/shard_map/reduce_sum | solution.py:118
  10.6 0.7 copy.79
  11.3 2.3 fusion.52
  13.7 3.7 %fusion.49 = (bf16[4,2,704,128]{3,2,1,0:T(8,128)(2,1)S(1)}, bf16[4,2,128,704]{2,3,1,0:T(8,128)(2,1)}) fusion(bf16[4,2,128,704]{2,3,1,0:T(8,128)(2,1)} %param.24, bf16[4,2,128,704]{2,3,1,0:T(8,128)(2,1)} %param.27), kind=kLoop, calls=%fused_computation.68 | loop fusion | flops 6488064 | bytes 5767168 | tf_op jit(solution)/shard_map/transpose | solution.py:115
  17.6 3.6 %fusion.42 = bf16[32,704,128]{2,1,0:T(8,128)(2,1)} fusion(bf16[16,256,128]{2,1,0:T(8,128)(2,1)S(1)} %copy.79, bf16[12,704,128]{2,1,0:T(8,128)(2,1)S(1)} %bitcast.80, bf16[32]{0:T(256)(128)(2,1)S(1)} %pad.23.clone), kind=kLoop, calls=%fused_computation.48 | loop fusion | flops 28835840 | bytes 8978496 | tf_op jit(solution)/shard_map/concatenate | solution.py:124
  21.2 8.6 %all-to-all-start = ((bf16[32,704,128]{2,1,0:T(8,128)(2,1)}), bf16[32,704,128]{2,1,0:T(8,128)(2,1)}, u32[]{:S(2)}, u32[]{:S(2)}) async-start(bf16[32,704,128]{2,1,0:T(8,128)(2,1)} %fusion.42), calls=%async_computation | async-start | bytes 11534336 | tf_op jit(solution)/shard_map/all_to_all | solution.py:131
  30.6 70.6 %all-to-all-done = bf16[32,704,128]{2,1,0:T(8,128)(2,1)} async-done(((bf16[32,704,128]{2,1,0:T(8,128)(2,1)}), bf16[32,704,128]{2,1,0:T(8,128)(2,1)}, u32[]{:S(2)}, u32[]{:S(2)}) %all-to-all-start) | async-done | bytes 5767200 | tf_op jit(solution)/shard_map/all_to_all | solution.py:131
  102.2 42.5 %all-gather.8.cloned.1.call-done = f32[32,1,8832]{2,1,0:T(1,128)} async-done(((f32[1,1,8832]{2,1,0:T(1,128)}), f32[32,1,8832]{2,1,0:T(1,128)}) %all-gather.8.cloned.1.call-update) | async-done | bytes 1130512 | tf_op jit(solution)/shard_map/all_gather | solution.py:141
  144.8 1.9 reduce_sum.71
  146.7 0.7 pad.18
  148.7 80.7 %conditional.1 = (bf16[32,704,128]{2,1,0:T(8,128)(2,1)}) conditional(s32[]{:T(128)} %bitcast.8, () %tuple.19, bf16[32,704,128]{2,1,0:T(8,128)(2,1)} %all-to-all-done, bf16[32,704,128]{2,1,0:T(8,128)(2,1)} %all-to-all-done), branch_computations={%region_2.3_spmd, %region_3.5_spmd, %region_5.7_spmd} | conditional | flops 27968143360 | bytes 129499200 | solution.py:171
  154.2 6.3 %fusion.21 = f32[]{:T(128)} fusion(bf16[32,704,128]{2,1,0:T(8,128)(2,1)} %param.2), kind=kLoop, calls=%fused_computation.24 | loop fusion | flops 8650751 | bytes 5767172 | tf_op jit(solution)/shard_map/cond/branch_2_fun/reduce_sum | solution.py:20
  161.2 4.2 %fusion.22 = bf16[32,704,128]{2,1,0:T(8,128)(2,1)S(1)} fusion(bf16[32,704,128]{2,1,0:T(8,128)(2,1)} %param.2, f32[]{:T(128)S(6)} %add.73), kind=kLoop, calls=%fused_computation.25 | loop fusion | flops 8650752 | bytes 11534340 | tf_op jit(solution)/shard_map/convert.3
  165.5 3.7 %copy.76 = bf16[8,4,704,128]{3,0,2,1:T(8,128)(2,1)S(1)} copy(bf16[8,4,704,128]{3,2,1,0:T(8,128)(2,1)S(1)} %bitcast.76) | data formatting | bytes 11534336 | tf_op jit(solution)/shard_map/cond/branch_2_fun/div | solution.py:21
  169.2 2.4 copy-done
  171.6 6.8 %fusion.23 = bf16[1024,1024]{1,0:T(8,128)(2,1)S(1)} fusion(bf16[352,8,8,128]{3,2,1,0:T(8,128)(2,1)S(1)} %bitcast.85), kind=kOutput, calls=%fused_computation.29 | convolution fusion | flops 5905580032 | bytes 7864320 | tf_op jit(solution)/shard_map/cond/branch_2_fun/dot_general | solution.py:23
  178.5 17.7 %add_convert_fusion.5 = bf16[2816,1024]{1,0:T(8,128)(2,1)} fusion(bf16[352,8,8,128]{3,2,1,0:T(8,128)(2,1)} %bitcast.86, bf16[1024,1024]{1,0:T(8,128)(2,1)S(1)} %fusion.23), kind=kOutput, calls=%fused_computation.27 | convolution fusion | flops 8069840896 | bytes 13631488 | tf_op jit(solution)/shard_map/cond/branch_2_fun/dot_general | solution.py:32
  196.2 9.9 %fusion.65 = bf16[1024,1024]{1,0:T(8,128)(2,1)S(1)} fusion(bf16[2816,1024]{1,0:T(8,128)(2,1)} %add_convert_fusion.5), kind=kOutput, calls=%fused_computation.88 | convolution fusion | flops 5905580032 | bytes 7864320 | tf_op jit(solution)/shard_map/cond/branch_2_fun/dot_general | solution.py:23
  206.1 14.7 %fusion.28 = bf16[352,8,8,128]{3,1,2,0:T(8,128)(2,1)} fusion(bf16[2816,1024]{1,0:T(8,128)(2,1)} %add_convert_fusion.5, bf16[1024,1024]{1,0:T(8,128)(2,1)S(1)} %fusion.65), kind=kOutput, calls=%fused_computation.36 | convolution fusion | flops 8069840896 | bytes 13631488 | tf_op jit(solution)/shard_map/cond/branch_2_fun/dot_general | solution.py:32
  220.8 4.1 %copy.88 = bf16[352,8,8,128]{3,2,1,0:T(8,128)(2,1)S(1)} copy(bf16[352,8,8,128]{3,1,2,0:T(8,128)(2,1)} %fusion.28) | data formatting | bytes 11534336 | tf_op jit(solution)/shard_map/cond
  225.3 3.9 %copy.77 = bf16[8,4,704,128]{3,2,1,0:T(8,128)(2,1)} copy(bf16[8,4,704,128]{3,0,2,1:T(8,128)(2,1)S(1)} %bitcast_bitcast_fusion.1) | data formatting | bytes 11534336 | tf_op jit(solution)/shard_map/cond/branch_2_fun/transpose | solution.py:155
  229.4 1.7 reshape.142
  231.1 5.6 %all-to-all-start.1 = ((bf16[32,704,128]{2,1,0:T(8,128)(2,1)}), bf16[32,704,128]{2,1,0:T(8,128)(2,1)}, u32[]{:S(2)}, u32[]{:S(2)}) async-start(bf16[32,704,128]{2,1,0:T(8,128)(2,1)} %get-tuple-element.118), calls=%async_computation.1 | async-start | bytes 11534336 | tf_op jit(solution)/shard_map/all_to_all | solution.py:173
  236.8 3.5 %multiply_subtract_fusion = (f32[251,1024]{1,0:T(8,128)}, f32[251,1024]{1,0:T(8,128)}, f32[251,1024]{1,0:T(8,128)}) fusion(f32[251,1024]{1,0:T(8,128)S(1)} %copy-done.1, bf16[251,1024]{1,0:T(8,128)(2,1)} %param.31, f32[251,1024]{1,0:T(8,128)S(1)} %copy-done.2, f32[251,1024]{1,0:T(8,128)} %param.32), kind=kLoop, calls=%fused_computation.73 | loop fusion | flops 3598336 | bytes 6682624 | tf_op jit(solution)/shard_map/sub | solution.py:52
  241.4 0.7 fusion.55
  242.7 0.7 multiply_subtract_fusion.1
  243.4 64.7 %all-to-all-done.1 = bf16[32,704,128]{2,1,0:T(8,128)(2,1)} async-done(((bf16[32,704,128]{2,1,0:T(8,128)(2,1)}), bf16[32,704,128]{2,1,0:T(8,128)(2,1)}, u32[]{:S(2)}, u32[]{:S(2)}) %all-to-all-start.1) | async-done | bytes 5767200 | tf_op jit(solution)/shard_map/all_to_all | solution.py:173
  308.1 2.1 convert_multiply_fusion.2
  310.2 1.2 slice_bitcast_fusion.1
  311.4 1.8 slice_bitcast_fusion
  313.2 1.5 convert_multiply_fusion.3
  314.6 1.8 copy.84
  (57 shorter events, 4.7 us)
Async XLA Ops:
  7.2 4.1 %copy-start.3 = (bf16[4,704,128]{2,1,0:T(8,128)(2,1)S(1)}, bf16[4,704,128]{2,1,0:T(8,128)(2,1)}, u32[]{:S(2)}) copy-start(bf16[4,704,128]{2,1,0:T(8,128)(2,1)} %param.25) | copy-start | bytes 2162692
  21.2 80.1 %copy-start.8 = (f32[1,32,16]{1,2,0:T(8,128)S(1)}, f32[1,32,16]{1,2,0:T(8,128)}, u32[]{:S(2)}) copy-start(f32[1,32,16]{1,2,0:T(8,128)} %param.39) | copy-start | bytes 6148
  21.2 80.2 %copy-start.7 = (f32[4,1,2048]{2,1,0:T(1,128)S(1)}, f32[4,1,2048]{2,1,0:T(1,128)}, u32[]{:S(2)}) copy-start(f32[4,1,2048]{2,1,0:T(1,128)} %param.35) | copy-start | bytes 98308
  21.2 80.1 %all-to-all-start = ((bf16[32,704,128]{2,1,0:T(8,128)(2,1)}), bf16[32,704,128]{2,1,0:T(8,128)(2,1)}, u32[]{:S(2)}, u32[]{:S(2)}) async-start(bf16[32,704,128]{2,1,0:T(8,128)(2,1)} %fusion.42), calls=%async_computation | async-start | bytes 11534336 | tf_op jit(solution)/shard_map/all_to_all | solution.py:131
  29.9 117.6 %copy-start.13 = (s32[32]{0:T(128)S(1)}, s32[32]{0:T(128)}, u32[]{:S(2)}) copy-start(s32[32]{0:T(128)} %constant.40.clone) | copy-start | bytes 388
  29.9 114.9 %all-gather.8.cloned.1.call-start = ((), (), s32[]{:S(2)}) async-start(), calls=%async_computation.3 | async-start | bytes 1165824 | tf_op jit(solution)/shard_map/all_gather | solution.py:141
  102.2 127.2 %all-gather.6.cloned.1.call-start = ((), (), s32[]{:S(2)}) async-start(), calls=%async_computation.2 | async-start | bytes 1310720 | tf_op jit(solution)/shard_map/all_gather | solution.py:143
  169.2 2.5 copy-start
  231.1 5.6 %copy-start.1 = (f32[251,1024]{1,0:T(8,128)S(1)}, f32[251,1024]{1,0:T(8,128)}, u32[]{:S(2)}) copy-start(f32[251,1024]{1,0:T(8,128)} %param.30) | copy-start | bytes 3084292
  231.1 5.6 %copy-start.2 = (f32[251,1024]{1,0:T(8,128)S(1)}, f32[251,1024]{1,0:T(8,128)}, u32[]{:S(2)}) copy-start(f32[251,1024]{1,0:T(8,128)} %param.33) | copy-start | bytes 3084292
  231.1 77.0 %all-to-all-start.1 = ((bf16[32,704,128]{2,1,0:T(8,128)(2,1)}), bf16[32,704,128]{2,1,0:T(8,128)(2,1)}, u32[]{:S(2)}, u32[]{:S(2)}) async-start(bf16[32,704,128]{2,1,0:T(8,128)(2,1)} %get-tuple-element.118), calls=%async_computation.1 | async-start | bytes 11534336 | tf_op jit(solution)/shard_map/all_to_all | solution.py:173
  236.7 4.7 %copy-start.12 = (s32[4,7]{1,0:T(4,128)S(1)}, s32[4,7]{1,0:T(4,128)}, u32[]{:S(2)}) copy-start(s32[4,7]{1,0:T(4,128)} %param.29) | copy-start | bytes 340
  236.7 5.4 %copy-start.9 = (f32[32,16]{0,1:T(8,128)S(1)}, f32[32,16]{0,1:T(8,128)}, u32[]{:S(2)}) copy-start(f32[32,16]{0,1:T(8,128)} %param.38) | copy-start | bytes 6148
  236.7 5.4 %copy-start.10 = (f32[32,16]{0,1:T(8,128)S(1)}, f32[32,16]{0,1:T(8,128)}, u32[]{:S(2)}) copy-start(f32[32,16]{0,1:T(8,128)} %param.41) | copy-start | bytes 6148
  236.8 5.3 %copy-start.11 = (f32[32,16]{0,1:T(8,128)S(1)}, f32[32,16]{0,1:T(8,128)}, u32[]{:S(2)}) copy-start(f32[32,16]{0,1:T(8,128)} %param.40) | copy-start | bytes 6148
  236.8 6.0 %copy-start.4 = (f32[4,2048]{1,0:T(4,128)S(1)}, f32[4,2048]{1,0:T(4,128)}, u32[]{:S(2)}) copy-start(f32[4,2048]{1,0:T(4,128)} %param.34) | copy-start | bytes 98308
  236.8 5.9 %copy-start.5 = (f32[4,2048]{1,0:T(4,128)S(1)}, f32[4,2048]{1,0:T(4,128)}, u32[]{:S(2)}) copy-start(f32[4,2048]{1,0:T(4,128)} %param.37) | copy-start | bytes 98308
  236.8 5.9 %copy-start.6 = (f32[4,2048]{1,0:T(4,128)S(1)}, f32[4,2048]{1,0:T(4,128)}, u32[]{:S(2)}) copy-start(f32[4,2048]{1,0:T(4,128)} %param.36) | copy-start | bytes 98308
Sparse Core Ops, SparseCore 0:
  102.3 42.4 all-gather.7
  147.6 23.6 all-gather.5

commit v5 on v4

--- a/solution.py
+++ b/solution.py
@@ -120,6 +120,12 @@
     def padded(block):
         return jnp.pad(block, ((0, ff_block - block.shape[0]), (0, 0)))
 
+    bias_flat = bias_partial.reshape(-1)
+    bias_across = lax.all_gather(
+        jnp.pad(bias_flat, (0, 65536 - bias_flat.shape[0])), "section", axis=0, tiled=False
+    )
+    bias_sections = jnp.sum(bias_across[:, : bias_flat.shape[0]], axis=0)
+
     idle_count = group_count - n_rect - n_square
     outgoing = jnp.concatenate(
         [
@@ -130,17 +136,14 @@
     )
     incoming = lax.all_to_all(outgoing, ("shards", "tensor"), split_axis=0, concat_axis=0, tiled=True)
 
-    norm_partial_late, square_ss, rect_ss, bias_partial_late, incoming = lax.optimization_barrier(
-        (norm_partial, square_ss, rect_ss, bias_partial, incoming)
+    norm_partial_late, square_ss, rect_ss, bias_sections, incoming = lax.optimization_barrier(
+        (norm_partial, square_ss, rect_ss, bias_sections, incoming)
     )
     norm_width = norm_partial.shape[0] * norm_partial.shape[2]
-    bias_flat = bias_partial_late.reshape(-1)
-    bias_width = bias_flat.shape[0]
-    packed = jnp.concatenate([norm_partial_late.reshape(norm_width), bias_flat, square_ss, rect_ss])
+    bias_width = bias_sections.shape[0]
+    packed = jnp.concatenate([norm_partial_late.reshape(norm_width), bias_sections, square_ss, rect_ss])
     packed = jnp.pad(packed, (0, (-packed.shape[0]) % 128))
     gathered = jnp.sum(lax.all_gather(packed, ("shards", "tensor"), axis=0, tiled=False), axis=0)
-    bias_section = jnp.pad(gathered[norm_width : norm_width + bias_width], (0, 65536 - bias_width))
-    bias_all = lax.all_gather(bias_section, "section", axis=0, tiled=False)
 
     def run(arrived_blocks, width):
         whole = (
@@ -169,14 +172,14 @@
         return jnp.zeros((group_count, ff_block, rows_block), jnp.bfloat16)
 
     returning = lax.switch(my_kind, [idle_branch, square_branch, rect_branch], incoming)
-    returning, gathered, bias_all = lax.optimization_barrier((returning, gathered, bias_all))
+    returning, gathered = lax.optimization_barrier((returning, gathered))
     arrived = lax.all_to_all(returning, ("shards", "tensor"), split_axis=0, concat_axis=0, tiled=True)
 
     norm_grad = gathered[:norm_width].reshape(norm_partial.shape[0], norm_partial.shape[2])
     ss_start = norm_width + bias_width
     square_norm = jnp.sqrt(gathered[ss_start : ss_start + n_square])
     rect_norm = jnp.sqrt(gathered[ss_start + n_square : ss_start + n_square + n_rect])
-    bias_grad = jnp.sum(bias_all, axis=0)[:bias_width].reshape(bias_table.shape)
+    bias_grad = gathered[norm_width : norm_width + bias_width].reshape(bias_table.shape)
     rms_all = jnp.concatenate(
         [
             square_norm.reshape(layers_here, 4) / math.sqrt(D * D),

time: 329 us -> 283 us (0.86)
  waiting for transfers between devices: 178 us -> 134 us
    all_gather x1, waiting for transfers between devices: 42.5 us -> 0.02 us  [on_device(): lax.all_gather(packed, ('shards', 'tensor'), axis=0, tiled=False)]
    all_to_all x1, waiting for transfers between devices: 70.6 us -> 41.2 us  [on_device(): lax.all_to_all(outgoing, ('shards', 'tensor'), split_axis=0, concat_axis=...]
    all_gather x1, waiting for transfers between devices: 0.02 us -> 26.7 us  [on_device(): lax.all_gather(jnp.pad(bias_flat, (0, 65536 - bias_flat.shape[0])), 'sect...]
  transfers between devices with their start and end apart: 4 -> 4, of which waited for: 3 -> 3; matrix products, arithmetic and copies ran while one was open for 25% -> 29% of each run, Pallas kernels for 0% -> 0%
where the time goes in v5:
time: 283 us; the launch traced here: 278 us
  waiting for transfers between devices  134 us (47%)
  matrix products  49.1 us (17%)
  other arithmetic  34.9 us (12%)
  local copies, waits for them, and re-layouts  24.6 us (9%)
  between operations  15.2 us (5%)
  starting transfers between devices  13.8 us (5%)
  loops' own time  6.46 us (2%)
    all_to_all x1, waiting for transfers between devices, on_device(): lax.all_to_all(returning, ('shards', 'tensor'), split_axis=0, concat_axis...  65.7 us
    all_to_all x1, waiting for transfers between devices, on_device(): lax.all_to_all(outgoing, ('shards', 'tensor'), split_axis=0, concat_axis=...  41.2 us
    dot_general x2, matrix products, newton_schulz_transposed(): lax.dot_general(current, polynomial, (((1,), (1,)), ((), ())), preferred_...  32.3 us
    all_gather x1, waiting for transfers between devices, on_device(): lax.all_gather(jnp.pad(bias_flat, (0, 65536 - bias_flat.shape[0])), 'sect...  26.7 us
    dot_general x2, matrix products, newton_schulz_transposed(): lax.dot_general(current, current, (((0,), (0,)), ((), ())), preferred_ele...  16.7 us
    all_to_all x1, starting transfers between devices, on_device(): lax.all_to_all(outgoing, ('shards', 'tensor'), split_axis=0, concat_axis=...  8.65 us
    cond x3, local copies, waits for them, and re-layouts  6.56 us
    another operation x1, loops' own time, on_device(): lax.switch(my_kind, [idle_branch, square_branch, rect_branch], incoming)  6.46 us
  transfers between devices with their start and end apart: 4, of which 3 were waited for; matrix products, arithmetic and copies ran while one was open for 29% of the time, Pallas kernels for 0%

profile of v5, /device:TPU:2, one launch (start us, length us, event | category | flops | bytes accessed | tf_op | source)
XLA Modules:
  0.0 277.6 jit_solution(3579538302872693677)
XLA Ops:
  7.2 3.4 %multiply_reduce_fusion.1 = (f32[4,4]{1,0:T(4,128)S(1)}, bf16[4,4,128,256]{3,2,1,0:T(8,128)(2,1)S(1)}, bf16[4,4,128,256]{3,2,1,0:T(8,128)(2,1)}) fusion(bf16[4,4,128,256]{3,2,1,0:T(8,128)(2,1)} %param.23, bf16[4,4,128,256]{3,2,1,0:T(8,128)(2,1)} %param.26), kind=kLoop, calls=%fused_computation.62 | loop fusion | flops 6291440 | bytes 4194368 | tf_op jit(solution)/shard_map/reduce_sum | solution.py:118
  10.6 0.7 copy.95
  11.3 2.3 fusion.52
  13.7 3.7 %fusion.49 = (bf16[4,2,704,128]{3,2,1,0:T(8,128)(2,1)S(1)}, bf16[4,2,128,704]{2,3,1,0:T(8,128)(2,1)}) fusion(bf16[4,2,128,704]{2,3,1,0:T(8,128)(2,1)} %param.24, bf16[4,2,128,704]{2,3,1,0:T(8,128)(2,1)} %param.27), kind=kLoop, calls=%fused_computation.68 | loop fusion | flops 6488064 | bytes 5767168 | tf_op jit(solution)/shard_map/transpose | solution.py:115
  17.6 3.6 %fusion.42 = bf16[32,704,128]{2,1,0:T(8,128)(2,1)} fusion(bf16[16,256,128]{2,1,0:T(8,128)(2,1)S(1)} %copy.95, bf16[12,704,128]{2,1,0:T(8,128)(2,1)S(1)} %bitcast.80, bf16[32]{0:T(256)(128)(2,1)S(1)} %pad.23.clone), kind=kLoop, calls=%fused_computation.48 | loop fusion | flops 28835840 | bytes 8978496 | tf_op jit(solution)/shard_map/concatenate | solution.py:130
  21.2 8.6 %all-to-all-start = ((bf16[32,704,128]{2,1,0:T(8,128)(2,1)}), bf16[32,704,128]{2,1,0:T(8,128)(2,1)}, u32[]{:S(2)}, u32[]{:S(2)}) async-start(bf16[32,704,128]{2,1,0:T(8,128)(2,1)} %fusion.42), calls=%async_computation | async-start | bytes 11534336 | tf_op jit(solution)/shard_map/all_to_all | solution.py:137
  30.1 0.7 pad.16
  31.6 26.7 %all-gather.6.cloned.1.call-done = f32[262144]{0:T(1024)} async-done(((f32[65536]{0:T(1024)}), f32[262144]{0:T(1024)}) %all-gather.6.cloned.1.call-update) | async-done | bytes 1048592 | tf_op jit(solution)/shard_map/all_gather | solution.py:124
  58.3 1.7 reshape.144
  60.1 41.2 %all-to-all-done = bf16[32,704,128]{2,1,0:T(8,128)(2,1)} async-done(((bf16[32,704,128]{2,1,0:T(8,128)(2,1)}), bf16[32,704,128]{2,1,0:T(8,128)(2,1)}, u32[]{:S(2)}, u32[]{:S(2)}) %all-to-all-start) | async-done | bytes 5767200 | tf_op jit(solution)/shard_map/all_to_all | solution.py:137
  103.3 80.5 %conditional.1 = (bf16[32,704,128]{2,1,0:T(8,128)(2,1)}) conditional(s32[]{:T(128)} %bitcast.8, () %tuple.19, bf16[32,704,128]{2,1,0:T(8,128)(2,1)} %all-to-all-done, bf16[32,704,128]{2,1,0:T(8,128)(2,1)} %all-to-all-done), branch_computations={%region_3.4_spmd, %region_4.6_spmd, %region_6.8_spmd} | conditional | flops 27968143360 | bytes 129499200 | solution.py:174
  108.8 6.2 %fusion.21 = f32[]{:T(128)} fusion(bf16[32,704,128]{2,1,0:T(8,128)(2,1)} %param.2), kind=kLoop, calls=%fused_computation.24 | loop fusion | flops 8650751 | bytes 5767172 | tf_op jit(solution)/shard_map/cond/branch_2_fun/reduce_sum | solution.py:20
  115.7 4.2 %fusion.22 = bf16[32,704,128]{2,1,0:T(8,128)(2,1)S(1)} fusion(bf16[32,704,128]{2,1,0:T(8,128)(2,1)} %param.2, f32[]{:T(128)S(6)} %add.73), kind=kLoop, calls=%fused_computation.25 | loop fusion | flops 8650752 | bytes 11534340 | tf_op jit(solution)/shard_map/convert.3
  119.9 3.7 %copy.91 = bf16[8,4,704,128]{3,0,2,1:T(8,128)(2,1)S(1)} copy(bf16[8,4,704,128]{3,2,1,0:T(8,128)(2,1)S(1)} %bitcast.76) | data formatting | bytes 11534336 | tf_op jit(solution)/shard_map/cond/branch_2_fun/div | solution.py:21
  123.6 2.4 copy-done
  126.1 6.8 %fusion.23 = bf16[1024,1024]{1,0:T(8,128)(2,1)S(1)} fusion(bf16[352,8,8,128]{3,2,1,0:T(8,128)(2,1)S(1)} %bitcast.85), kind=kOutput, calls=%fused_computation.29 | convolution fusion | flops 5905580032 | bytes 7864320 | tf_op jit(solution)/shard_map/cond/branch_2_fun/dot_general | solution.py:23
  132.9 17.6 %add_convert_fusion.5 = bf16[2816,1024]{1,0:T(8,128)(2,1)} fusion(bf16[352,8,8,128]{3,2,1,0:T(8,128)(2,1)} %bitcast.86, bf16[1024,1024]{1,0:T(8,128)(2,1)S(1)} %fusion.23), kind=kOutput, calls=%fused_computation.27 | convolution fusion | flops 8069840896 | bytes 13631488 | tf_op jit(solution)/shard_map/cond/branch_2_fun/dot_general | solution.py:32
  150.6 9.9 %fusion.65 = bf16[1024,1024]{1,0:T(8,128)(2,1)S(1)} fusion(bf16[2816,1024]{1,0:T(8,128)(2,1)} %add_convert_fusion.5), kind=kOutput, calls=%fused_computation.89 | convolution fusion | flops 5905580032 | bytes 7864320 | tf_op jit(solution)/shard_map/cond/branch_2_fun/dot_general | solution.py:23
  160.5 14.7 %fusion.28 = bf16[352,8,8,128]{3,1,2,0:T(8,128)(2,1)} fusion(bf16[2816,1024]{1,0:T(8,128)(2,1)} %add_convert_fusion.5, bf16[1024,1024]{1,0:T(8,128)(2,1)S(1)} %fusion.65), kind=kOutput, calls=%fused_computation.36 | convolution fusion | flops 8069840896 | bytes 13631488 | tf_op jit(solution)/shard_map/cond/branch_2_fun/dot_general | solution.py:32
  175.2 4.1 %copy.103 = bf16[352,8,8,128]{3,2,1,0:T(8,128)(2,1)S(1)} copy(bf16[352,8,8,128]{3,1,2,0:T(8,128)(2,1)} %fusion.28) | data formatting | bytes 11534336 | tf_op jit(solution)/shard_map/cond
  179.7 3.9 %copy.92 = bf16[8,4,704,128]{3,2,1,0:T(8,128)(2,1)} copy(bf16[8,4,704,128]{3,0,2,1:T(8,128)(2,1)S(1)} %bitcast_bitcast_fusion.1) | data formatting | bytes 11534336 | tf_op jit(solution)/shard_map/cond/branch_2_fun/transpose | solution.py:158
  183.8 1.9 reduce_sum.72
  185.8 5.1 %all-to-all-start.1 = ((bf16[32,704,128]{2,1,0:T(8,128)(2,1)}), bf16[32,704,128]{2,1,0:T(8,128)(2,1)}, u32[]{:S(2)}, u32[]{:S(2)}) async-start(bf16[32,704,128]{2,1,0:T(8,128)(2,1)} %get-tuple-element.132), calls=%async_computation.1 | async-start | bytes 11534336 | tf_op jit(solution)/shard_map/all_to_all | solution.py:176
  190.9 3.2 %multiply_subtract_fusion = (f32[251,1024]{1,0:T(8,128)}, f32[251,1024]{1,0:T(8,128)}, f32[251,1024]{1,0:T(8,128)}) fusion(f32[251,1024]{1,0:T(8,128)S(1)} %copy-done.1, bf16[251,1024]{1,0:T(8,128)(2,1)} %param.31, f32[251,1024]{1,0:T(8,128)S(1)} %copy-done.2, f32[251,1024]{1,0:T(8,128)S(1)} %copy-done.3), kind=kLoop, calls=%fused_computation.73 | loop fusion | flops 3598336 | bytes 6682624 | tf_op jit(solution)/shard_map/sub | solution.py:52
  194.6 0.7 fusion.55
  195.9 0.7 multiply_subtract_fusion.1
  196.6 65.7 %all-to-all-done.1 = bf16[32,704,128]{2,1,0:T(8,128)(2,1)} async-done(((bf16[32,704,128]{2,1,0:T(8,128)(2,1)}), bf16[32,704,128]{2,1,0:T(8,128)(2,1)}, u32[]{:S(2)}, u32[]{:S(2)}) %all-to-all-start.1) | async-done | bytes 5767200 | tf_op jit(solution)/shard_map/all_to_all | solution.py:176
  262.3 2.1 convert_multiply_fusion.2
  264.3 1.2 slice_bitcast_fusion.1
  265.5 1.8 slice_bitcast_fusion
  267.3 1.5 convert_multiply_fusion.3
  268.7 1.8 copy.99
  (58 shorter events, 4.1 us)
Async XLA Ops:
  7.2 4.1 %copy-start.4 = (bf16[4,704,128]{2,1,0:T(8,128)(2,1)S(1)}, bf16[4,704,128]{2,1,0:T(8,128)(2,1)}, u32[]{:S(2)}) copy-start(bf16[4,704,128]{2,1,0:T(8,128)(2,1)} %param.25) | copy-start | bytes 2162692
  21.2 8.7 %copy-start.9 = (f32[1,32,16]{1,2,0:T(8,128)S(1)}, f32[1,32,16]{1,2,0:T(8,128)}, u32[]{:S(2)}) copy-start(f32[1,32,16]{1,2,0:T(8,128)} %param.39) | copy-start | bytes 6148
  21.2 80.1 %all-to-all-start = ((bf16[32,704,128]{2,1,0:T(8,128)(2,1)}), bf16[32,704,128]{2,1,0:T(8,128)(2,1)}, u32[]{:S(2)}, u32[]{:S(2)}) async-start(bf16[32,704,128]{2,1,0:T(8,128)(2,1)} %fusion.42), calls=%async_computation | async-start | bytes 11534336 | tf_op jit(solution)/shard_map/all_to_all | solution.py:137
  29.8 71.4 %copy-start.8 = (f32[4,1,2048]{2,1,0:T(1,128)S(1)}, f32[4,1,2048]{2,1,0:T(1,128)}, u32[]{:S(2)}) copy-start(f32[4,1,2048]{2,1,0:T(1,128)} %param.35) | copy-start | bytes 98308
  29.8 72.2 %copy-start.14 = (s32[32]{0:T(128)S(1)}, s32[32]{0:T(128)}, u32[]{:S(2)}) copy-start(s32[32]{0:T(128)} %constant.40.clone) | copy-start | bytes 388
  29.9 28.5 %all-gather.6.cloned.1.call-start = ((), (), s32[]{:S(2)}) async-start(), calls=%async_computation.2 | async-start | bytes 1310720 | tf_op jit(solution)/shard_map/all_gather | solution.py:124
  30.8 153.0 %all-gather.8.cloned.1.call-start = ((), (), s32[]{:S(2)}) async-start(), calls=%async_computation.3 | async-start | bytes 1165824 | tf_op jit(solution)/shard_map/all_gather | solution.py:146
  123.6 2.4 copy-start
  185.7 5.1 %copy-start.1 = (f32[251,1024]{1,0:T(8,128)S(1)}, f32[251,1024]{1,0:T(8,128)}, u32[]{:S(2)}) copy-start(f32[251,1024]{1,0:T(8,128)} %param.30) | copy-start | bytes 3084292
  185.7 5.1 %copy-start.2 = (f32[251,1024]{1,0:T(8,128)S(1)}, f32[251,1024]{1,0:T(8,128)}, u32[]{:S(2)}) copy-start(f32[251,1024]{1,0:T(8,128)} %param.33) | copy-start | bytes 3084292
  185.8 5.1 %copy-start.3 = (f32[251,1024]{1,0:T(8,128)S(1)}, f32[251,1024]{1,0:T(8,128)}, u32[]{:S(2)}) copy-start(f32[251,1024]{1,0:T(8,128)} %param.32) | copy-start | bytes 3084292
  185.8 76.5 %all-to-all-start.1 = ((bf16[32,704,128]{2,1,0:T(8,128)(2,1)}), bf16[32,704,128]{2,1,0:T(8,128)(2,1)}, u32[]{:S(2)}, u32[]{:S(2)}) async-start(bf16[32,704,128]{2,1,0:T(8,128)(2,1)} %get-tuple-element.132), calls=%async_computation.1 | async-start | bytes 11534336 | tf_op jit(solution)/shard_map/all_to_all | solution.py:176
  190.9 3.7 %copy-start.13 = (s32[4,7]{1,0:T(4,128)S(1)}, s32[4,7]{1,0:T(4,128)}, u32[]{:S(2)}) copy-start(s32[4,7]{1,0:T(4,128)} %param.29) | copy-start | bytes 340
  190.9 4.4 %copy-start.10 = (f32[32,16]{0,1:T(8,128)S(1)}, f32[32,16]{0,1:T(8,128)}, u32[]{:S(2)}) copy-start(f32[32,16]{0,1:T(8,128)} %param.38) | copy-start | bytes 6148
  190.9 4.4 %copy-start.11 = (f32[32,16]{0,1:T(8,128)S(1)}, f32[32,16]{0,1:T(8,128)}, u32[]{:S(2)}) copy-start(f32[32,16]{0,1:T(8,128)} %param.41) | copy-start | bytes 6148
  190.9 4.4 %copy-start.12 = (f32[32,16]{0,1:T(8,128)S(1)}, f32[32,16]{0,1:T(8,128)}, u32[]{:S(2)}) copy-start(f32[32,16]{0,1:T(8,128)} %param.40) | copy-start | bytes 6148
  190.9 5.0 %copy-start.5 = (f32[4,2048]{1,0:T(4,128)S(1)}, f32[4,2048]{1,0:T(4,128)}, u32[]{:S(2)}) copy-start(f32[4,2048]{1,0:T(4,128)} %param.34) | copy-start | bytes 98308
  190.9 5.0 %copy-start.6 = (f32[4,2048]{1,0:T(4,128)S(1)}, f32[4,2048]{1,0:T(4,128)}, u32[]{:S(2)}) copy-start(f32[4,2048]{1,0:T(4,128)} %param.37) | copy-start | bytes 98308
  190.9 5.0 %copy-start.7 = (f32[4,2048]{1,0:T(4,128)S(1)}, f32[4,2048]{1,0:T(4,128)}, u32[]{:S(2)}) copy-start(f32[4,2048]{1,0:T(4,128)} %param.36) | copy-start | bytes 98308
Sparse Core Ops, SparseCore 0:
  32.9 25.3 all-gather.5
  102.1 42.4 all-gather.7

commit v6 on v5

--- a/solution.py
+++ b/solution.py
@@ -15,10 +15,8 @@
 coef_third = 2.0315
 
 
-def newton_schulz_transposed(rows_bf16):
-    as_f32 = rows_bf16.astype(jnp.float32)
-    norm_value = jnp.sqrt(jnp.sum(as_f32 * as_f32))
-    current = (as_f32 / (norm_value + 1e-07)).astype(jnp.bfloat16)
+def newton_schulz_transposed(rows_bf16, norm_value):
+    current = (rows_bf16.astype(jnp.float32) / (norm_value + 1e-07)).astype(jnp.bfloat16)
     for sweep_index in range(NS_STEPS):
         gram_form = lax.dot_general(
             current, current, (((0,), (0,)), ((), ())), preferred_element_type=jnp.float32
@@ -120,11 +118,15 @@
     def padded(block):
         return jnp.pad(block, ((0, ff_block - block.shape[0]), (0, 0)))
 
+    norm_width = norm_partial.shape[0] * norm_partial.shape[2]
     bias_flat = bias_partial.reshape(-1)
-    bias_across = lax.all_gather(
-        jnp.pad(bias_flat, (0, 65536 - bias_flat.shape[0])), "section", axis=0, tiled=False
-    )
-    bias_sections = jnp.sum(bias_across[:, : bias_flat.shape[0]], axis=0)
+    bias_width = bias_flat.shape[0]
+    packed = jnp.concatenate([norm_partial.reshape(norm_width), bias_flat, square_ss, rect_ss])
+    packed = jnp.pad(packed, (0, (-packed.shape[0]) % 128))
+    gathered = jnp.sum(lax.all_gather(packed, ("shards", "tensor"), axis=0, tiled=False), axis=0)
+    ss_start = norm_width + bias_width
+    square_norm = jnp.sqrt(gathered[ss_start : ss_start + n_square])
+    rect_norm = jnp.sqrt(gathered[ss_start + n_square : ss_start + n_square + n_rect])
 
     idle_count = group_count - n_rect - n_square
     outgoing = jnp.concatenate(
@@ -136,23 +138,21 @@
     )
     incoming = lax.all_to_all(outgoing, ("shards", "tensor"), split_axis=0, concat_axis=0, tiled=True)
 
-    norm_partial_late, square_ss, rect_ss, bias_sections, incoming = lax.optimization_barrier(
-        (norm_partial, square_ss, rect_ss, bias_sections, incoming)
-    )
-    norm_width = norm_partial.shape[0] * norm_partial.shape[2]
-    bias_width = bias_sections.shape[0]
-    packed = jnp.concatenate([norm_partial_late.reshape(norm_width), bias_sections, square_ss, rect_ss])
-    packed = jnp.pad(packed, (0, (-packed.shape[0]) % 128))
-    gathered = jnp.sum(lax.all_gather(packed, ("shards", "tensor"), axis=0, tiled=False), axis=0)
-
-    def run(arrived_blocks, width):
+    bias_group, incoming = lax.optimization_barrier(
+        (gathered[norm_width : norm_width + bias_width], incoming)
+    )
+    bias_all = lax.all_gather(
+        jnp.pad(bias_group, (0, 65536 - bias_width)), "section", axis=0, tiled=False
+    )
+
+    def run(arrived_blocks, width, norm_value):
         whole = (
             arrived_blocks[:, :width]
             .reshape(shards_count, tensor_count, width, rows_block)
             .transpose(1, 2, 0, 3)
             .reshape(tensor_count * width, shards_count * rows_block)
         )
-        done = newton_schulz_transposed(whole)
+        done = newton_schulz_transposed(whole, norm_value)
         back = (
             done.reshape(tensor_count, width, shards_count, rows_block)
             .transpose(2, 0, 1, 3)
@@ -161,25 +161,23 @@
         return jnp.pad(back, ((0, 0), (0, ff_block - width), (0, 0)))
 
     my_kind = kind_table[my_index]
+    my_mat = index_table[my_index]
 
     def square_branch(arrived_blocks):
-        return run(arrived_blocks, cols_block)
+        return run(arrived_blocks, cols_block, square_norm[my_mat])
 
     def rect_branch(arrived_blocks):
-        return run(arrived_blocks, ff_block)
+        return run(arrived_blocks, ff_block, rect_norm[my_mat])
 
     def idle_branch(arrived_blocks):
         return jnp.zeros((group_count, ff_block, rows_block), jnp.bfloat16)
 
     returning = lax.switch(my_kind, [idle_branch, square_branch, rect_branch], incoming)
-    returning, gathered = lax.optimization_barrier((returning, gathered))
+    returning, bias_all = lax.optimization_barrier((returning, bias_all))
     arrived = lax.all_to_all(returning, ("shards", "tensor"), split_axis=0, concat_axis=0, tiled=True)
 
     norm_grad = gathered[:norm_width].reshape(norm_partial.shape[0], norm_partial.shape[2])
-    ss_start = norm_width + bias_width
-    square_norm = jnp.sqrt(gathered[ss_start : ss_start + n_square])
-    rect_norm = jnp.sqrt(gathered[ss_start + n_square : ss_start + n_square + n_rect])
-    bias_grad = gathered[norm_width : norm_width + bias_width].reshape(bias_table.shape)
+    bias_grad = jnp.sum(bias_all[:, :bias_width], axis=0).reshape(bias_table.shape)
     rms_all = jnp.concatenate(
         [
             square_norm.reshape(layers_here, 4) / math.sqrt(D * D),

time: 283 us -> 287 us (1.014)
  waiting for transfers between devices: 134 us -> 142 us
  other arithmetic: 34.9 us -> 28 us
    all_gather x1, waiting for transfers between devices: 0.02 us -> 76.3 us  [on_device(): lax.all_gather(packed, ('shards', 'tensor'), axis=0, tiled=False)]
    all_to_all x1, waiting for transfers between devices: 41.2 us -> 0.01 us  [on_device(): lax.all_to_all(outgoing, ('shards', 'tensor'), split_axis=0, concat_axis=...]
    all_gather x1, waiting for transfers between devices: 26.7 us -> 0.02 us  [on_device(): lax.all_gather(jnp.pad(bias_group, (0, 65536 - bias_width)), 'section', a...]
    reduce_sum x2 -> x1, other arithmetic: 6.22 us -> 0.02 us  [on_device(): jnp.sum(bias_all[:, :bias_width], axis=0).reshape(bias_table.shape)]
  transfers between devices with their start and end apart: 4 -> 4, of which waited for: 3 -> 2; matrix products, arithmetic and copies ran while one was open for 29% -> 27% of each run, Pallas kernels for 0% -> 0%
where the time goes in v6:
time: 287 us; the launch traced here: 281 us
  waiting for transfers between devices  142 us (49%)
  matrix products  49.1 us (17%)
  other arithmetic  28 us (10%)
  local copies, waits for them, and re-layouts  25.8 us (9%)
  between operations  15.2 us (5%)
  starting transfers between devices  14.1 us (5%)
  loops' own time  7.12 us (2%)
    all_gather x1, waiting for transfers between devices, on_device(): lax.all_gather(packed, ('shards', 'tensor'), axis=0, tiled=False)  76.3 us
    all_to_all x1, waiting for transfers between devices, on_device(): lax.all_to_all(returning, ('shards', 'tensor'), split_axis=0, concat_axis...  65.4 us
    dot_general x2, matrix products, newton_schulz_transposed(): lax.dot_general(current, polynomial, (((1,), (1,)), ((), ())), preferred_...  32.3 us
    dot_general x2, matrix products, newton_schulz_transposed(): lax.dot_general(current, current, (((0,), (0,)), ((), ())), preferred_ele...  16.8 us
    all_to_all x1, starting transfers between devices, on_device(): lax.all_to_all(outgoing, ('shards', 'tensor'), split_axis=0, concat_axis=...  8.65 us
    another operation x1, loops' own time, on_device(): lax.switch(my_kind, [idle_branch, square_branch, rect_branch], incoming)  7.12 us
    cond x3, local copies, waits for them, and re-layouts  6.59 us
  transfers between devices with their start and end apart: 4, of which 2 were waited for; matrix products, arithmetic and copies ran while one was open for 27% of the time, Pallas kernels for 0%

profile of v6, /device:TPU:2, one launch (start us, length us, event | category | flops | bytes accessed | tf_op | source)
XLA Modules:
  0.0 281.1 jit_solution(7881326985511902637)
XLA Ops:
  7.2 3.3 %multiply_reduce_fusion.1 = (f32[4,4]{1,0:T(4,128)S(1)}, bf16[4,4,128,256]{3,2,1,0:T(8,128)(2,1)S(1)}, bf16[4,4,128,256]{3,2,1,0:T(8,128)(2,1)}) fusion(bf16[4,4,128,256]{3,2,1,0:T(8,128)(2,1)} %param.24, bf16[4,4,128,256]{3,2,1,0:T(8,128)(2,1)} %param.27), kind=kLoop, calls=%fused_computation.56 | loop fusion | flops 6291440 | bytes 4194368 | tf_op jit(solution)/shard_map/reduce_sum | solution.py:116
  10.5 0.7 copy.96
  11.2 3.8 %fusion.45 = (bf16[4,2,704,128]{3,2,1,0:T(8,128)(2,1)S(1)}, bf16[4,2,128,704]{2,3,1,0:T(8,128)(2,1)}) fusion(bf16[4,2,128,704]{2,3,1,0:T(8,128)(2,1)} %param.25, bf16[4,2,128,704]{2,3,1,0:T(8,128)(2,1)} %param.28), kind=kLoop, calls=%fused_computation.62 | loop fusion | flops 6488064 | bytes 5767168 | tf_op jit(solution)/shard_map/transpose | solution.py:113
  15.0 1.2 fusion.48
  16.5 3.6 %fusion.38 = bf16[32,704,128]{2,1,0:T(8,128)(2,1)} fusion(bf16[16,256,128]{2,1,0:T(8,128)(2,1)S(1)} %copy.96, bf16[12,704,128]{2,1,0:T(8,128)(2,1)S(1)} %bitcast.83, bf16[32]{0:T(256)(128)(2,1)S(1)} %pad.23.clone), kind=kLoop, calls=%fused_computation.42 | loop fusion | flops 28835840 | bytes 8978496 | tf_op jit(solution)/shard_map/concatenate | solution.py:132
  20.1 8.6 %all-to-all-start = ((bf16[32,704,128]{2,1,0:T(8,128)(2,1)}), bf16[32,704,128]{2,1,0:T(8,128)(2,1)}, u32[]{:S(2)}, u32[]{:S(2)}) async-start(bf16[32,704,128]{2,1,0:T(8,128)(2,1)} %fusion.38), calls=%async_computation | async-start | bytes 11534336 | tf_op jit(solution)/shard_map/all_to_all | solution.py:139
  29.8 0.6 reshape.140
  30.5 76.3 %all-gather.8.cloned.1.call-done = f32[32,1,8832]{2,1,0:T(1,128)} async-done(((f32[1,1,8832]{2,1,0:T(1,128)}), f32[32,1,8832]{2,1,0:T(1,128)}) %all-gather.8.cloned.1.call-update) | async-done | bytes 1130512 | tf_op jit(solution)/shard_map/all_gather | solution.py:126
  106.8 1.9 reduce_sum.53
  108.7 0.7 pad.18
  111.4 75.7 %conditional.1 = (bf16[32,704,128]{2,1,0:T(8,128)(2,1)}) conditional(s32[]{:T(128)} %bitcast.10, () %tuple.19, (bf16[32,704,128]{2,1,0:T(8,128)(2,1)}, f32[16]{0:T(128)S(1)}, s32[]{:T(128)}) %tuple.21, (bf16[32,704,128]{2,1,0:T(8,128)(2,1)}, f32[12]{0:T(128)S(1)}, s32[]{:T(128)}) %tuple.22), branch_computations={%region_3.4_spmd, %region_4.5_spmd, %region_5.6_spmd} | conditional | flops 27959492608 | bytes 123732160 | solution.py:175
  118.9 4.3 %divide_convert_fusion.1 = bf16[32,704,128]{2,1,0:T(8,128)(2,1)S(1)} fusion(bf16[32,704,128]{2,1,0:T(8,128)(2,1)} %get-tuple-element.21, f32[]{:T(128)} %bitcast.5), kind=kLoop, calls=%fused_computation.21 | loop fusion | flops 8650752 | bytes 11534340 | tf_op jit(solution)/shard_map/convert.3
  123.2 3.7 %copy.92 = bf16[8,4,704,128]{3,0,2,1:T(8,128)(2,1)S(1)} copy(bf16[8,4,704,128]{3,2,1,0:T(8,128)(2,1)S(1)} %bitcast.79) | data formatting | bytes 11534336 | tf_op jit(solution)/shard_map/cond/branch_2_fun/div | solution.py:19
  126.9 2.5 copy-done
  129.4 6.8 %fusion.19 = bf16[1024,1024]{1,0:T(8,128)(2,1)S(1)} fusion(bf16[352,8,8,128]{3,2,1,0:T(8,128)(2,1)S(1)} %bitcast.88), kind=kOutput, calls=%fused_computation.23 | convolution fusion | flops 5905580032 | bytes 7864320 | tf_op jit(solution)/shard_map/cond/branch_2_fun/dot_general | solution.py:21
  136.2 17.6 %add_convert_fusion.5 = bf16[2816,1024]{1,0:T(8,128)(2,1)} fusion(bf16[352,8,8,128]{3,2,1,0:T(8,128)(2,1)} %bitcast.89, bf16[1024,1024]{1,0:T(8,128)(2,1)S(1)} %fusion.19), kind=kOutput, calls=%fused_computation.20 | convolution fusion | flops 8069840896 | bytes 13631488 | tf_op jit(solution)/shard_map/cond/branch_2_fun/dot_general | solution.py:30
  153.9 9.9 %fusion.61 = bf16[1024,1024]{1,0:T(8,128)(2,1)S(1)} fusion(bf16[2816,1024]{1,0:T(8,128)(2,1)} %add_convert_fusion.5), kind=kOutput, calls=%fused_computation.83 | convolution fusion | flops 5905580032 | bytes 7864320 | tf_op jit(solution)/shard_map/cond/branch_2_fun/dot_general | solution.py:21
  163.8 14.7 %fusion.24 = bf16[352,8,8,128]{3,1,2,0:T(8,128)(2,1)} fusion(bf16[2816,1024]{1,0:T(8,128)(2,1)} %add_convert_fusion.5, bf16[1024,1024]{1,0:T(8,128)(2,1)S(1)} %fusion.61), kind=kOutput, calls=%fused_computation.30 | convolution fusion | flops 8069840896 | bytes 13631488 | tf_op jit(solution)/shard_map/cond/branch_2_fun/dot_general | solution.py:30
  178.5 4.1 %copy.104 = bf16[352,8,8,128]{3,2,1,0:T(8,128)(2,1)S(1)} copy(bf16[352,8,8,128]{3,1,2,0:T(8,128)(2,1)} %fusion.24) | data formatting | bytes 11534336 | tf_op jit(solution)/shard_map/cond
  183.0 3.9 %copy.93 = bf16[8,4,704,128]{3,2,1,0:T(8,128)(2,1)} copy(bf16[8,4,704,128]{3,0,2,1:T(8,128)(2,1)S(1)} %bitcast_bitcast_fusion.1) | data formatting | bytes 11534336 | tf_op jit(solution)/shard_map/cond/branch_2_fun/transpose | solution.py:158
  187.1 1.7 reshape.139
  188.9 5.4 %all-to-all-start.1 = ((bf16[32,704,128]{2,1,0:T(8,128)(2,1)}), bf16[32,704,128]{2,1,0:T(8,128)(2,1)}, u32[]{:S(2)}, u32[]{:S(2)}) async-start(bf16[32,704,128]{2,1,0:T(8,128)(2,1)} %get-tuple-element.148), calls=%async_computation.1 | async-start | bytes 11534336 | tf_op jit(solution)/shard_map/all_to_all | solution.py:177
  194.4 3.5 %multiply_subtract_fusion = (f32[251,1024]{1,0:T(8,128)}, f32[251,1024]{1,0:T(8,128)}, f32[251,1024]{1,0:T(8,128)}) fusion(f32[251,1024]{1,0:T(8,128)S(1)} %copy-done.1, bf16[251,1024]{1,0:T(8,128)(2,1)} %param.32, f32[251,1024]{1,0:T(8,128)S(1)} %copy-done.2, f32[251,1024]{1,0:T(8,128)} %param.33), kind=kLoop, calls=%fused_computation.67 | loop fusion | flops 3598336 | bytes 6682624 | tf_op jit(solution)/shard_map/sub | solution.py:50
  198.1 0.7 fusion.51
  198.8 0.7 multiply_subtract_fusion.1
  199.7 0.6 multiply_subtract_fusion.2
  200.3 65.4 %all-to-all-done.1 = bf16[32,704,128]{2,1,0:T(8,128)(2,1)} async-done(((bf16[32,704,128]{2,1,0:T(8,128)(2,1)}), bf16[32,704,128]{2,1,0:T(8,128)(2,1)}, u32[]{:S(2)}, u32[]{:S(2)}) %all-to-all-start.1) | async-done | bytes 5767200 | tf_op jit(solution)/shard_map/all_to_all | solution.py:177
  265.7 2.1 convert_multiply_fusion
  267.8 1.8 slice_bitcast_fusion
  269.5 1.2 slice_bitcast_fusion.1
  270.7 1.5 convert_multiply_fusion.1
  272.2 1.8 copy.100
  (62 shorter events, 4.0 us)
Async XLA Ops:
  11.1 3.9 %copy-start.3 = (bf16[4,704,128]{2,1,0:T(8,128)(2,1)S(1)}, bf16[4,704,128]{2,1,0:T(8,128)(2,1)}, u32[]{:S(2)}) copy-start(bf16[4,704,128]{2,1,0:T(8,128)(2,1)} %param.26) | copy-start | bytes 2162692
  11.2 3.8 %copy-start.4 = (bf16[4,704,128]{2,1,0:T(8,128)(2,1)S(1)}, bf16[4,704,128]{2,1,0:T(8,128)(2,1)}, u32[]{:S(2)}) copy-start(bf16[4,704,128]{2,1,0:T(8,128)(2,1)} %param.29) | copy-start | bytes 2162692
  20.1 8.7 %copy-start.9 = (f32[1,32,16]{1,2,0:T(8,128)S(1)}, f32[1,32,16]{1,2,0:T(8,128)}, u32[]{:S(2)}) copy-start(f32[1,32,16]{1,2,0:T(8,128)} %param.40) | copy-start | bytes 6148
  20.1 9.6 %copy-start.8 = (f32[4,1,2048]{2,1,0:T(1,128)S(1)}, f32[4,1,2048]{2,1,0:T(1,128)}, u32[]{:S(2)}) copy-start(f32[4,1,2048]{2,1,0:T(1,128)} %param.36) | copy-start | bytes 98308
  20.1 88.6 %all-to-all-start = ((bf16[32,704,128]{2,1,0:T(8,128)(2,1)}), bf16[32,704,128]{2,1,0:T(8,128)(2,1)}, u32[]{:S(2)}, u32[]{:S(2)}) async-start(bf16[32,704,128]{2,1,0:T(8,128)(2,1)} %fusion.38), calls=%async_computation | async-start | bytes 11534336 | tf_op jit(solution)/shard_map/all_to_all | solution.py:139
  28.8 80.7 %copy-start.15 = (s32[32]{0:T(128)S(1)}, s32[32]{0:T(128)}, u32[]{:S(2)}) copy-start(s32[32]{0:T(128)} %constant.45.clone) | copy-start | bytes 388
  28.8 81.3 %copy-start.14 = (s32[32]{0:T(128)S(1)}, s32[32]{0:T(128)}, u32[]{:S(2)}) copy-start(s32[32]{0:T(128)} %constant.102.clone) | copy-start | bytes 388
  28.8 78.0 %all-gather.8.cloned.1.call-start = ((), (), s32[]{:S(2)}) async-start(), calls=%async_computation.3 | async-start | bytes 1165824 | tf_op jit(solution)/shard_map/all_gather | solution.py:126
  30.5 156.6 %all-gather.6.cloned.1.call-start = ((), (), s32[]{:S(2)}) async-start(), calls=%async_computation.2 | async-start | bytes 1310720 | tf_op jit(solution)/shard_map/all_gather | solution.py:144
  126.9 2.5 copy-start
  188.8 5.4 %copy-start.1 = (f32[251,1024]{1,0:T(8,128)S(1)}, f32[251,1024]{1,0:T(8,128)}, u32[]{:S(2)}) copy-start(f32[251,1024]{1,0:T(8,128)} %param.31) | copy-start | bytes 3084292
  188.9 5.4 %copy-start.2 = (f32[251,1024]{1,0:T(8,128)S(1)}, f32[251,1024]{1,0:T(8,128)}, u32[]{:S(2)}) copy-start(f32[251,1024]{1,0:T(8,128)} %param.34) | copy-start | bytes 3084292
  188.9 76.8 %all-to-all-start.1 = ((bf16[32,704,128]{2,1,0:T(8,128)(2,1)}), bf16[32,704,128]{2,1,0:T(8,128)(2,1)}, u32[]{:S(2)}, u32[]{:S(2)}) async-start(bf16[32,704,128]{2,1,0:T(8,128)(2,1)} %get-tuple-element.148), calls=%async_computation.1 | async-start | bytes 11534336 | tf_op jit(solution)/shard_map/all_to_all | solution.py:177
  194.3 3.8 %copy-start.13 = (s32[4,7]{1,0:T(4,128)S(1)}, s32[4,7]{1,0:T(4,128)}, u32[]{:S(2)}) copy-start(s32[4,7]{1,0:T(4,128)} %param.30) | copy-start | bytes 340
  194.3 4.5 %copy-start.5 = (f32[4,2048]{1,0:T(4,128)S(1)}, f32[4,2048]{1,0:T(4,128)}, u32[]{:S(2)}) copy-start(f32[4,2048]{1,0:T(4,128)} %param.35) | copy-start | bytes 98308
  194.3 4.5 %copy-start.6 = (f32[4,2048]{1,0:T(4,128)S(1)}, f32[4,2048]{1,0:T(4,128)}, u32[]{:S(2)}) copy-start(f32[4,2048]{1,0:T(4,128)} %param.38) | copy-start | bytes 98308
  194.3 4.5 %copy-start.7 = (f32[4,2048]{1,0:T(4,128)S(1)}, f32[4,2048]{1,0:T(4,128)}, u32[]{:S(2)}) copy-start(f32[4,2048]{1,0:T(4,128)} %param.37) | copy-start | bytes 98308
  194.3 5.3 %copy-start.10 = (f32[32,16]{0,1:T(8,128)S(1)}, f32[32,16]{0,1:T(8,128)}, u32[]{:S(2)}) copy-start(f32[32,16]{0,1:T(8,128)} %param.39) | copy-start | bytes 6148
  194.4 5.3 %copy-start.11 = (f32[32,16]{0,1:T(8,128)S(1)}, f32[32,16]{0,1:T(8,128)}, u32[]{:S(2)}) copy-start(f32[32,16]{0,1:T(8,128)} %param.42) | copy-start | bytes 6148
  194.4 5.3 %copy-start.12 = (f32[32,16]{0,1:T(8,128)S(1)}, f32[32,16]{0,1:T(8,128)}, u32[]{:S(2)}) copy-start(f32[32,16]{0,1:T(8,128)} %param.41) | copy-start | bytes 6148
Sparse Core Ops, SparseCore 0:
  32.5 74.2 all-gather.7
  109.6 24.1 all-gather.5

commit v7 on v5

--- a/solution.py
+++ b/solution.py
@@ -97,8 +97,6 @@
     n_rect = layers_here * 3
     kind_list, index_list = block_plan(shards_count, tensor_count, n_square, n_rect)
     assert sum(k == 1 for k in kind_list) == n_square and sum(k == 2 for k in kind_list) == n_rect
-    kind_table = jnp.array(kind_list, jnp.int32)
-    index_table = jnp.array(index_list, jnp.int32)
     square_home = [0] * n_square
     rect_home = [0] * n_rect
     for device, (k, i) in enumerate(zip(kind_list, index_list)):
@@ -160,18 +158,7 @@
         )
         return jnp.pad(back, ((0, 0), (0, ff_block - width), (0, 0)))
 
-    my_kind = kind_table[my_index]
-
-    def square_branch(arrived_blocks):
-        return run(arrived_blocks, cols_block)
-
-    def rect_branch(arrived_blocks):
-        return run(arrived_blocks, ff_block)
-
-    def idle_branch(arrived_blocks):
-        return jnp.zeros((group_count, ff_block, rows_block), jnp.bfloat16)
-
-    returning = lax.switch(my_kind, [idle_branch, square_branch, rect_branch], incoming)
+    returning = run(incoming, ff_block)
     returning, gathered = lax.optimization_barrier((returning, gathered))
     arrived = lax.all_to_all(returning, ("shards", "tensor"), split_axis=0, concat_axis=0, tiled=True)
 

time: 283 us -> 295 us (1.042); the launches traced: 278 us -> 294 us
  waiting for transfers between devices: 134 us -> 151 us
  loops' own time: 6.46 us -> 0 us
  matrix products: 49.1 us -> 55.2 us
    all_gather x1, waiting for transfers between devices: 0.02 us -> 17 us  [on_device(): lax.all_gather(packed, ('shards', 'tensor'), axis=0, tiled=False)]
    unnamed x31 -> x30, local copies, waits for them, and re-layouts: 2.61 us -> 9.27 us
    cond x3 -> x0, local copies, waits for them, and re-layouts: 6.56 us -> none
    another operation x1 -> x0, loops' own time: 6.46 us -> none  [on_device(): lax.switch(my_kind, [idle_branch, square_branch, rect_branch], incoming)]
    dot_general x2, matrix products: 32.3 us -> 36.9 us  [newton_schulz_transposed(): lax.dot_general(current, polynomial, (((1,), (1,)), ((), ())), preferred_...]
    div x1 -> x0, local copies, waits for them, and re-layouts: 3.71 us -> none  [newton_schulz_transposed(): current = (as_f32 / (norm_value + 1e-07)).astype(jnp.bfloat16)]
    convert_element_type x0 -> x1, local copies, waits for them, and re-layouts: none -> 3.71 us  [newton_schulz_transposed(): current = (as_f32 / (norm_value + 1e-07)).astype(jnp.bfloat16)]
    transpose x2 -> x1, local copies, waits for them, and re-layouts: 4.28 us -> 0.65 us  [on_device(): jnp.swapaxes(attn_ahead, 2, 3).reshape(n_square, cols_block, rows_block)]
  transfers between devices with their start and end apart: 4 -> 4, of which waited for: 3 -> 4; matrix products, arithmetic and copies ran while one was open for 29% -> 12% of each run, Pallas kernels for 0% -> 0%
where the time goes in v7:
time: 295 us; the launch traced here: 294 us
  waiting for transfers between devices  151 us (51%)
  matrix products  55.2 us (19%)
  other arithmetic  35 us (12%)
  local copies, waits for them, and re-layouts  23.6 us (8%)
  between operations  15 us (5%)
  starting transfers between devices  14.9 us (5%)
    all_to_all x1, waiting for transfers between devices, on_device(): lax.all_to_all(returning, ('shards', 'tensor'), split_axis=0, concat_axis...  65.7 us
    all_to_all x1, waiting for transfers between devices, on_device(): lax.all_to_all(outgoing, ('shards', 'tensor'), split_axis=0, concat_axis=...  41.2 us
    dot_general x2, matrix products, newton_schulz_transposed(): lax.dot_general(current, polynomial, (((1,), (1,)), ((), ())), preferred_...  36.9 us
    all_gather x1, waiting for transfers between devices, on_device(): lax.all_gather(jnp.pad(bias_flat, (0, 65536 - bias_flat.shape[0])), 'sect...  26.7 us
    dot_general x2, matrix products, newton_schulz_transposed(): lax.dot_general(current, current, (((0,), (0,)), ((), ())), preferred_ele...  18.3 us
    all_gather x1, waiting for transfers between devices, on_device(): lax.all_gather(packed, ('shards', 'tensor'), axis=0, tiled=False)  17 us
    unnamed x30, local copies, waits for them, and re-layouts  9.27 us
    all_to_all x1, starting transfers between devices, on_device(): lax.all_to_all(outgoing, ('shards', 'tensor'), split_axis=0, concat_axis=...  8.65 us
  transfers between devices with their start and end apart: 4, of which 4 were waited for; matrix products, arithmetic and copies ran while one was open for 12% of the time, Pallas kernels for 0%

profile of v7, /device:TPU:2, one launch (start us, length us, event | category | flops | bytes accessed | tf_op | source)
XLA Modules:
  0.0 294.4 jit_solution(5345478219415925891)
XLA Ops:
  7.2 3.3 %multiply_reduce_fusion.1 = (f32[4,4]{1,0:T(4,128)S(1)}, bf16[4,4,256,128]{2,3,1,0:T(8,128)(2,1)S(1)}, bf16[4,4,128,256]{3,2,1,0:T(8,128)(2,1)}) fusion(bf16[4,4,128,256]{3,2,1,0:T(8,128)(2,1)} %param.19, bf16[4,4,128,256]{3,2,1,0:T(8,128)(2,1)} %param.22), kind=kLoop, calls=%fused_computation.35 | loop fusion | flops 6291440 | bytes 4194368 | tf_op jit(solution)/shard_map/reduce_sum | solution.py:116
  10.5 0.7 copy.79
  11.1 3.7 %fusion.20 = (bf16[4,2,704,128]{3,2,1,0:T(8,128)(2,1)S(1)}, bf16[4,2,128,704]{2,3,1,0:T(8,128)(2,1)}) fusion(bf16[4,2,128,704]{2,3,1,0:T(8,128)(2,1)} %param.20, bf16[4,2,128,704]{2,3,1,0:T(8,128)(2,1)} %param.23), kind=kLoop, calls=%fused_computation.41 | loop fusion | flops 6488064 | bytes 5767168 | tf_op jit(solution)/shard_map/transpose | solution.py:113
  14.9 2.6 fusion.24
  17.7 3.6 %fusion.5 = bf16[32,704,128]{2,1,0:T(8,128)(2,1)} fusion(bf16[16,256,128]{2,1,0:T(8,128)(2,1)S(1)} %bitcast.54, bf16[12,704,128]{2,1,0:T(8,128)(2,1)S(1)} %bitcast.50, bf16[32]{0:T(256)(128)(2,1)S(1)} %pad.19.clone), kind=kLoop, calls=%fused_computation.11 | loop fusion | flops 28835840 | bytes 8978496 | tf_op jit(solution)/shard_map/concatenate | solution.py:128
  21.3 8.6 %all-to-all-start = ((bf16[32,704,128]{2,1,0:T(8,128)(2,1)}), bf16[32,704,128]{2,1,0:T(8,128)(2,1)}, u32[]{:S(2)}, u32[]{:S(2)}) async-start(bf16[32,704,128]{2,1,0:T(8,128)(2,1)} %fusion.5), calls=%async_computation | async-start | bytes 11534336 | tf_op jit(solution)/shard_map/all_to_all | solution.py:135
  30.2 0.7 pad.12
  31.7 26.7 %all-gather.6.cloned.1.call-done = f32[262144]{0:T(1024)} async-done(((f32[65536]{0:T(1024)}), f32[262144]{0:T(1024)}) %all-gather.6.cloned.1.call-update) | async-done | bytes 1048592 | tf_op jit(solution)/shard_map/all_gather | solution.py:122
  58.4 1.7 reshape.120
  60.1 41.2 %all-to-all-done = bf16[32,704,128]{2,1,0:T(8,128)(2,1)} async-done(((bf16[32,704,128]{2,1,0:T(8,128)(2,1)}), bf16[32,704,128]{2,1,0:T(8,128)(2,1)}, u32[]{:S(2)}, u32[]{:S(2)}) %all-to-all-start) | async-done | bytes 5767200 | tf_op jit(solution)/shard_map/all_to_all | solution.py:135
  101.4 6.2 %fusion = f32[]{:T(128)} fusion(bf16[32,704,128]{2,1,0:T(8,128)(2,1)} %all-to-all-done), kind=kLoop, calls=%fused_computation.4 | loop fusion | flops 8650751 | bytes 5767172 | tf_op jit(solution)/shard_map/reduce_sum | solution.py:20
  108.3 4.2 %fusion.1 = bf16[32,704,128]{2,1,0:T(8,128)(2,1)S(1)} fusion(bf16[32,704,128]{2,1,0:T(8,128)(2,1)} %all-to-all-done, f32[]{:T(128)S(6)} %add.93), kind=kLoop, calls=%fused_computation.5 | loop fusion | flops 8650752 | bytes 11534340 | tf_op jit(solution)/shard_map/convert.1
  112.5 3.7 %copy.80 = bf16[4,704,8,128]{3,2,1,0:T(8,128)(2,1)S(1)} copy(bf16[4,704,8,128]{3,1,0,2:T(8,128)(2,1)S(1)} %bitcast.46) | data formatting | bytes 11534336 | tf_op jit(solution)/shard_map/convert_element_type | solution.py:21
  116.2 2.5 copy-done
  118.7 7.4 %fusion.6 = bf16[1024,1024]{1,0:T(8,128)(2,1)} fusion(bf16[352,8,8,128]{3,2,1,0:T(8,128)(2,1)S(1)} %bitcast.52), kind=kOutput, calls=%fused_computation.12 | convolution fusion | flops 5905580032 | bytes 7864320 | tf_op jit(solution)/shard_map/dot_general | solution.py:23
  126.1 19.3 %add_convert_fusion.1 = bf16[2816,1024]{1,0:T(8,128)(2,1)} fusion(bf16[352,8,8,128]{3,2,1,0:T(8,128)(2,1)} %bitcast.53, bf16[1024,1024]{1,0:T(8,128)(2,1)} %fusion.6), kind=kOutput, calls=%fused_computation.7 | convolution fusion | flops 8069840896 | bytes 13631488 | tf_op jit(solution)/shard_map/dot_general | solution.py:32
  145.5 10.9 %fusion.44 = bf16[1024,1024]{1,0:T(8,128)(2,1)} fusion(bf16[2816,1024]{1,0:T(8,128)(2,1)} %add_convert_fusion.1), kind=kOutput, calls=%fused_computation.66 | convolution fusion | flops 5905580032 | bytes 7864320 | tf_op jit(solution)/shard_map/dot_general | solution.py:23
  157.1 17.5 %fusion.13 = bf16[352,8,8,128]{3,1,2,0:T(8,128)(2,1)} fusion(bf16[2816,1024]{1,0:T(8,128)(2,1)} %add_convert_fusion.1, bf16[1024,1024]{1,0:T(8,128)(2,1)} %fusion.44), kind=kOutput, calls=%fused_computation.28 | convolution fusion | flops 8069840896 | bytes 13631488 | tf_op jit(solution)/shard_map/dot_general | solution.py:32
  174.7 4.1 %copy.87 = bf16[352,8,8,128]{3,2,1,0:T(8,128)(2,1)S(1)} copy(bf16[352,8,8,128]{3,1,2,0:T(8,128)(2,1)} %fusion.13) | data formatting | bytes 11534336
  178.8 3.8 %copy.81 = bf16[4,704,8,128]{3,1,0,2:T(8,128)(2,1)} copy(bf16[4,704,8,128]{3,2,1,0:T(8,128)(2,1)S(1)} %bitcast.47) | data formatting | bytes 11534336 | tf_op jit(solution)/shard_map/reshape | solution.py:155
  182.6 17.0 %all-gather.8.cloned.1.call-done = f32[32,1,8832]{2,1,0:T(1,128)} async-done(((f32[1,1,8832]{2,1,0:T(1,128)}), f32[32,1,8832]{2,1,0:T(1,128)}) %all-gather.8.cloned.1.call-update) | async-done | bytes 1130512 | tf_op jit(solution)/shard_map/all_gather | solution.py:144
  199.7 1.9 reduce_sum.64
  201.6 6.2 %all-to-all-start.1 = ((bf16[32,704,128]{2,1,0:T(8,128)(2,1)}), bf16[32,704,128]{2,1,0:T(8,128)(2,1)}, u32[]{:S(2)}, u32[]{:S(2)}) async-start(bf16[32,704,128]{2,1,0:T(8,128)(2,1)} %bitcast.45), calls=%async_computation.1 | async-start | bytes 11534336 | tf_op jit(solution)/shard_map/all_to_all | solution.py:163
  207.9 3.2 %multiply_subtract_fusion = (f32[251,1024]{1,0:T(8,128)}, f32[251,1024]{1,0:T(8,128)}, f32[251,1024]{1,0:T(8,128)}) fusion(f32[251,1024]{1,0:T(8,128)S(1)} %copy-done.1, bf16[251,1024]{1,0:T(8,128)(2,1)} %param.27, f32[251,1024]{1,0:T(8,128)S(1)} %copy-done.2, f32[251,1024]{1,0:T(8,128)S(1)} %copy-done.3), kind=kLoop, calls=%fused_computation.47 | loop fusion | flops 3598336 | bytes 6682624 | tf_op jit(solution)/shard_map/sub | solution.py:52
  211.6 0.7 fusion.31
  212.9 0.7 multiply_subtract_fusion.1
  213.6 65.7 %all-to-all-done.1 = bf16[32,704,128]{2,1,0:T(8,128)(2,1)} async-done(((bf16[32,704,128]{2,1,0:T(8,128)(2,1)}), bf16[32,704,128]{2,1,0:T(8,128)(2,1)}, u32[]{:S(2)}, u32[]{:S(2)}) %all-to-all-start.1) | async-done | bytes 5767200 | tf_op jit(solution)/shard_map/all_to_all | solution.py:163
  279.2 2.1 convert_multiply_fusion.1
  281.3 1.8 slice_bitcast_fusion
  283.1 1.2 slice_bitcast_fusion.1
  284.3 1.5 convert_multiply_fusion.2
  285.7 1.8 copy.85
  (51 shorter events, 3.1 us)
Async XLA Ops:
  21.3 8.7 %copy-start.8 = (f32[1,32,16]{1,2,0:T(8,128)S(1)}, f32[1,32,16]{1,2,0:T(8,128)}, u32[]{:S(2)}) copy-start(f32[1,32,16]{1,2,0:T(8,128)} %param.35) | copy-start | bytes 6148
  21.3 80.1 %all-to-all-start = ((bf16[32,704,128]{2,1,0:T(8,128)(2,1)}), bf16[32,704,128]{2,1,0:T(8,128)(2,1)}, u32[]{:S(2)}, u32[]{:S(2)}) async-start(bf16[32,704,128]{2,1,0:T(8,128)(2,1)} %fusion.5), calls=%async_computation | async-start | bytes 11534336 | tf_op jit(solution)/shard_map/all_to_all | solution.py:135
  29.9 28.5 %all-gather.6.cloned.1.call-start = ((), (), s32[]{:S(2)}) async-start(), calls=%async_computation.2 | async-start | bytes 1310720 | tf_op jit(solution)/shard_map/all_gather | solution.py:122
  30.9 168.8 %all-gather.8.cloned.1.call-start = ((), (), s32[]{:S(2)}) async-start(), calls=%async_computation.3 | async-start | bytes 1165824 | tf_op jit(solution)/shard_map/all_gather | solution.py:144
  116.2 2.5 copy-start
  145.5 10.9 %copy-start.7 = (f32[4,1,2048]{2,1,0:T(1,128)S(1)}, f32[4,1,2048]{2,1,0:T(1,128)}, u32[]{:S(2)}) copy-start(f32[4,1,2048]{2,1,0:T(1,128)} %param.31) | copy-start | bytes 98308
  201.6 6.3 %copy-start.1 = (f32[251,1024]{1,0:T(8,128)S(1)}, f32[251,1024]{1,0:T(8,128)}, u32[]{:S(2)}) copy-start(f32[251,1024]{1,0:T(8,128)} %param.26) | copy-start | bytes 3084292
  201.6 6.3 %copy-start.2 = (f32[251,1024]{1,0:T(8,128)S(1)}, f32[251,1024]{1,0:T(8,128)}, u32[]{:S(2)}) copy-start(f32[251,1024]{1,0:T(8,128)} %param.29) | copy-start | bytes 3084292
  201.6 6.3 %copy-start.3 = (f32[251,1024]{1,0:T(8,128)S(1)}, f32[251,1024]{1,0:T(8,128)}, u32[]{:S(2)}) copy-start(f32[251,1024]{1,0:T(8,128)} %param.28) | copy-start | bytes 3084292
  201.6 77.6 %all-to-all-start.1 = ((bf16[32,704,128]{2,1,0:T(8,128)(2,1)}), bf16[32,704,128]{2,1,0:T(8,128)(2,1)}, u32[]{:S(2)}, u32[]{:S(2)}) async-start(bf16[32,704,128]{2,1,0:T(8,128)(2,1)} %bitcast.45), calls=%async_computation.1 | async-start | bytes 11534336 | tf_op jit(solution)/shard_map/all_to_all | solution.py:163
  207.8 3.7 %copy-start.12 = (s32[4,7]{1,0:T(4,128)S(1)}, s32[4,7]{1,0:T(4,128)}, u32[]{:S(2)}) copy-start(s32[4,7]{1,0:T(4,128)} %param.25) | copy-start | bytes 340
  207.8 4.4 %copy-start.9 = (f32[32,16]{0,1:T(8,128)S(1)}, f32[32,16]{0,1:T(8,128)}, u32[]{:S(2)}) copy-start(f32[32,16]{0,1:T(8,128)} %param.34) | copy-start | bytes 6148
  207.8 4.4 %copy-start.10 = (f32[32,16]{0,1:T(8,128)S(1)}, f32[32,16]{0,1:T(8,128)}, u32[]{:S(2)}) copy-start(f32[32,16]{0,1:T(8,128)} %param.37) | copy-start | bytes 6148
  207.9 4.4 %copy-start.11 = (f32[32,16]{0,1:T(8,128)S(1)}, f32[32,16]{0,1:T(8,128)}, u32[]{:S(2)}) copy-start(f32[32,16]{0,1:T(8,128)} %param.36) | copy-start | bytes 6148
  207.9 5.0 %copy-start.4 = (f32[4,2048]{1,0:T(4,128)S(1)}, f32[4,2048]{1,0:T(4,128)}, u32[]{:S(2)}) copy-start(f32[4,2048]{1,0:T(4,128)} %param.30) | copy-start | bytes 98308
  207.9 5.0 %copy-start.5 = (f32[4,2048]{1,0:T(4,128)S(1)}, f32[4,2048]{1,0:T(4,128)}, u32[]{:S(2)}) copy-start(f32[4,2048]{1,0:T(4,128)} %param.33) | copy-start | bytes 98308
  207.9 5.0 %copy-start.6 = (f32[4,2048]{1,0:T(4,128)S(1)}, f32[4,2048]{1,0:T(4,128)}, u32[]{:S(2)}) copy-start(f32[4,2048]{1,0:T(4,128)} %param.32) | copy-start | bytes 98308
Sparse Core Ops, SparseCore 0:
  33.0 25.3 all-gather.5
  157.2 42.4 all-gather.7

commit v8 on v5

--- a/solution.py
+++ b/solution.py
@@ -143,7 +143,7 @@
     bias_width = bias_sections.shape[0]
     packed = jnp.concatenate([norm_partial_late.reshape(norm_width), bias_sections, square_ss, rect_ss])
     packed = jnp.pad(packed, (0, (-packed.shape[0]) % 128))
-    gathered = jnp.sum(lax.all_gather(packed, ("shards", "tensor"), axis=0, tiled=False), axis=0)
+    gathered_all = lax.all_gather(packed, ("shards", "tensor"), axis=0, tiled=False)
 
     def run(arrived_blocks, width):
         whole = (
@@ -172,9 +172,10 @@
         return jnp.zeros((group_count, ff_block, rows_block), jnp.bfloat16)
 
     returning = lax.switch(my_kind, [idle_branch, square_branch, rect_branch], incoming)
-    returning, gathered = lax.optimization_barrier((returning, gathered))
+    returning, gathered_all = lax.optimization_barrier((returning, gathered_all))
     arrived = lax.all_to_all(returning, ("shards", "tensor"), split_axis=0, concat_axis=0, tiled=True)
 
+    gathered = jnp.sum(gathered_all, axis=0)
     norm_grad = gathered[:norm_width].reshape(norm_partial.shape[0], norm_partial.shape[2])
     ss_start = norm_width + bias_width
     square_norm = jnp.sqrt(gathered[ss_start : ss_start + n_square])

time: 283 us -> 282 us (level)
  no operation moved by 1% of the time
where the time goes in v8:
time: 282 us; the launch traced here: 277 us
  waiting for transfers between devices  133 us (47%)
  matrix products  49.1 us (17%)
  other arithmetic  33.5 us (12%)
  local copies, waits for them, and re-layouts  25.9 us (9%)
  between operations  15.2 us (5%)
  starting transfers between devices  13.7 us (5%)
  loops' own time  6.46 us (2%)
    all_to_all x1, waiting for transfers between devices, on_device(): lax.all_to_all(returning, ('shards', 'tensor'), split_axis=0, concat_axis...  65.2 us
    all_to_all x1, waiting for transfers between devices, on_device(): lax.all_to_all(outgoing, ('shards', 'tensor'), split_axis=0, concat_axis=...  41.2 us
    dot_general x2, matrix products, newton_schulz_transposed(): lax.dot_general(current, polynomial, (((1,), (1,)), ((), ())), preferred_...  32.3 us
    all_gather x1, waiting for transfers between devices, on_device(): lax.all_gather(jnp.pad(bias_flat, (0, 65536 - bias_flat.shape[0])), 'sect...  26.7 us
    dot_general x2, matrix products, newton_schulz_transposed(): lax.dot_general(current, current, (((0,), (0,)), ((), ())), preferred_ele...  16.7 us
    all_to_all x1, starting transfers between devices, on_device(): lax.all_to_all(outgoing, ('shards', 'tensor'), split_axis=0, concat_axis=...  8.65 us
    cond x3, local copies, waits for them, and re-layouts  6.57 us
    another operation x1, loops' own time, on_device(): lax.switch(my_kind, [idle_branch, square_branch, rect_branch], incoming)  6.46 us
  transfers between devices with their start and end apart: 4, of which 3 were waited for; matrix products, arithmetic and copies ran while one was open for 29% of the time, Pallas kernels for 0%

profile of v8, /device:TPU:2, one launch (start us, length us, event | category | flops | bytes accessed | tf_op | source)
XLA Modules:
  0.0 276.9 jit_solution(5399345326253699425)
XLA Ops:
  7.2 3.4 %multiply_reduce_fusion.1 = (f32[4,4]{1,0:T(4,128)S(1)}, bf16[4,4,128,256]{3,2,1,0:T(8,128)(2,1)S(1)}, bf16[4,4,128,256]{3,2,1,0:T(8,128)(2,1)}) fusion(bf16[4,4,128,256]{3,2,1,0:T(8,128)(2,1)} %param.23, bf16[4,4,128,256]{3,2,1,0:T(8,128)(2,1)} %param.26), kind=kLoop, calls=%fused_computation.62 | loop fusion | flops 6291440 | bytes 4194368 | tf_op jit(solution)/shard_map/reduce_sum | solution.py:118
  10.6 0.7 copy.95
  11.3 2.3 fusion.52
  13.7 3.7 %fusion.49 = (bf16[4,2,704,128]{3,2,1,0:T(8,128)(2,1)S(1)}, bf16[4,2,128,704]{2,3,1,0:T(8,128)(2,1)}) fusion(bf16[4,2,128,704]{2,3,1,0:T(8,128)(2,1)} %param.24, bf16[4,2,128,704]{2,3,1,0:T(8,128)(2,1)} %param.27), kind=kLoop, calls=%fused_computation.68 | loop fusion | flops 6488064 | bytes 5767168 | tf_op jit(solution)/shard_map/transpose | solution.py:115
  17.6 3.6 %fusion.42 = bf16[32,704,128]{2,1,0:T(8,128)(2,1)} fusion(bf16[16,256,128]{2,1,0:T(8,128)(2,1)S(1)} %copy.95, bf16[12,704,128]{2,1,0:T(8,128)(2,1)S(1)} %bitcast.83, bf16[32]{0:T(256)(128)(2,1)S(1)} %pad.23.clone), kind=kLoop, calls=%fused_computation.48 | loop fusion | flops 28835840 | bytes 8978496 | tf_op jit(solution)/shard_map/concatenate | solution.py:130
  21.2 8.6 %all-to-all-start = ((bf16[32,704,128]{2,1,0:T(8,128)(2,1)}), bf16[32,704,128]{2,1,0:T(8,128)(2,1)}, u32[]{:S(2)}, u32[]{:S(2)}) async-start(bf16[32,704,128]{2,1,0:T(8,128)(2,1)} %fusion.42), calls=%async_computation | async-start | bytes 11534336 | tf_op jit(solution)/shard_map/all_to_all | solution.py:137
  30.1 0.7 pad.16
  31.6 26.7 %all-gather.6.cloned.1.call-done = f32[262144]{0:T(1024)} async-done(((f32[65536]{0:T(1024)}), f32[262144]{0:T(1024)}) %all-gather.6.cloned.1.call-update) | async-done | bytes 1048592 | tf_op jit(solution)/shard_map/all_gather | solution.py:124
  58.3 1.7 reshape.144
  60.1 41.2 %all-to-all-done = bf16[32,704,128]{2,1,0:T(8,128)(2,1)} async-done(((bf16[32,704,128]{2,1,0:T(8,128)(2,1)}), bf16[32,704,128]{2,1,0:T(8,128)(2,1)}, u32[]{:S(2)}, u32[]{:S(2)}) %all-to-all-start) | async-done | bytes 5767200 | tf_op jit(solution)/shard_map/all_to_all | solution.py:137
  103.3 80.5 %conditional.1 = (bf16[32,704,128]{2,1,0:T(8,128)(2,1)}) conditional(s32[]{:T(128)} %bitcast.8, () %tuple.19, bf16[32,704,128]{2,1,0:T(8,128)(2,1)} %all-to-all-done, bf16[32,704,128]{2,1,0:T(8,128)(2,1)} %all-to-all-done), branch_computations={%region_3.4_spmd, %region_4.6_spmd, %region_6.8_spmd} | conditional | flops 27968143360 | bytes 129499200 | solution.py:174
  108.8 6.2 %fusion.21 = f32[]{:T(128)} fusion(bf16[32,704,128]{2,1,0:T(8,128)(2,1)} %param.2), kind=kLoop, calls=%fused_computation.24 | loop fusion | flops 8650751 | bytes 5767172 | tf_op jit(solution)/shard_map/cond/branch_2_fun/reduce_sum | solution.py:20
  115.7 4.2 %fusion.22 = bf16[32,704,128]{2,1,0:T(8,128)(2,1)S(1)} fusion(bf16[32,704,128]{2,1,0:T(8,128)(2,1)} %param.2, f32[]{:T(128)S(6)} %add.73), kind=kLoop, calls=%fused_computation.25 | loop fusion | flops 8650752 | bytes 11534340 | tf_op jit(solution)/shard_map/convert.3
  119.9 3.7 %copy.91 = bf16[8,4,704,128]{3,0,2,1:T(8,128)(2,1)S(1)} copy(bf16[8,4,704,128]{3,2,1,0:T(8,128)(2,1)S(1)} %bitcast.79) | data formatting | bytes 11534336 | tf_op jit(solution)/shard_map/cond/branch_2_fun/div | solution.py:21
  123.7 2.4 copy-done
  126.1 6.8 %fusion.23 = bf16[1024,1024]{1,0:T(8,128)(2,1)S(1)} fusion(bf16[352,8,8,128]{3,2,1,0:T(8,128)(2,1)S(1)} %bitcast.88), kind=kOutput, calls=%fused_computation.29 | convolution fusion | flops 5905580032 | bytes 7864320 | tf_op jit(solution)/shard_map/cond/branch_2_fun/dot_general | solution.py:23
  132.9 17.7 %add_convert_fusion.5 = bf16[2816,1024]{1,0:T(8,128)(2,1)} fusion(bf16[352,8,8,128]{3,2,1,0:T(8,128)(2,1)} %bitcast.89, bf16[1024,1024]{1,0:T(8,128)(2,1)S(1)} %fusion.23), kind=kOutput, calls=%fused_computation.27 | convolution fusion | flops 8069840896 | bytes 13631488 | tf_op jit(solution)/shard_map/cond/branch_2_fun/dot_general | solution.py:32
  150.6 9.9 %fusion.67 = bf16[1024,1024]{1,0:T(8,128)(2,1)S(1)} fusion(bf16[2816,1024]{1,0:T(8,128)(2,1)} %add_convert_fusion.5), kind=kOutput, calls=%fused_computation.92 | convolution fusion | flops 5905580032 | bytes 7864320 | tf_op jit(solution)/shard_map/cond/branch_2_fun/dot_general | solution.py:23
  160.5 14.7 %fusion.28 = bf16[352,8,8,128]{3,1,2,0:T(8,128)(2,1)} fusion(bf16[2816,1024]{1,0:T(8,128)(2,1)} %add_convert_fusion.5, bf16[1024,1024]{1,0:T(8,128)(2,1)S(1)} %fusion.67), kind=kOutput, calls=%fused_computation.36 | convolution fusion | flops 8069840896 | bytes 13631488 | tf_op jit(solution)/shard_map/cond/branch_2_fun/dot_general | solution.py:32
  175.2 4.1 %copy.104 = bf16[352,8,8,128]{3,2,1,0:T(8,128)(2,1)S(1)} copy(bf16[352,8,8,128]{3,1,2,0:T(8,128)(2,1)} %fusion.28) | data formatting | bytes 11534336 | tf_op jit(solution)/shard_map/cond
  179.7 3.9 %copy.92 = bf16[8,4,704,128]{3,2,1,0:T(8,128)(2,1)} copy(bf16[8,4,704,128]{3,0,2,1:T(8,128)(2,1)S(1)} %bitcast_bitcast_fusion.1) | data formatting | bytes 11534336 | tf_op jit(solution)/shard_map/cond/branch_2_fun/transpose | solution.py:158
  183.8 1.3 copy.122
  185.2 4.9 %all-to-all-start.1 = ((bf16[32,704,128]{2,1,0:T(8,128)(2,1)}), bf16[32,704,128]{2,1,0:T(8,128)(2,1)}, u32[]{:S(2)}, u32[]{:S(2)}) async-start(bf16[32,704,128]{2,1,0:T(8,128)(2,1)} %get-tuple-element.132), calls=%async_computation.1 | async-start | bytes 11534336 | tf_op jit(solution)/shard_map/all_to_all | solution.py:176
  190.2 3.6 %multiply_subtract_fusion = (f32[251,1024]{1,0:T(8,128)}, f32[251,1024]{1,0:T(8,128)}, f32[251,1024]{1,0:T(8,128)}) fusion(f32[251,1024]{1,0:T(8,128)S(1)} %copy-done.1, bf16[251,1024]{1,0:T(8,128)(2,1)} %param.31, f32[251,1024]{1,0:T(8,128)S(1)} %copy-done.2, f32[251,1024]{1,0:T(8,128)} %param.32), kind=kLoop, calls=%fused_computation.74 | loop fusion | flops 3598336 | bytes 6682624 | tf_op jit(solution)/shard_map/sub | solution.py:52
  194.4 0.7 fusion.55
  195.7 0.7 multiply_subtract_fusion.1
  196.4 65.2 %all-to-all-done.1 = bf16[32,704,128]{2,1,0:T(8,128)(2,1)} async-done(((bf16[32,704,128]{2,1,0:T(8,128)(2,1)}), bf16[32,704,128]{2,1,0:T(8,128)(2,1)}, u32[]{:S(2)}, u32[]{:S(2)}) %all-to-all-start.1) | async-done | bytes 5767200 | tf_op jit(solution)/shard_map/all_to_all | solution.py:176
  261.5 2.1 convert_multiply_fusion.2
  263.6 1.2 slice_bitcast_fusion.1
  264.8 1.8 slice_bitcast_fusion
  266.6 1.5 convert_multiply_fusion.3
  268.0 1.8 copy.99
  (57 shorter events, 4.2 us)
Async XLA Ops:
  7.2 4.1 %copy-start.3 = (bf16[4,704,128]{2,1,0:T(8,128)(2,1)S(1)}, bf16[4,704,128]{2,1,0:T(8,128)(2,1)}, u32[]{:S(2)}) copy-start(bf16[4,704,128]{2,1,0:T(8,128)(2,1)} %param.25) | copy-start | bytes 2162692
  21.2 8.7 %copy-start.8 = (f32[1,32,16]{1,2,0:T(8,128)S(1)}, f32[1,32,16]{1,2,0:T(8,128)}, u32[]{:S(2)}) copy-start(f32[1,32,16]{1,2,0:T(8,128)} %param.39) | copy-start | bytes 6148
  21.2 80.1 %all-to-all-start = ((bf16[32,704,128]{2,1,0:T(8,128)(2,1)}), bf16[32,704,128]{2,1,0:T(8,128)(2,1)}, u32[]{:S(2)}, u32[]{:S(2)}) async-start(bf16[32,704,128]{2,1,0:T(8,128)(2,1)} %fusion.42), calls=%async_computation | async-start | bytes 11534336 | tf_op jit(solution)/shard_map/all_to_all | solution.py:137
  29.9 71.4 %copy-start.7 = (f32[4,1,2048]{2,1,0:T(1,128)S(1)}, f32[4,1,2048]{2,1,0:T(1,128)}, u32[]{:S(2)}) copy-start(f32[4,1,2048]{2,1,0:T(1,128)} %param.35) | copy-start | bytes 98308
  29.9 72.2 %copy-start.13 = (s32[32]{0:T(128)S(1)}, s32[32]{0:T(128)}, u32[]{:S(2)}) copy-start(s32[32]{0:T(128)} %constant.40.clone) | copy-start | bytes 388
  29.9 28.5 %all-gather.6.cloned.1.call-start = ((), (), s32[]{:S(2)}) async-start(), calls=%async_computation.2 | async-start | bytes 1310720 | tf_op jit(solution)/shard_map/all_gather | solution.py:124
  30.8 153.0 %all-gather.8.cloned.1.call-start = ((), (), s32[]{:S(2)}) async-start(), calls=%async_computation.3 | async-start | bytes 1165824 | tf_op jit(solution)/shard_map/all_gather | solution.py:146
  123.7 2.5 copy-start
  185.2 5.0 %copy-start.1 = (f32[251,1024]{1,0:T(8,128)S(1)}, f32[251,1024]{1,0:T(8,128)}, u32[]{:S(2)}) copy-start(f32[251,1024]{1,0:T(8,128)} %param.30) | copy-start | bytes 3084292
  185.2 5.0 %copy-start.2 = (f32[251,1024]{1,0:T(8,128)S(1)}, f32[251,1024]{1,0:T(8,128)}, u32[]{:S(2)}) copy-start(f32[251,1024]{1,0:T(8,128)} %param.33) | copy-start | bytes 3084292
  185.2 76.4 %all-to-all-start.1 = ((bf16[32,704,128]{2,1,0:T(8,128)(2,1)}), bf16[32,704,128]{2,1,0:T(8,128)(2,1)}, u32[]{:S(2)}, u32[]{:S(2)}) async-start(bf16[32,704,128]{2,1,0:T(8,128)(2,1)} %get-tuple-element.132), calls=%async_computation.1 | async-start | bytes 11534336 | tf_op jit(solution)/shard_map/all_to_all | solution.py:176
  190.1 4.2 %copy-start.12 = (s32[4,7]{1,0:T(4,128)S(1)}, s32[4,7]{1,0:T(4,128)}, u32[]{:S(2)}) copy-start(s32[4,7]{1,0:T(4,128)} %param.29) | copy-start | bytes 340
  190.2 4.9 %copy-start.9 = (f32[32,16]{0,1:T(8,128)S(1)}, f32[32,16]{0,1:T(8,128)}, u32[]{:S(2)}) copy-start(f32[32,16]{0,1:T(8,128)} %param.38) | copy-start | bytes 6148
  190.2 4.9 %copy-start.10 = (f32[32,16]{0,1:T(8,128)S(1)}, f32[32,16]{0,1:T(8,128)}, u32[]{:S(2)}) copy-start(f32[32,16]{0,1:T(8,128)} %param.41) | copy-start | bytes 6148
  190.2 4.9 %copy-start.11 = (f32[32,16]{0,1:T(8,128)S(1)}, f32[32,16]{0,1:T(8,128)}, u32[]{:S(2)}) copy-start(f32[32,16]{0,1:T(8,128)} %param.40) | copy-start | bytes 6148
  190.2 5.5 %copy-start.4 = (f32[4,2048]{1,0:T(4,128)S(1)}, f32[4,2048]{1,0:T(4,128)}, u32[]{:S(2)}) copy-start(f32[4,2048]{1,0:T(4,128)} %param.34) | copy-start | bytes 98308
  190.2 5.5 %copy-start.5 = (f32[4,2048]{1,0:T(4,128)S(1)}, f32[4,2048]{1,0:T(4,128)}, u32[]{:S(2)}) copy-start(f32[4,2048]{1,0:T(4,128)} %param.37) | copy-start | bytes 98308
  190.2 5.5 %copy-start.6 = (f32[4,2048]{1,0:T(4,128)S(1)}, f32[4,2048]{1,0:T(4,128)}, u32[]{:S(2)}) copy-start(f32[4,2048]{1,0:T(4,128)} %param.36) | copy-start | bytes 98308
Sparse Core Ops, SparseCore 0:
  32.9 25.3 all-gather.5
  102.1 42.4 all-gather.7

commit v9 on v8

--- a/solution.py
+++ b/solution.py
@@ -15,10 +15,8 @@
 coef_third = 2.0315
 
 
-def newton_schulz_transposed(rows_bf16):
-    as_f32 = rows_bf16.astype(jnp.float32)
-    norm_value = jnp.sqrt(jnp.sum(as_f32 * as_f32))
-    current = (as_f32 / (norm_value + 1e-07)).astype(jnp.bfloat16)
+def newton_schulz_transposed(rows_bf16, norm_value):
+    current = (rows_bf16.astype(jnp.float32) / (norm_value + 1e-07)).astype(jnp.bfloat16)
     for sweep_index in range(NS_STEPS):
         gram_form = lax.dot_general(
             current, current, (((0,), (0,)), ((), ())), preferred_element_type=jnp.float32
@@ -152,7 +150,9 @@
             .transpose(1, 2, 0, 3)
             .reshape(tensor_count * width, shards_count * rows_block)
         )
-        done = newton_schulz_transposed(whole)
+        block_sum = jnp.sum(jnp.square(arrived_blocks.astype(jnp.float32)), axis=0)
+        norm_value = jnp.sqrt(jnp.sum(lax.optimization_barrier(block_sum)))
+        done = newton_schulz_transposed(whole, norm_value)
         back = (
             done.reshape(tensor_count, width, shards_count, rows_block)
             .transpose(2, 0, 1, 3)

time: 282 us -> 280 us (level)
    reduce_sum x1 -> x2, other arithmetic: 6.21 us -> 4.48 us  [the longest x1 3.79 us: run(): block_sum = jnp.sum(jnp.square(arrived_blocks.astype(jnp.float32)), axis=0)]
where the time goes in v9:
time: 280 us; the launch traced here: 275 us
  waiting for transfers between devices  133 us (48%)
  matrix products  49.3 us (18%)
  other arithmetic  31.8 us (11%)
  local copies, waits for them, and re-layouts  25.9 us (9%)
  between operations  15.2 us (5%)
  starting transfers between devices  13.7 us (5%)
  loops' own time  6 us (2%)
    all_to_all x1, waiting for transfers between devices, on_device(): lax.all_to_all(returning, ('shards', 'tensor'), split_axis=0, concat_axis...  65.2 us
    all_to_all x1, waiting for transfers between devices, on_device(): lax.all_to_all(outgoing, ('shards', 'tensor'), split_axis=0, concat_axis=...  41.2 us
    dot_general x2, matrix products, newton_schulz_transposed(): lax.dot_general(current, polynomial, (((1,), (1,)), ((), ())), preferred_...  32.7 us
    all_gather x1, waiting for transfers between devices, on_device(): lax.all_gather(jnp.pad(bias_flat, (0, 65536 - bias_flat.shape[0])), 'sect...  26.7 us
    dot_general x2, matrix products, newton_schulz_transposed(): lax.dot_general(current, current, (((0,), (0,)), ((), ())), preferred_ele...  16.6 us
    all_to_all x1, starting transfers between devices, on_device(): lax.all_to_all(outgoing, ('shards', 'tensor'), split_axis=0, concat_axis=...  8.65 us
    cond x3, local copies, waits for them, and re-layouts  6.58 us
    another operation x1, loops' own time, on_device(): lax.switch(my_kind, [idle_branch, square_branch, rect_branch], incoming)  6 us
  transfers between devices with their start and end apart: 4, of which 3 were waited for; matrix products, arithmetic and copies ran while one was open for 29% of the time, Pallas kernels for 0%

profile of v9, /device:TPU:2, one launch (start us, length us, event | category | flops | bytes accessed | tf_op | source)
XLA Modules:
  0.0 274.9 jit_solution(10592992038355681385)
XLA Ops:
  7.2 3.4 %multiply_reduce_fusion.2 = (f32[4,4]{1,0:T(4,128)S(1)}, bf16[4,4,128,256]{3,2,1,0:T(8,128)(2,1)S(1)}, bf16[4,4,128,256]{3,2,1,0:T(8,128)(2,1)}) fusion(bf16[4,4,128,256]{3,2,1,0:T(8,128)(2,1)} %param.23, bf16[4,4,128,256]{3,2,1,0:T(8,128)(2,1)} %param.26), kind=kLoop, calls=%fused_computation.60 | loop fusion | flops 6291440 | bytes 4194368 | tf_op jit(solution)/shard_map/reduce_sum | solution.py:116
  11.3 2.3 fusion.50
  13.7 3.7 %fusion.47 = (bf16[4,2,704,128]{3,2,1,0:T(8,128)(2,1)S(1)}, bf16[4,2,128,704]{2,3,1,0:T(8,128)(2,1)}) fusion(bf16[4,2,128,704]{2,3,1,0:T(8,128)(2,1)} %param.24, bf16[4,2,128,704]{2,3,1,0:T(8,128)(2,1)} %param.27), kind=kLoop, calls=%fused_computation.66 | loop fusion | flops 6488064 | bytes 5767168 | tf_op jit(solution)/shard_map/transpose | solution.py:113
  17.6 3.6 %fusion.40 = bf16[32,704,128]{2,1,0:T(8,128)(2,1)} fusion(bf16[16,256,128]{2,1,0:T(8,128)(2,1)S(1)} %copy.95, bf16[12,704,128]{2,1,0:T(8,128)(2,1)S(1)} %bitcast.83, bf16[32]{0:T(256)(128)(2,1)S(1)} %pad.23.clone), kind=kLoop, calls=%fused_computation.46 | loop fusion | flops 28835840 | bytes 8978496 | tf_op jit(solution)/shard_map/concatenate | solution.py:128
  21.2 8.6 %all-to-all-start = ((bf16[32,704,128]{2,1,0:T(8,128)(2,1)}), bf16[32,704,128]{2,1,0:T(8,128)(2,1)}, u32[]{:S(2)}, u32[]{:S(2)}) async-start(bf16[32,704,128]{2,1,0:T(8,128)(2,1)} %fusion.40), calls=%async_computation | async-start | bytes 11534336 | tf_op jit(solution)/shard_map/all_to_all | solution.py:135
  30.1 0.7 pad.16
  31.6 26.7 %all-gather.6.cloned.1.call-done = f32[262144]{0:T(1024)} async-done(((f32[65536]{0:T(1024)}), f32[262144]{0:T(1024)}) %all-gather.6.cloned.1.call-update) | async-done | bytes 1048592 | tf_op jit(solution)/shard_map/all_gather | solution.py:122
  58.3 1.7 reshape.142
  60.1 41.2 %all-to-all-done = bf16[32,704,128]{2,1,0:T(8,128)(2,1)} async-done(((bf16[32,704,128]{2,1,0:T(8,128)(2,1)}), bf16[32,704,128]{2,1,0:T(8,128)(2,1)}, u32[]{:S(2)}, u32[]{:S(2)}) %all-to-all-start) | async-done | bytes 5767200 | tf_op jit(solution)/shard_map/all_to_all | solution.py:135
  103.3 78.6 %conditional.1 = (bf16[32,704,128]{2,1,0:T(8,128)(2,1)}) conditional(s32[]{:T(128)} %bitcast.8, () %tuple.19, bf16[32,704,128]{2,1,0:T(8,128)(2,1)} %all-to-all-done, bf16[32,704,128]{2,1,0:T(8,128)(2,1)} %all-to-all-done), branch_computations={%region_3.4_spmd, %region_4.7_spmd, %region_7.10_spmd} | conditional | flops 27968143360 | bytes 130220104 | solution.py:174
  108.4 3.8 %fusion.19 = f32[704,128]{1,0:T(8,128)S(1)} fusion(bf16[32,704,128]{2,1,0:T(8,128)(2,1)} %param.2), kind=kLoop, calls=%fused_computation.22 | loop fusion | flops 8560640 | bytes 6127616 | tf_op jit(solution)/shard_map/cond/branch_2_fun/reduce_sum | solution.py:153
  112.2 0.7 reduce_sum.77
  113.6 4.2 %fusion.20 = bf16[32,704,128]{2,1,0:T(8,128)(2,1)S(1)} fusion(bf16[32,704,128]{2,1,0:T(8,128)(2,1)} %param.2, f32[]{:T(128)S(6)} %add.73), kind=kLoop, calls=%fused_computation.23 | loop fusion | flops 8650752 | bytes 11534340 | tf_op jit(solution)/shard_map/convert.3
  117.8 3.7 %copy.91 = bf16[8,4,704,128]{3,0,2,1:T(8,128)(2,1)S(1)} copy(bf16[8,4,704,128]{3,2,1,0:T(8,128)(2,1)S(1)} %bitcast.79) | data formatting | bytes 11534336 | tf_op jit(solution)/shard_map/cond/branch_2_fun/div | solution.py:19
  121.5 2.5 copy-done
  124.0 6.7 %fusion.21 = bf16[1024,1024]{1,0:T(8,128)(2,1)S(1)} fusion(bf16[352,8,8,128]{3,2,1,0:T(8,128)(2,1)S(1)} %bitcast.88), kind=kOutput, calls=%fused_computation.27 | convolution fusion | flops 5905580032 | bytes 7864320 | tf_op jit(solution)/shard_map/cond/branch_2_fun/dot_general | solution.py:21
  130.7 17.7 %add_convert_fusion.5 = bf16[2816,1024]{1,0:T(8,128)(2,1)} fusion(bf16[352,8,8,128]{3,2,1,0:T(8,128)(2,1)} %bitcast.89, bf16[1024,1024]{1,0:T(8,128)(2,1)S(1)} %fusion.21), kind=kOutput, calls=%fused_computation.25 | convolution fusion | flops 8069840896 | bytes 13631488 | tf_op jit(solution)/shard_map/cond/branch_2_fun/dot_general | solution.py:30
  148.4 9.9 %fusion.65 = bf16[1024,1024]{1,0:T(8,128)(2,1)S(1)} fusion(bf16[2816,1024]{1,0:T(8,128)(2,1)} %add_convert_fusion.5), kind=kOutput, calls=%fused_computation.90 | convolution fusion | flops 5905580032 | bytes 7864320 | tf_op jit(solution)/shard_map/cond/branch_2_fun/dot_general | solution.py:21
  158.3 15.0 %fusion.26 = bf16[352,8,8,128]{3,1,2,0:T(8,128)(2,1)} fusion(bf16[2816,1024]{1,0:T(8,128)(2,1)} %add_convert_fusion.5, bf16[1024,1024]{1,0:T(8,128)(2,1)S(1)} %fusion.65), kind=kOutput, calls=%fused_computation.34 | convolution fusion | flops 8069840896 | bytes 13631488 | tf_op jit(solution)/shard_map/cond/branch_2_fun/dot_general | solution.py:30
  173.3 4.1 %copy.104 = bf16[352,8,8,128]{3,2,1,0:T(8,128)(2,1)S(1)} copy(bf16[352,8,8,128]{3,1,2,0:T(8,128)(2,1)} %fusion.26) | data formatting | bytes 11534336 | tf_op jit(solution)/shard_map/cond
  177.8 3.9 %copy.92 = bf16[8,4,704,128]{3,2,1,0:T(8,128)(2,1)} copy(bf16[8,4,704,128]{3,0,2,1:T(8,128)(2,1)S(1)} %bitcast_bitcast_fusion.1) | data formatting | bytes 11534336 | tf_op jit(solution)/shard_map/cond/branch_2_fun/transpose | solution.py:158
  181.9 1.3 copy.122
  183.2 4.9 %all-to-all-start.1 = ((bf16[32,704,128]{2,1,0:T(8,128)(2,1)}), bf16[32,704,128]{2,1,0:T(8,128)(2,1)}, u32[]{:S(2)}, u32[]{:S(2)}) async-start(bf16[32,704,128]{2,1,0:T(8,128)(2,1)} %get-tuple-element.132), calls=%async_computation.1 | async-start | bytes 11534336 | tf_op jit(solution)/shard_map/all_to_all | solution.py:176
  188.3 3.6 %multiply_subtract_fusion = (f32[251,1024]{1,0:T(8,128)}, f32[251,1024]{1,0:T(8,128)}, f32[251,1024]{1,0:T(8,128)}) fusion(f32[251,1024]{1,0:T(8,128)S(1)} %copy-done.1, bf16[251,1024]{1,0:T(8,128)(2,1)} %param.31, f32[251,1024]{1,0:T(8,128)S(1)} %copy-done.2, f32[251,1024]{1,0:T(8,128)} %param.32), kind=kLoop, calls=%fused_computation.72 | loop fusion | flops 3598336 | bytes 6682624 | tf_op jit(solution)/shard_map/sub | solution.py:50
  192.4 0.7 fusion.53
  193.7 0.7 multiply_subtract_fusion.1
  194.4 65.2 %all-to-all-done.1 = bf16[32,704,128]{2,1,0:T(8,128)(2,1)} async-done(((bf16[32,704,128]{2,1,0:T(8,128)(2,1)}), bf16[32,704,128]{2,1,0:T(8,128)(2,1)}, u32[]{:S(2)}, u32[]{:S(2)}) %all-to-all-start.1) | async-done | bytes 5767200 | tf_op jit(solution)/shard_map/all_to_all | solution.py:176
  259.6 2.1 convert_multiply_fusion.1
  261.7 1.2 slice_bitcast_fusion.1
  262.8 1.8 slice_bitcast_fusion
  264.6 1.5 convert_multiply_fusion.2
  266.1 1.8 copy.99
  (58 shorter events, 4.9 us)
Async XLA Ops:
  7.2 4.1 %copy-start.3 = (bf16[4,704,128]{2,1,0:T(8,128)(2,1)S(1)}, bf16[4,704,128]{2,1,0:T(8,128)(2,1)}, u32[]{:S(2)}) copy-start(bf16[4,704,128]{2,1,0:T(8,128)(2,1)} %param.25) | copy-start | bytes 2162692
  21.2 8.7 %copy-start.8 = (f32[1,32,16]{1,2,0:T(8,128)S(1)}, f32[1,32,16]{1,2,0:T(8,128)}, u32[]{:S(2)}) copy-start(f32[1,32,16]{1,2,0:T(8,128)} %param.39) | copy-start | bytes 6148
  21.2 80.1 %all-to-all-start = ((bf16[32,704,128]{2,1,0:T(8,128)(2,1)}), bf16[32,704,128]{2,1,0:T(8,128)(2,1)}, u32[]{:S(2)}, u32[]{:S(2)}) async-start(bf16[32,704,128]{2,1,0:T(8,128)(2,1)} %fusion.40), calls=%async_computation | async-start | bytes 11534336 | tf_op jit(solution)/shard_map/all_to_all | solution.py:135
  29.9 71.4 %copy-start.7 = (f32[4,1,2048]{2,1,0:T(1,128)S(1)}, f32[4,1,2048]{2,1,0:T(1,128)}, u32[]{:S(2)}) copy-start(f32[4,1,2048]{2,1,0:T(1,128)} %param.35) | copy-start | bytes 98308
  29.9 72.2 %copy-start.13 = (s32[32]{0:T(128)S(1)}, s32[32]{0:T(128)}, u32[]{:S(2)}) copy-start(s32[32]{0:T(128)} %constant.40.clone) | copy-start | bytes 388
  29.9 28.5 %all-gather.6.cloned.1.call-start = ((), (), s32[]{:S(2)}) async-start(), calls=%async_computation.2 | async-start | bytes 1310720 | tf_op jit(solution)/shard_map/all_gather | solution.py:122
  30.8 151.0 %all-gather.8.cloned.1.call-start = ((), (), s32[]{:S(2)}) async-start(), calls=%async_computation.3 | async-start | bytes 1165824 | tf_op jit(solution)/shard_map/all_gather | solution.py:144
  121.5 2.5 copy-start
  183.2 5.0 %copy-start.1 = (f32[251,1024]{1,0:T(8,128)S(1)}, f32[251,1024]{1,0:T(8,128)}, u32[]{:S(2)}) copy-start(f32[251,1024]{1,0:T(8,128)} %param.30) | copy-start | bytes 3084292
  183.2 5.0 %copy-start.2 = (f32[251,1024]{1,0:T(8,128)S(1)}, f32[251,1024]{1,0:T(8,128)}, u32[]{:S(2)}) copy-start(f32[251,1024]{1,0:T(8,128)} %param.33) | copy-start | bytes 3084292
  183.2 76.4 %all-to-all-start.1 = ((bf16[32,704,128]{2,1,0:T(8,128)(2,1)}), bf16[32,704,128]{2,1,0:T(8,128)(2,1)}, u32[]{:S(2)}, u32[]{:S(2)}) async-start(bf16[32,704,128]{2,1,0:T(8,128)(2,1)} %get-tuple-element.132), calls=%async_computation.1 | async-start | bytes 11534336 | tf_op jit(solution)/shard_map/all_to_all | solution.py:176
  188.2 4.2 %copy-start.12 = (s32[4,7]{1,0:T(4,128)S(1)}, s32[4,7]{1,0:T(4,128)}, u32[]{:S(2)}) copy-start(s32[4,7]{1,0:T(4,128)} %param.29) | copy-start | bytes 340
  188.2 4.9 %copy-start.9 = (f32[32,16]{0,1:T(8,128)S(1)}, f32[32,16]{0,1:T(8,128)}, u32[]{:S(2)}) copy-start(f32[32,16]{0,1:T(8,128)} %param.38) | copy-start | bytes 6148
  188.2 4.9 %copy-start.10 = (f32[32,16]{0,1:T(8,128)S(1)}, f32[32,16]{0,1:T(8,128)}, u32[]{:S(2)}) copy-start(f32[32,16]{0,1:T(8,128)} %param.41) | copy-start | bytes 6148
  188.2 4.9 %copy-start.11 = (f32[32,16]{0,1:T(8,128)S(1)}, f32[32,16]{0,1:T(8,128)}, u32[]{:S(2)}) copy-start(f32[32,16]{0,1:T(8,128)} %param.40) | copy-start | bytes 6148
  188.2 5.5 %copy-start.4 = (f32[4,2048]{1,0:T(4,128)S(1)}, f32[4,2048]{1,0:T(4,128)}, u32[]{:S(2)}) copy-start(f32[4,2048]{1,0:T(4,128)} %param.34) | copy-start | bytes 98308
  188.3 5.5 %copy-start.5 = (f32[4,2048]{1,0:T(4,128)S(1)}, f32[4,2048]{1,0:T(4,128)}, u32[]{:S(2)}) copy-start(f32[4,2048]{1,0:T(4,128)} %param.37) | copy-start | bytes 98308
  188.3 5.5 %copy-start.6 = (f32[4,2048]{1,0:T(4,128)S(1)}, f32[4,2048]{1,0:T(4,128)}, u32[]{:S(2)}) copy-start(f32[4,2048]{1,0:T(4,128)} %param.36) | copy-start | bytes 98308
Sparse Core Ops, SparseCore 0:
  32.9 25.3 all-gather.5
  102.1 42.4 all-gather.7

commit v10 on v9

--- a/solution.py
+++ b/solution.py
@@ -113,8 +113,14 @@
         [jnp.swapaxes(inner_ahead, 2, 3), outer_ahead[:, None]], axis=1
     ).reshape(n_rect, ff_block, rows_block)
 
-    square_ss = jnp.sum(jnp.square(square_table.astype(jnp.float32)), axis=(1, 2))
-    rect_ss = jnp.sum(jnp.square(rect_table.astype(jnp.float32)), axis=(1, 2))
+    square_rows_ss, rect_rows_ss = lax.optimization_barrier(
+        (
+            jnp.sum(jnp.square(square_table.astype(jnp.float32)), axis=1),
+            jnp.sum(jnp.square(rect_table.astype(jnp.float32)), axis=1),
+        )
+    )
+    square_ss = jnp.sum(square_rows_ss, axis=1)
+    rect_ss = jnp.sum(rect_rows_ss, axis=1)
     def padded(block):
         return jnp.pad(block, ((0, ff_block - block.shape[0]), (0, 0)))
 

time: 280 us -> 280 us (level)
  no operation moved by 1% of the time
where the time goes in v10:
time: 280 us; the launch traced here: 275 us
  waiting for transfers between devices  133 us (48%)
  matrix products  49.3 us (18%)
  other arithmetic  31.7 us (11%)
  local copies, waits for them, and re-layouts  25.7 us (9%)
  between operations  15.2 us (5%)
  starting transfers between devices  13.7 us (5%)
  loops' own time  6 us (2%)
    all_to_all x1, waiting for transfers between devices, on_device(): lax.all_to_all(returning, ('shards', 'tensor'), split_axis=0, concat_axis...  65.2 us
    all_to_all x1, waiting for transfers between devices, on_device(): lax.all_to_all(outgoing, ('shards', 'tensor'), split_axis=0, concat_axis=...  41.2 us
    dot_general x2, matrix products, newton_schulz_transposed(): lax.dot_general(current, polynomial, (((1,), (1,)), ((), ())), preferred_...  32.7 us
    all_gather x1, waiting for transfers between devices, on_device(): lax.all_gather(jnp.pad(bias_flat, (0, 65536 - bias_flat.shape[0])), 'sect...  26.8 us
    dot_general x2, matrix products, newton_schulz_transposed(): lax.dot_general(current, current, (((0,), (0,)), ((), ())), preferred_ele...  16.6 us
    all_to_all x1, starting transfers between devices, on_device(): lax.all_to_all(outgoing, ('shards', 'tensor'), split_axis=0, concat_axis=...  8.65 us
    cond x3, local copies, waits for them, and re-layouts  6.56 us
    another operation x1, loops' own time, on_device(): lax.switch(my_kind, [idle_branch, square_branch, rect_branch], incoming)  6 us
  transfers between devices with their start and end apart: 4, of which 3 were waited for; matrix products, arithmetic and copies ran while one was open for 29% of the time, Pallas kernels for 0%

profile of v10, /device:TPU:2, one launch (start us, length us, event | category | flops | bytes accessed | tf_op | source)
XLA Modules:
  0.0 274.7 jit_solution(8951131166698750731)
XLA Ops:
  7.2 3.2 %multiply_reduce_fusion.2 = (f32[4,4,128]{2,1,0:T(4,128)S(1)}, bf16[4,4,128,256]{3,2,1,0:T(8,128)(2,1)S(1)}, bf16[4,4,128,256]{3,2,1,0:T(8,128)(2,1)}) fusion(bf16[4,4,128,256]{3,2,1,0:T(8,128)(2,1)} %param.23, bf16[4,4,128,256]{3,2,1,0:T(8,128)(2,1)} %param.26), kind=kLoop, calls=%fused_computation.60 | loop fusion | flops 6289408 | bytes 4202496 | tf_op jit(solution)/shard_map/reduce_sum | solution.py:118
  11.1 2.3 fusion.50
  13.5 3.7 %fusion.47 = (bf16[4,2,704,128]{3,2,1,0:T(8,128)(2,1)S(1)}, bf16[4,2,128,704]{2,3,1,0:T(8,128)(2,1)}) fusion(bf16[4,2,128,704]{2,3,1,0:T(8,128)(2,1)} %param.24, bf16[4,2,128,704]{2,3,1,0:T(8,128)(2,1)} %param.27), kind=kLoop, calls=%fused_computation.66 | loop fusion | flops 6488064 | bytes 5767168 | tf_op jit(solution)/shard_map/transpose | solution.py:113
  17.4 3.6 %fusion.40 = bf16[32,704,128]{2,1,0:T(8,128)(2,1)} fusion(bf16[16,256,128]{2,1,0:T(8,128)(2,1)S(1)} %copy.95, bf16[12,704,128]{2,1,0:T(8,128)(2,1)S(1)} %bitcast.84, bf16[32]{0:T(256)(128)(2,1)S(1)} %pad.23.clone), kind=kLoop, calls=%fused_computation.46 | loop fusion | flops 28835840 | bytes 8978496 | tf_op jit(solution)/shard_map/concatenate | solution.py:134
  21.0 8.6 %all-to-all-start = ((bf16[32,704,128]{2,1,0:T(8,128)(2,1)}), bf16[32,704,128]{2,1,0:T(8,128)(2,1)}, u32[]{:S(2)}, u32[]{:S(2)}) async-start(bf16[32,704,128]{2,1,0:T(8,128)(2,1)} %fusion.40), calls=%async_computation | async-start | bytes 11534336 | tf_op jit(solution)/shard_map/all_to_all | solution.py:141
  29.9 0.7 pad.16
  31.4 26.8 %all-gather.6.cloned.1.call-done = f32[262144]{0:T(1024)} async-done(((f32[65536]{0:T(1024)}), f32[262144]{0:T(1024)}) %all-gather.6.cloned.1.call-update) | async-done | bytes 1048592 | tf_op jit(solution)/shard_map/all_gather | solution.py:128
  58.2 1.7 reshape.142
  59.9 41.2 %all-to-all-done = bf16[32,704,128]{2,1,0:T(8,128)(2,1)} async-done(((bf16[32,704,128]{2,1,0:T(8,128)(2,1)}), bf16[32,704,128]{2,1,0:T(8,128)(2,1)}, u32[]{:S(2)}, u32[]{:S(2)}) %all-to-all-start) | async-done | bytes 5767200 | tf_op jit(solution)/shard_map/all_to_all | solution.py:141
  103.1 78.5 %conditional.1 = (bf16[32,704,128]{2,1,0:T(8,128)(2,1)}) conditional(s32[]{:T(128)} %bitcast.8, () %tuple.20, bf16[32,704,128]{2,1,0:T(8,128)(2,1)} %all-to-all-done, bf16[32,704,128]{2,1,0:T(8,128)(2,1)} %all-to-all-done), branch_computations={%region_5.6_spmd, %region_6.9_spmd, %region_9.12_spmd} | conditional | flops 27968143360 | bytes 130220104 | solution.py:180
  108.2 3.8 %fusion.19 = f32[704,128]{1,0:T(8,128)S(1)} fusion(bf16[32,704,128]{2,1,0:T(8,128)(2,1)} %param.2), kind=kLoop, calls=%fused_computation.22 | loop fusion | flops 8560640 | bytes 6127616 | tf_op jit(solution)/shard_map/cond/branch_2_fun/reduce_sum | solution.py:159
  112.0 0.7 reduce_sum.93
  113.4 4.2 %fusion.20 = bf16[32,704,128]{2,1,0:T(8,128)(2,1)S(1)} fusion(bf16[32,704,128]{2,1,0:T(8,128)(2,1)} %param.2, f32[]{:T(128)S(6)} %add.73), kind=kLoop, calls=%fused_computation.23 | loop fusion | flops 8650752 | bytes 11534340 | tf_op jit(solution)/shard_map/convert.3
  117.6 3.7 %copy.91 = bf16[8,4,704,128]{3,0,2,1:T(8,128)(2,1)S(1)} copy(bf16[8,4,704,128]{3,2,1,0:T(8,128)(2,1)S(1)} %bitcast.80) | data formatting | bytes 11534336 | tf_op jit(solution)/shard_map/cond/branch_2_fun/div | solution.py:19
  121.3 2.4 copy-done
  123.8 6.7 %fusion.21 = bf16[1024,1024]{1,0:T(8,128)(2,1)S(1)} fusion(bf16[352,8,8,128]{3,2,1,0:T(8,128)(2,1)S(1)} %bitcast.89), kind=kOutput, calls=%fused_computation.27 | convolution fusion | flops 5905580032 | bytes 7864320 | tf_op jit(solution)/shard_map/cond/branch_2_fun/dot_general | solution.py:21
  130.5 17.7 %add_convert_fusion.5 = bf16[2816,1024]{1,0:T(8,128)(2,1)} fusion(bf16[352,8,8,128]{3,2,1,0:T(8,128)(2,1)} %bitcast.90, bf16[1024,1024]{1,0:T(8,128)(2,1)S(1)} %fusion.21), kind=kOutput, calls=%fused_computation.25 | convolution fusion | flops 8069840896 | bytes 13631488 | tf_op jit(solution)/shard_map/cond/branch_2_fun/dot_general | solution.py:30
  148.2 9.9 %fusion.65 = bf16[1024,1024]{1,0:T(8,128)(2,1)S(1)} fusion(bf16[2816,1024]{1,0:T(8,128)(2,1)} %add_convert_fusion.5), kind=kOutput, calls=%fused_computation.90 | convolution fusion | flops 5905580032 | bytes 7864320 | tf_op jit(solution)/shard_map/cond/branch_2_fun/dot_general | solution.py:21
  158.1 15.0 %fusion.26 = bf16[352,8,8,128]{3,1,2,0:T(8,128)(2,1)} fusion(bf16[2816,1024]{1,0:T(8,128)(2,1)} %add_convert_fusion.5, bf16[1024,1024]{1,0:T(8,128)(2,1)S(1)} %fusion.65), kind=kOutput, calls=%fused_computation.34 | convolution fusion | flops 8069840896 | bytes 13631488 | tf_op jit(solution)/shard_map/cond/branch_2_fun/dot_general | solution.py:30
  173.0 4.1 %copy.104 = bf16[352,8,8,128]{3,2,1,0:T(8,128)(2,1)S(1)} copy(bf16[352,8,8,128]{3,1,2,0:T(8,128)(2,1)} %fusion.26) | data formatting | bytes 11534336 | tf_op jit(solution)/shard_map/cond
  177.6 3.9 %copy.92 = bf16[8,4,704,128]{3,2,1,0:T(8,128)(2,1)} copy(bf16[8,4,704,128]{3,0,2,1:T(8,128)(2,1)S(1)} %bitcast_bitcast_fusion.1) | data formatting | bytes 11534336 | tf_op jit(solution)/shard_map/cond/branch_2_fun/transpose | solution.py:164
  181.7 1.3 copy.122
  183.0 4.9 %all-to-all-start.1 = ((bf16[32,704,128]{2,1,0:T(8,128)(2,1)}), bf16[32,704,128]{2,1,0:T(8,128)(2,1)}, u32[]{:S(2)}, u32[]{:S(2)}) async-start(bf16[32,704,128]{2,1,0:T(8,128)(2,1)} %get-tuple-element.136), calls=%async_computation.1 | async-start | bytes 11534336 | tf_op jit(solution)/shard_map/all_to_all | solution.py:182
  188.1 3.6 %multiply_subtract_fusion = (f32[251,1024]{1,0:T(8,128)}, f32[251,1024]{1,0:T(8,128)}, f32[251,1024]{1,0:T(8,128)}) fusion(f32[251,1024]{1,0:T(8,128)S(1)} %copy-done.1, bf16[251,1024]{1,0:T(8,128)(2,1)} %param.31, f32[251,1024]{1,0:T(8,128)S(1)} %copy-done.2, f32[251,1024]{1,0:T(8,128)} %param.32), kind=kLoop, calls=%fused_computation.72 | loop fusion | flops 3598336 | bytes 6682624 | tf_op jit(solution)/shard_map/sub | solution.py:50
  192.2 0.7 fusion.53
  193.5 0.7 multiply_subtract_fusion.1
  194.2 65.2 %all-to-all-done.1 = bf16[32,704,128]{2,1,0:T(8,128)(2,1)} async-done(((bf16[32,704,128]{2,1,0:T(8,128)(2,1)}), bf16[32,704,128]{2,1,0:T(8,128)(2,1)}, u32[]{:S(2)}, u32[]{:S(2)}) %all-to-all-start.1) | async-done | bytes 5767200 | tf_op jit(solution)/shard_map/all_to_all | solution.py:182
  259.4 2.1 convert_multiply_fusion.1
  261.5 1.2 slice_bitcast_fusion.1
  262.6 1.8 slice_bitcast_fusion
  264.4 1.5 convert_multiply_fusion.2
  265.9 1.8 copy.99
  (59 shorter events, 4.8 us)
Async XLA Ops:
  7.2 4.0 %copy-start.3 = (bf16[4,704,128]{2,1,0:T(8,128)(2,1)S(1)}, bf16[4,704,128]{2,1,0:T(8,128)(2,1)}, u32[]{:S(2)}) copy-start(bf16[4,704,128]{2,1,0:T(8,128)(2,1)} %param.25) | copy-start | bytes 2162692
  21.0 8.7 %copy-start.8 = (f32[1,32,16]{1,2,0:T(8,128)S(1)}, f32[1,32,16]{1,2,0:T(8,128)}, u32[]{:S(2)}) copy-start(f32[1,32,16]{1,2,0:T(8,128)} %param.39) | copy-start | bytes 6148
  21.0 80.1 %all-to-all-start = ((bf16[32,704,128]{2,1,0:T(8,128)(2,1)}), bf16[32,704,128]{2,1,0:T(8,128)(2,1)}, u32[]{:S(2)}, u32[]{:S(2)}) async-start(bf16[32,704,128]{2,1,0:T(8,128)(2,1)} %fusion.40), calls=%async_computation | async-start | bytes 11534336 | tf_op jit(solution)/shard_map/all_to_all | solution.py:141
  29.7 71.4 %copy-start.7 = (f32[4,1,2048]{2,1,0:T(1,128)S(1)}, f32[4,1,2048]{2,1,0:T(1,128)}, u32[]{:S(2)}) copy-start(f32[4,1,2048]{2,1,0:T(1,128)} %param.35) | copy-start | bytes 98308
  29.7 72.2 %copy-start.13 = (s32[32]{0:T(128)S(1)}, s32[32]{0:T(128)}, u32[]{:S(2)}) copy-start(s32[32]{0:T(128)} %constant.40.clone) | copy-start | bytes 388
  29.7 28.5 %all-gather.6.cloned.1.call-start = ((), (), s32[]{:S(2)}) async-start(), calls=%async_computation.2 | async-start | bytes 1310720 | tf_op jit(solution)/shard_map/all_gather | solution.py:128
  30.7 151.0 %all-gather.8.cloned.1.call-start = ((), (), s32[]{:S(2)}) async-start(), calls=%async_computation.3 | async-start | bytes 1165824 | tf_op jit(solution)/shard_map/all_gather | solution.py:150
  121.3 2.4 copy-start
  183.0 5.0 %copy-start.1 = (f32[251,1024]{1,0:T(8,128)S(1)}, f32[251,1024]{1,0:T(8,128)}, u32[]{:S(2)}) copy-start(f32[251,1024]{1,0:T(8,128)} %param.30) | copy-start | bytes 3084292
  183.0 5.0 %copy-start.2 = (f32[251,1024]{1,0:T(8,128)S(1)}, f32[251,1024]{1,0:T(8,128)}, u32[]{:S(2)}) copy-start(f32[251,1024]{1,0:T(8,128)} %param.33) | copy-start | bytes 3084292
  183.0 76.4 %all-to-all-start.1 = ((bf16[32,704,128]{2,1,0:T(8,128)(2,1)}), bf16[32,704,128]{2,1,0:T(8,128)(2,1)}, u32[]{:S(2)}, u32[]{:S(2)}) async-start(bf16[32,704,128]{2,1,0:T(8,128)(2,1)} %get-tuple-element.136), calls=%async_computation.1 | async-start | bytes 11534336 | tf_op jit(solution)/shard_map/all_to_all | solution.py:182
  188.0 4.2 %copy-start.12 = (s32[4,7]{1,0:T(4,128)S(1)}, s32[4,7]{1,0:T(4,128)}, u32[]{:S(2)}) copy-start(s32[4,7]{1,0:T(4,128)} %param.29) | copy-start | bytes 340
  188.0 4.9 %copy-start.9 = (f32[32,16]{0,1:T(8,128)S(1)}, f32[32,16]{0,1:T(8,128)}, u32[]{:S(2)}) copy-start(f32[32,16]{0,1:T(8,128)} %param.38) | copy-start | bytes 6148
  188.0 4.9 %copy-start.10 = (f32[32,16]{0,1:T(8,128)S(1)}, f32[32,16]{0,1:T(8,128)}, u32[]{:S(2)}) copy-start(f32[32,16]{0,1:T(8,128)} %param.41) | copy-start | bytes 6148
  188.0 4.9 %copy-start.11 = (f32[32,16]{0,1:T(8,128)S(1)}, f32[32,16]{0,1:T(8,128)}, u32[]{:S(2)}) copy-start(f32[32,16]{0,1:T(8,128)} %param.40) | copy-start | bytes 6148
  188.0 5.5 %copy-start.4 = (f32[4,2048]{1,0:T(4,128)S(1)}, f32[4,2048]{1,0:T(4,128)}, u32[]{:S(2)}) copy-start(f32[4,2048]{1,0:T(4,128)} %param.34) | copy-start | bytes 98308
  188.1 5.5 %copy-start.5 = (f32[4,2048]{1,0:T(4,128)S(1)}, f32[4,2048]{1,0:T(4,128)}, u32[]{:S(2)}) copy-start(f32[4,2048]{1,0:T(4,128)} %param.37) | copy-start | bytes 98308
  188.1 5.5 %copy-start.6 = (f32[4,2048]{1,0:T(4,128)S(1)}, f32[4,2048]{1,0:T(4,128)}, u32[]{:S(2)}) copy-start(f32[4,2048]{1,0:T(4,128)} %param.36) | copy-start | bytes 98308
Sparse Core Ops, SparseCore 0:
  32.7 25.3 all-gather.5
  102.0 42.4 all-gather.7
